TPU v7x, 512 devices: a whole 4x4x16 slice. The times are simulated.
512 devices in a mesh: seq: 64 (over z, y), head: 8 (over x, core).
Axes of the slice: x: 4, y: 4, z: 16, core: 2. Of those that a mesh axis runs over, the one named last changes fastest.
Arguments:
- tokens_in: bfloat16 [8192, 2048], P('seq', 'head'), may hold values from -40 to 40
- mixed_qkv: bfloat16 [8192, 8192], P('seq', 'head'), may hold values from -6 to 6
- conv_weight: bfloat16 [4, 8192], P(None, 'head'), may hold values from -3 to 3
- conv_cache: bfloat16 [3, 8192], P(None, 'head'), may hold values from -6 to 6
- gate_z: bfloat16 [8192, 4096], P('seq', 'head'), may hold values from -6 to 6
- beta_logit: float32 [32, 8192], P('head', 'seq'), may hold values from -10 to 2.5
- log_decay: float32 [32, 8192], P('head', 'seq'), may hold values from -0.8 to 0
- init_state: float32 [32, 128, 128], P('head'), may hold values from -0.18 to 0.18
- norm_weight: float32 [128], replicated, may hold values from 0.25 to 1.75
- out_weight: bfloat16 [4096, 2048], P('head'), may hold values from -0.09375 to 0.09375
- steer_table: float32 [16, 2048], P(None, 'head'), may hold values from -4.2 to 4.2
- steer_index: int32 [8192], P('seq'), may hold values from 0 to 15
- post_norm_weight: float32 [2048], P('head'), may hold values from 0.25 to 1.75
- route_ids: int32 [8192, 10], P('seq'), may hold values from 0 to 255, all different within a row; in each aligned block of 128 rows (0 to 127, 128 to 255, ...) at most 6 rows name the same one
- route_weight: float32 [8192, 10], P('seq'), may hold values from 0.1 to 1
- w_gate_up: bfloat16 [256, 2048, 512], P('seq', 'head'), may hold values from -0.125 to 0.125
- w_down: bfloat16 [256, 256, 2048], P('seq', None, 'head'), may hold values from -0.375 to 0.375
Outputs:
- layer_out: bfloat16 [8192, 2048], P('seq', 'head')
Inputs may be any that keep to these rules, and one draw needn't show every extreme that they name: `route_ids`: each row names 10 different experts. Among the 128 rows of one device no expert is named more than 6 times, and in some devices' rows some expert is named exactly 6 times.
All inputs are finite; a program needn't handle non-finite values.
Results may differ from a plain program's by a relative error of at most 0.017.
Values may be sent and summed in bfloat16 or wider, within the bound.
No kernel may reach another device: no remote copies, remote signals or barrier semaphores. Data moves between devices by JAX's collectives and lax.ppermute only.
A program may use at most 128 MiB of HBM per device.

v0:
```python
import functools

import jax
import jax.numpy as jnp
from jax import lax
from jax.sharding import PartitionSpec as P

D = 2048
HK = 16
VALUE_HEAD_COUNT = 32
DK = 128
DV = 128
KCONV = 4
STRETCH = 64


EPS = 1e-06
EXACT_ARITHMETIC = lax.Precision.HIGHEST


def prefix(value, axis, combine, identity):
    count, position = (lax.axis_size(axis), lax.axis_index(axis))
    everything = jax.tree.map(
        lambda part, kind: lax.all_gather(part.astype(kind), axis),
        value,
        (jnp.bfloat16, jnp.bfloat16),
    )
    start = jax.tree.map(
        lambda part, zero: jnp.broadcast_to(jnp.asarray(zero, part.dtype), part.shape),
        value,
        identity,
    )

    def hop(k, before):
        reached = k < position
        new = combine(
            before, jax.tree.map(lambda part, own: part[k].astype(own.dtype), everything, value)
        )
        return jax.tree.map(lambda a, b: jnp.where(reached, a, b), new, before)

    return lax.fori_loop(0, count, hop, start)


def passed_along(value, axis, steps):
    count = lax.axis_size(axis)
    first, last = (max(0, -steps), min(count, count - steps))
    return lax.ppermute(value, axis, [(source, source + steps) for source in range(first, last)])


def unit_rows(vectors):
    return vectors / jnp.sqrt(jnp.sum(vectors * vectors, axis=-1, keepdims=True) + EPS)


def delta_block(want_output, carry_state, block):
    query_block, key_block, value_block, beta_block, decay_block = block
    block_len = query_block.shape[1]
    cum_decay = jnp.cumsum(decay_block, axis=-1)
    positions = jnp.arange(block_len)
    lower_mask = positions[:, None] >= positions[None, :]
    strict = positions[:, None] > positions[None, :]
    decay_diff = cum_decay[:, :, None] - cum_decay[:, None, :]
    inner = jnp.where(lower_mask, jnp.exp(jnp.where(lower_mask, decay_diff, 0.0)), 0.0)
    keys_keys = jnp.einsum("hck,hdk->hcd", key_block, key_block, precision=EXACT_ARITHMETIC)
    system = jnp.eye(block_len, dtype=jnp.float32) + beta_block[:, :, None] * jnp.where(
        strict, inner * keys_keys, 0.0
    )
    growth = jnp.exp(cum_decay)
    known_part = jnp.einsum("hck,hkw->hcw", key_block, carry_state, precision=EXACT_ARITHMETIC)
    target = beta_block[:, :, None] * (value_block - growth[:, :, None] * known_part)
    update = lax.linalg.triangular_solve(
        system, target, left_side=True, lower=True, unit_diagonal=True
    )
    tail_decay = jnp.exp(cum_decay[:, -1:] - cum_decay)
    new_state = growth[:, -1][:, None, None] * carry_state + jnp.einsum(
        "hck,hcw->hkw", key_block * tail_decay[:, :, None], update, precision=EXACT_ARITHMETIC
    )
    if not want_output:
        return (new_state, None)
    query_keys = jnp.einsum("hck,hdk->hcd", query_block, key_block, precision=EXACT_ARITHMETIC)
    output = growth[:, :, None] * jnp.einsum(
        "hck,hkw->hcw", query_block, carry_state, precision=EXACT_ARITHMETIC
    )
    output = output + jnp.einsum(
        "hcd,hdw->hcw", inner * query_keys, update, precision=EXACT_ARITHMETIC
    )
    return (new_state, output)


def delta_pass(queries, key_rows, values, beta_rate, decays, state_start, want_output):
    value_heads, length = beta_rate.shape
    block_count = length // STRETCH

    def to_blocks(tensor):
        shaped = tensor.reshape((value_heads, block_count, STRETCH) + tensor.shape[2:])
        return jnp.moveaxis(shaped, 1, 0)

    state_end, outputs = lax.scan(
        functools.partial(delta_block, want_output),
        state_start,
        (
            to_blocks(queries),
            to_blocks(key_rows),
            to_blocks(values),
            to_blocks(beta_rate),
            to_blocks(decays),
        ),
    )
    if want_output:
        outputs = jnp.moveaxis(outputs, 0, 1).reshape(value_heads, length, -1)
    return (state_end, outputs)


def compose(earlier, later):
    map_early, shift_early = earlier
    map_late, shift_late = later
    joined_map = jnp.einsum("hij,hjk->hik", map_late, map_early, precision=EXACT_ARITHMETIC)
    joined_shift = (
        jnp.einsum("hij,hjk->hik", map_late, shift_early, precision=EXACT_ARITHMETIC) + shift_late
    )
    return (joined_map, joined_shift)


def entering_state(transfer, carried, init_state):
    identity_maps = jnp.broadcast_to(jnp.eye(DK, dtype=jnp.float32), transfer.shape)
    prior_map, prior_shift = prefix(
        (transfer, carried), "seq", compose, (identity_maps, jnp.zeros_like(carried))
    )
    return (
        jnp.einsum("hij,hjk->hik", prior_map, init_state, precision=EXACT_ARITHMETIC) + prior_shift
    )


def local(
    tokens_in,
    mixed_qkv,
    conv_weight,
    conv_cache,
    gate_z,
    beta_logit,
    log_decay,
    init_state,
    norm_weight,
    out_weight,
    steer_table,
    steer_index,
    post_norm_weight,
    route_ids,
    route_weight,
    w_gate_up,
    w_down,
):
    length, channels = mixed_qkv.shape
    value_heads = beta_logit.shape[0]
    group_width = 2 * DK + VALUE_HEAD_COUNT // HK * DV
    key_heads = channels // group_width
    group_size = value_heads // key_heads
    boundary_rows = passed_along(mixed_qkv[length - (KCONV - 1) :], "seq", 1)
    is_first = (lax.axis_index("seq") == 0).astype(jnp.float32)
    preceding = boundary_rows.astype(jnp.float32) + is_first * conv_cache.astype(jnp.float32)
    padded = jnp.concatenate([preceding, mixed_qkv.astype(jnp.float32)], axis=0)
    conv_taps = conv_weight.astype(jnp.float32)
    convolved = conv_taps[0] * padded[0:length]
    for offset in range(1, KCONV):
        convolved = convolved + conv_taps[offset] * padded[offset : offset + length]
    convolved = jax.nn.silu(convolved).reshape(length, key_heads, group_width)
    queries = jnp.repeat(unit_rows(convolved[:, :, :DK]) * DK ** (-0.5), group_size, axis=1)
    key_rows = jnp.repeat(unit_rows(convolved[:, :, DK : 2 * DK]), group_size, axis=1)
    values = convolved[:, :, 2 * DK :].reshape(length, value_heads, DV)
    queries = jnp.transpose(queries, (1, 0, 2))
    key_rows = jnp.transpose(key_rows, (1, 0, 2))
    values = jnp.transpose(values, (1, 0, 2))
    beta_rate = jax.nn.sigmoid(beta_logit)
    identity_maps = jnp.broadcast_to(jnp.eye(DK, dtype=jnp.float32), (value_heads, DK, DK))
    state_start = jnp.concatenate(
        [jnp.zeros((value_heads, DK, DV), jnp.float32), identity_maps], axis=2
    )
    wide_values = jnp.concatenate(
        [values, jnp.zeros((value_heads, length, DK), jnp.float32)], axis=2
    )
    state_end, unused_out = delta_pass(
        queries, key_rows, wide_values, beta_rate, log_decay, state_start, False
    )
    entering = entering_state(state_end[:, :, DV:], state_end[:, :, :DV], init_state)
    unused_end, delta_out = delta_pass(
        queries, key_rows, values, beta_rate, log_decay, entering, True
    )
    delta_out = jnp.transpose(delta_out, (1, 0, 2))
    inv_rms = lax.rsqrt(jnp.mean(delta_out * delta_out, axis=-1, keepdims=True) + EPS)
    gate_act = jax.nn.silu(gate_z.astype(jnp.float32)).reshape(length, value_heads, DV)
    normed_heads = (
        (delta_out * inv_rms * norm_weight * gate_act)
        .astype(jnp.bfloat16)
        .reshape(length, value_heads * DV)
    )
    partial_value = jnp.dot(normed_heads, out_weight, preferred_element_type=jnp.float32)
    attended = lax.psum_scatter(
        partial_value.astype(jnp.bfloat16), "head", scatter_dimension=1, tiled=True
    ).astype(jnp.float32)
    hidden = tokens_in.astype(jnp.float32) + attended
    steer_onehot = (steer_index[:, None] == jnp.arange(steer_table.shape[0])[None, :]).astype(
        jnp.float32
    )
    steered = hidden + jnp.dot(
        steer_onehot, steer_table, precision=EXACT_ARITHMETIC, preferred_element_type=jnp.float32
    )
    sum_hidden, sum_steered = lax.psum(
        (jnp.sum(hidden * hidden, axis=1), jnp.sum(steered * steered, axis=1)), "head"
    )
    rescaled = steered * jnp.sqrt((sum_hidden / D + EPS) / (sum_steered / D + EPS))[:, None]
    normed = (post_norm_weight * steered * lax.rsqrt(sum_steered / D + EPS)[:, None]).astype(
        jnp.bfloat16
    )
    experts_here = w_gate_up.shape[0]
    seq_size = lax.axis_size("seq")
    experts = experts_here * seq_size
    top_count = route_ids.shape[1]
    capacity = 5 * length * top_count // (4 * experts)
    slot_count = seq_size * capacity * experts_here
    flat_ids = route_ids.reshape(-1)
    expert_hits = (flat_ids[:, None] == jnp.arange(experts, dtype=jnp.int32)[None, :]).astype(
        jnp.int32
    )
    slot_rank = jnp.sum(jnp.cumsum(expert_hits, axis=0) * expert_hits, axis=1) - 1
    owner_dev = flat_ids // experts_here
    local_expert = flat_ids % experts_here
    slot_place = (owner_dev * capacity + slot_rank) * experts_here + local_expert
    source = (
        jnp.full((slot_count,), length, jnp.int32)
        .at[slot_place]
        .set(jnp.arange(flat_ids.shape[0], dtype=jnp.int32) // top_count)
    )
    padded_rows = jnp.concatenate([normed, jnp.zeros((1, normed.shape[1]), jnp.bfloat16)], axis=0)
    outgoing = jnp.take(padded_rows, source, axis=0).reshape(seq_size, capacity, experts_here, -1)
    arrived = lax.all_to_all(outgoing, "seq", split_axis=0, concat_axis=0, tiled=True)
    row_count = seq_size * capacity
    arrived = arrived.reshape(row_count, experts_here, -1)
    ffn_width = w_down.shape[1]
    term_rows = jnp.einsum("red,edf->ref", arrived, w_gate_up, preferred_element_type=jnp.float32)
    summed = lax.psum(term_rows.reshape(row_count, -1).astype(jnp.bfloat16), "head").astype(
        jnp.float32
    )
    activate_summed = summed
    activate_summed = activate_summed.reshape(activate_summed.shape[0], experts_here, 2 * ffn_width)
    results = jnp.einsum(
        "ref,efd->red",
        (jax.nn.silu(activate_summed[:, :, :ffn_width]) * activate_summed[:, :, ffn_width:]).astype(
            jnp.bfloat16
        ),
        w_down,
        preferred_element_type=jnp.float32,
    ).astype(jnp.bfloat16)
    returned = lax.all_to_all(
        results.reshape(seq_size, capacity, experts_here, -1),
        "seq",
        split_axis=0,
        concat_axis=0,
        tiled=True,
    )
    returned = returned.reshape(slot_count, -1)
    route_mix = route_weight / jnp.sum(route_weight, axis=1, keepdims=True)
    picked = jnp.take(returned, slot_place, axis=0).reshape(length, top_count, -1)
    expert_mix = jnp.sum(picked.astype(jnp.float32) * route_mix[:, :, None], axis=1)
    return (rescaled + expert_mix).astype(jnp.bfloat16)


def solution(mesh):
    placed = (
        P("seq", "head"),
        P("seq", "head"),
        P(None, "head"),
        P(None, "head"),
        P("seq", "head"),
        P("head", "seq"),
        P("head", "seq"),
        P("head", None, None),
        P(),
        P("head", None),
        P(None, "head"),
        P("seq"),
        P("head"),
        P("seq", None),
        P("seq", None),
        P("seq", "head", None),
        P("seq", None, "head"),
    )
    return jax.shard_map(
        local, mesh=mesh, in_specs=placed, out_specs=P("seq", "head"), check_vma=False
    )
```

profile of v0, /device:TPU:15, one launch (start us, length us, event | category | flops | bytes accessed | tf_op | source)
XLA Modules:
  0.0 884.9 jit_solution(3141794068398965709)
XLA Ops:
  7.4 3.2 collective-permute-start
  12.2 1.8 convert_element_type.105
  16.8 2.8 divide_multiply_fusion
  19.6 2.0 copy.114
  22.7 1.7 slice.107
  24.3 1.6 divide_multiply_fusion.1
  28.1 51.1 %while.38 = (s32[]{:T(128)}, f32[4,128,256]{2,1,0:T(8,128)S(1)}, f32[2,4,64]{2,1,0:T(4,128)}, f32[2,4,64,128]{3,2,1,0:T(8,128)S(1)}, f32[2,4,64]{2,1,0:T(4,128)}...) while((s32[]{:T(128)}, f32[4,128,256]{2,1,0:T(8,128)S(1)}, f32[2,4,64]{2,1,0:T(4,128)}, ...), condition=%wide.region_3.4_spmd, body=%wide.region_1.0_spmd.sunk | while | flops 277508160 | bytes 3566773 | solution.py:97
  31.8 20.4 %custom-call.14 = f32[4,1,64,64]{2,3,1,0:T(8,128)S(1)} custom-call(f32[4,1,64,64]{3,2,1,0:T(8,128)} %fusion.169), custom_call_target="InvertDiagBlocksLowerTriangular" | custom-call | tf_op jit(solution)/shard_map/while/body/eval_jaxpr/triangular_solve | solution.py:70
  57.4 20.4 %custom-call.14 = f32[4,1,64,64]{2,3,1,0:T(8,128)S(1)} custom-call(f32[4,1,64,64]{3,2,1,0:T(8,128)} %fusion.169), custom_call_target="InvertDiagBlocksLowerTriangular" | custom-call | tf_op jit(solution)/shard_map/while/body/eval_jaxpr/triangular_solve | solution.py:70
  85.6 1.8 broadcast_add_fusion
  87.5 1.8 copy.135
  89.4 142.0 %all-gather.5.cloned.1.call-done = bf16[256,128,128]{2,1,0:T(8,128)(2,1)} async-done(((bf16[4,128,128]{2,1,0:T(8,128)(2,1)}), bf16[256,128,128]{2,1,0:T(8,128)(2,1)}) %all-gather.5.cloned.1.call-update) | async-done | bytes 8388624 | tf_op jit(solution)/shard_map/all_gather | solution.py:24
  231.4 154.0 %all-gather.7.cloned.1.call-done = bf16[256,128,128]{2,1,0:T(8,128)(2,1)} async-done(((bf16[4,128,128]{2,1,0:T(8,128)(2,1)}), bf16[256,128,128]{2,1,0:T(8,128)(2,1)}) %all-gather.7.cloned.1.call-update) | async-done | bytes 8388624 | tf_op jit(solution)/shard_map/all_gather | solution.py:24
  385.4 163.0 %while.40 = (s32[]{:T(128)}, f32[4,128,128]{2,1,0:T(8,128)S(1)}, f32[4,128,128]{2,1,0:T(8,128)S(1)}, s32[]{:T(128)}, bf16[64,4,128,128]{3,2,1,0:T(8,128)(2,1)}, ...) while((s32[]{:T(128)}, f32[4,128,128]{2,1,0:T(8,128)S(1)}, ...), condition=%wide.region_5.6_spmd.clone, body=%wide.region_4.5_spmd.clone.sunk | while | flops 201719808 | bytes 3017832 | solution.py:41
  549.8 54.6 %while.39 = (s32[]{:T(128)}, f32[4,128,128]{2,1,0:T(8,128)S(1)}, f32[2,4,64,128]{3,2,0,1:T(8,128)}, f32[2,4,64]{2,1,0:T(4,128)}, f32[2,4,64,128]{3,2,1,0:T(8,128...) while((s32[]{:T(128)}, f32[4,128,128]{2,1,0:T(8,128)S(1)}, ...), condition=%wide.region_9.10_spmd, body=%wide.region_7.9_spmd.sunk | while | flops 252244032 | bytes 3451077 | solution.py:97
  553.1 20.4 %custom-call.15 = f32[4,1,64,64]{2,3,1,0:T(8,128)S(1)} custom-call(f32[4,1,64,64]{3,2,1,0:T(8,128)} %fusion.185), custom_call_target="InvertDiagBlocksLowerTriangular" | custom-call | tf_op jit(solution)/shard_map/while/body/eval_jaxpr/triangular_solve | solution.py:70
  580.4 20.4 %custom-call.15 = f32[4,1,64,64]{2,3,1,0:T(8,128)S(1)} custom-call(f32[4,1,64,64]{3,2,1,0:T(8,128)} %fusion.185), custom_call_target="InvertDiagBlocksLowerTriangular" | custom-call | tf_op jit(solution)/shard_map/while/body/eval_jaxpr/triangular_solve | solution.py:70
  607.6 2.2 convolution_convert_fusion
  610.7 5.2 scatter_custom_fusion
  616.2 35.1 %reduce-scatter.2.cloned.1.call-done = bf16[128,256]{1,0:T(8,128)(2,1)} async-done(((bf16[128,2048]{1,0:T(8,128)(2,1)}), bf16[128,256]{1,0:T(8,128)(2,1)}) %reduce-scatter.2.cloned.1.call-update) | async-done | bytes 65552 | tf_op jit(solution)/shard_map/reduce_scatter | solution.py:196
  653.5 11.9 %all-reduce.3 = (f32[128]{0:T(128)S(1)}, f32[128]{0:T(128)S(1)}) all-reduce(f32[128]{0:T(128)S(1)} %get-tuple-element.340, f32[128]{0:T(128)S(1)} %multiply_reduce_fusion.2), channel_id=1, replica_groups=mesh['seq'=64,'head'=8] {'head'}, use_global_device_ids=true, to_apply=%region_15.16 | all-reduce | flops 256 | bytes 2048 | tf_op jit(solution)/shard_map/psum | solution.py:206
  666.2 5.3 gather_fusion
  671.5 1.7 gather.13
  673.9 59.0 %all_to_all.10 = bf16[64,6,4,256]{3,2,1,0:T(4,128)(2,1)S(1)} all-to-all(bf16[64,6,4,256]{3,2,1,0:T(4,128)(2,1)S(1)} %broadcast_select_fusion), channel_id=1, replica_groups=mesh['seq'=64,'head'=8] {'seq'}, dimensions={0} | all-to-all | bytes 1572864 | tf_op jit(solution)/shard_map/all_to_all | solution.py:234
  732.9 1.7 fusion.67
  734.7 70.6 %all-reduce.6.cloned.1.call-done = bf16[384,4,512]{2,0,1:T(8,128)(2,1)} async-done(((bf16[384,4,512]{2,0,1:T(8,128)(2,1)}), bf16[384,4,512]{2,0,1:T(8,128)(2,1)}) %all-reduce.6.cloned.1.call-update) | async-done | bytes 1572880 | tf_op jit(solution)/shard_map/psum | solution.py:239
  805.3 1.8 reshape.363
  807.8 1.5 copy.140
  809.3 15.3 %all-to-all-start.1 = ((bf16[64,6,4,256]{3,2,1,0:T(4,128)(2,1)}), bf16[64,6,4,256]{3,2,1,0:T(4,128)(2,1)}, u32[]{:S(2)}, u32[]{:S(2)}) async-start(bf16[64,6,4,256]{3,2,1,0:T(4,128)(2,1)} %bitcast.54), calls=%async_computation.2 | async-start | bytes 1572864 | tf_op jit(solution)/shard_map/all_to_all | solution.py:252
  825.2 44.2 %all-to-all-done.1 = bf16[64,6,4,256]{3,2,1,0:T(4,128)(2,1)} async-done(((bf16[64,6,4,256]{3,2,1,0:T(4,128)(2,1)}), bf16[64,6,4,256]{3,2,1,0:T(4,128)(2,1)}, u32[]{:S(2)}, u32[]{:S(2)}) %all-to-all-start.1) | async-done | bytes 786464 | tf_op jit(solution)/shard_map/all_to_all | solution.py:252
  869.3 1.6 reshape.365
  870.9 4.7 gather_fusion.1
  (419 shorter events, 211.3 us)
Async XLA Ops:
  6.5 601.0 %copy-start = (bf16[512,2048]{1,0:T(8,128)(2,1)S(1)}, bf16[512,2048]{1,0:T(8,128)(2,1)}, u32[]{:S(2)}) copy-start(bf16[512,2048]{1,0:T(8,128)(2,1)} %param.32) | copy-start | bytes 6291460
  6.5 224.9 %all-gather.5.cloned.1.call-start = ((), (), s32[]{:S(2)}) async-start(), calls=%async_computation.5 | async-start | bytes 8519680 | tf_op jit(solution)/shard_map/all_gather | solution.py:24
  7.4 8.7 collective-permute-start
  27.2 0.9 copy-start.2
  28.1 52.7 %copy-start.10 = (s32[128,10]{0,1:T(8,128)S(1)}, s32[128,10]{0,1:T(8,128)}, u32[]{:S(2)}) copy-start(s32[128,10]{0,1:T(8,128)} %param.36) | copy-start | bytes 15364
  80.0 305.4 %all-gather.7.cloned.1.call-start = ((), (), s32[]{:S(2)}) async-start(), calls=%async_computation.6 | async-start | bytes 8519680 | tf_op jit(solution)/shard_map/all_gather | solution.py:24
  80.8 570.6 %reduce-scatter.2.cloned.1.call-start = ((), (), s32[]{:S(2)}) async-start(), calls=%async_computation.3 | async-start | bytes 589824 | tf_op jit(solution)/shard_map/reduce_scatter | solution.py:196
  80.9 6.5 copy-start.5
  84.2 1.4 copy-start.1
  87.4 1.8 copy-start.8
  385.4 164.3 %copy-start.3 = (f32[4,128,128]{2,1,0:T(8,128)S(1)}, f32[4,128,128]{2,1,0:T(8,128)}, u32[]{:S(2)}) copy-start(f32[4,128,128]{2,1,0:T(8,128)} %copy-done.2) | copy-start | bytes 786436
  605.5 4.5 copy-start.4
  605.5 4.5 copy-start.13
  607.6 2.9 copy-start.6
  607.6 43.8 %copy-start.9 = (bf16[128,256]{1,0:T(8,128)(2,1)S(1)}, bf16[128,256]{1,0:T(8,128)(2,1)}, u32[]{:S(2)}) copy-start(bf16[128,256]{1,0:T(8,128)(2,1)} %param.23) | copy-start | bytes 196612
  609.8 195.5 %all-reduce.6.cloned.1.call-start = ((), (), s32[]{:S(2)}) async-start(), calls=%async_computation.4 | async-start | bytes 3145728 | tf_op jit(solution)/shard_map/psum | solution.py:239
  673.2 59.7 %copy-start.7 = (bf16[4,256,512]{2,1,0:T(8,128)(2,1)S(1)}, bf16[4,256,512]{2,1,0:T(8,128)(2,1)}, u32[]{:S(2)}) copy-start(bf16[4,256,512]{2,1,0:T(8,128)(2,1)} %param.38) | copy-start | bytes 3145732
  734.7 72.5 %copy-start.14 = (bf16[4,256,256]{2,1,0:T(8,128)(2,1)S(1)}, bf16[4,256,256]{2,1,0:T(8,128)(2,1)}, u32[]{:S(2)}) copy-start(bf16[4,256,256]{2,1,0:T(8,128)(2,1)} %param.39) | copy-start | bytes 1572868
  807.7 17.1 %copy-start.11 = (s32[128,10]{0,1:T(8,128)S(1)}, s32[128,10]{0,1:T(8,128)}, u32[]{:S(2)}) copy-start(s32[128,10]{0,1:T(8,128)} %param.36) | copy-start | bytes 15364
  807.8 17.3 %copy-start.12 = (f32[128,10]{0,1:T(8,128)S(1)}, f32[128,10]{0,1:T(8,128)}, u32[]{:S(2)}) copy-start(f32[128,10]{0,1:T(8,128)} %param.37) | copy-start | bytes 15364
  809.3 60.1 %all-to-all-start.1 = ((bf16[64,6,4,256]{3,2,1,0:T(4,128)(2,1)}), bf16[64,6,4,256]{3,2,1,0:T(4,128)(2,1)}, u32[]{:S(2)}, u32[]{:S(2)}) async-start(bf16[64,6,4,256]{3,2,1,0:T(4,128)(2,1)} %bitcast.54), calls=%async_computation.2 | async-start | bytes 1572864 | tf_op jit(solution)/shard_map/all_to_all | solution.py:252
Sparse Core Ops, SparseCore 0:
  80.1 151.2 all-gather.4
  234.4 151.0 all-gather.6
  609.9 41.3 reduce-scatter.1
  734.8 70.4 all-reduce.5
where the time goes:
time: 889 us; the launch traced here: 885 us
  waiting for transfers between devices  447 us (50%)
  matrix products  181 us (20%)
  other arithmetic  104 us (12%)
  blocking collectives  70.9 us (8%)
  local copies, waits for them, and re-layouts  46.1 us (5%)
  starting transfers between devices  18.8 us (2%)
  between operations  13.6 us (2%)
    all_gather x2, waiting for transfers between devices, prefix(): lax.all_gather(part.astype(kind), axis)  296 us
    another operation x16, other arithmetic, delta_block(): lax.linalg.triangular_solve(system, target, left_side=True, lower=True, u...  81.9 us
    dot_general x64, matrix products, compose(): jnp.einsum('hij,hjk->hik', map_late, shift_early, precision=EXACT_ARITHME...  80.9 us
    dot_general x64, matrix products, compose(): jnp.einsum('hij,hjk->hik', map_late, map_early, precision=EXACT_ARITHMETIC)  76.2 us
    psum x1, waiting for transfers between devices, local(): lax.psum(term_rows.reshape(row_count, -1).astype(jnp.bfloat16), 'head')  70.6 us
    all_to_all x1, blocking collectives, local(): lax.all_to_all(outgoing, 'seq', split_axis=0, concat_axis=0, tiled=True)  59 us
    all_to_all x1, waiting for transfers between devices, local(): lax.all_to_all(results.reshape(seq_size, capacity, experts_here, -1), 'se...  44.2 us
    reduce_scatter x1, waiting for transfers between devices, local(): lax.psum_scatter(partial_value.astype(jnp.bfloat16), 'head', scatter_dime...  35.1 us
  transfers between devices with their start and end apart: 6, of which 5 were waited for; matrix products, arithmetic and copies ran while one was open for 2% of the time, Pallas kernels for 0%

commit v1 on v0

--- a/solution.py
+++ b/solution.py
@@ -16,29 +16,6 @@
 
 EPS = 1e-06
 EXACT_ARITHMETIC = lax.Precision.HIGHEST
-
-
-def prefix(value, axis, combine, identity):
-    count, position = (lax.axis_size(axis), lax.axis_index(axis))
-    everything = jax.tree.map(
-        lambda part, kind: lax.all_gather(part.astype(kind), axis),
-        value,
-        (jnp.bfloat16, jnp.bfloat16),
-    )
-    start = jax.tree.map(
-        lambda part, zero: jnp.broadcast_to(jnp.asarray(zero, part.dtype), part.shape),
-        value,
-        identity,
-    )
-
-    def hop(k, before):
-        reached = k < position
-        new = combine(
-            before, jax.tree.map(lambda part, own: part[k].astype(own.dtype), everything, value)
-        )
-        return jax.tree.map(lambda a, b: jnp.where(reached, a, b), new, before)
-
-    return lax.fori_loop(0, count, hop, start)
 
 
 def passed_along(value, axis, steps):
@@ -110,24 +87,31 @@
     return (state_end, outputs)
 
 
-def compose(earlier, later):
-    map_early, shift_early = earlier
-    map_late, shift_late = later
-    joined_map = jnp.einsum("hij,hjk->hik", map_late, map_early, precision=EXACT_ARITHMETIC)
-    joined_shift = (
-        jnp.einsum("hij,hjk->hik", map_late, shift_early, precision=EXACT_ARITHMETIC) + shift_late
-    )
-    return (joined_map, joined_shift)
-
-
 def entering_state(transfer, carried, init_state):
-    identity_maps = jnp.broadcast_to(jnp.eye(DK, dtype=jnp.float32), transfer.shape)
-    prior_map, prior_shift = prefix(
-        (transfer, carried), "seq", compose, (identity_maps, jnp.zeros_like(carried))
-    )
-    return (
-        jnp.einsum("hij,hjk->hik", prior_map, init_state, precision=EXACT_ARITHMETIC) + prior_shift
-    )
+    count, position = (lax.axis_size("seq"), lax.axis_index("seq"))
+    first = position == 0
+    folded = (
+        jnp.einsum("hij,hjk->hik", transfer, init_state, precision=EXACT_ARITHMETIC) + carried
+    )
+    shift = jnp.where(first, folded, carried)
+    mapping = jnp.where(first, jnp.zeros_like(transfer), transfer)
+    step = 1
+    while step < count:
+        if 2 * step >= count:
+            shift_in = passed_along(shift, "seq", step)
+            shift = (
+                jnp.einsum("hij,hjk->hik", mapping, shift_in, precision=EXACT_ARITHMETIC) + shift
+            )
+        else:
+            both_in = passed_along(jnp.concatenate([mapping, shift], axis=2), "seq", step)
+            map_in, shift_in = both_in[:, :, :DK], both_in[:, :, DK:]
+            shift = (
+                jnp.einsum("hij,hjk->hik", mapping, shift_in, precision=EXACT_ARITHMETIC) + shift
+            )
+            mapping = jnp.einsum("hij,hjk->hik", mapping, map_in, precision=EXACT_ARITHMETIC)
+        step *= 2
+    before = passed_along(shift, "seq", 1)
+    return before + first.astype(jnp.float32) * init_state
 
 
 def local(
@@ -177,12 +161,12 @@
     wide_values = jnp.concatenate(
         [values, jnp.zeros((value_heads, length, DK), jnp.float32)], axis=2
     )
-    state_end, unused_out = delta_pass(
-        queries, key_rows, wide_values, beta_rate, log_decay, state_start, False
+    state_end, wide_out = delta_pass(
+        queries, key_rows, wide_values, beta_rate, log_decay, state_start, True
     )
     entering = entering_state(state_end[:, :, DV:], state_end[:, :, :DV], init_state)
-    unused_end, delta_out = delta_pass(
-        queries, key_rows, values, beta_rate, log_decay, entering, True
+    delta_out = wide_out[:, :, :DV] + jnp.einsum(
+        "hlk,hkv->hlv", wide_out[:, :, DV:], entering, precision=EXACT_ARITHMETIC
     )
     delta_out = jnp.transpose(delta_out, (1, 0, 2))
     inv_rms = lax.rsqrt(jnp.mean(delta_out * delta_out, axis=-1, keepdims=True) + EPS)

time: 889 us -> 529 us (0.60)
  waiting for transfers between devices: 447 us -> 241 us
  matrix products: 181 us -> 27 us
  starting transfers between devices: 18.8 us -> 79.1 us
  other arithmetic: 104 us -> 58.7 us
  local copies, waits for them, and re-layouts: 46.1 us -> 35.9 us
    all_gather x2 -> x0, waiting for transfers between devices: 296 us -> none  [prefix(): lax.all_gather(part.astype(kind), axis)]
    dot_general x129 -> x13, matrix products: 158 us -> 9.04 us  [the longest x5 3.86 us: entering_state(): jnp.einsum('hij,hjk->hik', mapping, map_in, precision=EXACT_ARITHMETIC)]
    ppermute x1 -> x8, waiting for transfers between devices: 0.01 us -> 88.2 us  [passed_along(): lax.ppermute(value, axis, [(source, source + steps) for source in range(f...]
    ppermute x1 -> x8, starting transfers between devices: 3.19 us -> 63.7 us  [passed_along(): lax.ppermute(value, axis, [(source, source + steps) for source in range(f...]
    another operation x16 -> x8, other arithmetic: 81.9 us -> 41 us  [delta_block(): lax.linalg.triangular_solve(system, target, left_side=True, lower=True, u...]
  transfers between devices with their start and end apart: 6 -> 11, of which waited for: 5 -> 10; matrix products, arithmetic and copies ran while one was open for 2% -> 3% of each run, Pallas kernels for 0% -> 0%
where the time goes in v1:
time: 529 us; the launch traced here: 527 us
  waiting for transfers between devices  241 us (46%)
  starting transfers between devices  79.1 us (15%)
  blocking collectives  70.8 us (13%)
  other arithmetic  58.7 us (11%)
  local copies, waits for them, and re-layouts  35.9 us (7%)
  matrix products  27 us (5%)
  between operations  14.1 us (3%)
    ppermute x8, waiting for transfers between devices, passed_along(): lax.ppermute(value, axis, [(source, source + steps) for source in range(f...  88.2 us
    psum x1, waiting for transfers between devices, local(): lax.psum(term_rows.reshape(row_count, -1).astype(jnp.bfloat16), 'head')  70.5 us
    ppermute x8, starting transfers between devices, passed_along(): lax.ppermute(value, axis, [(source, source + steps) for source in range(f...  63.7 us
    all_to_all x1, blocking collectives, local(): lax.all_to_all(outgoing, 'seq', split_axis=0, concat_axis=0, tiled=True)  59 us
    all_to_all x1, waiting for transfers between devices, local(): lax.all_to_all(results.reshape(seq_size, capacity, experts_here, -1), 'se...  44.2 us
    another operation x8, other arithmetic, delta_block(): lax.linalg.triangular_solve(system, target, left_side=True, lower=True, u...  41 us
    reduce_scatter x1, waiting for transfers between devices, local(): lax.psum_scatter(partial_value.astype(jnp.bfloat16), 'head', scatter_dime...  38.4 us
    all_to_all x1, starting transfers between devices, local(): lax.all_to_all(results.reshape(seq_size, capacity, experts_here, -1), 'se...  15.3 us
  transfers between devices with their start and end apart: 11, of which 10 were waited for; matrix products, arithmetic and copies ran while one was open for 3% of the time, Pallas kernels for 0%

profile of v1, /device:TPU:15, one launch (start us, length us, event | category | flops | bytes accessed | tf_op | source)
XLA Modules:
  0.0 527.1 jit_solution(4921147383437931352)
XLA Ops:
  7.4 3.2 collective-permute-start
  21.2 57.3 %while.12 = (s32[]{:T(128)}, f32[4,128,256]{2,1,0:T(8,128)S(1)}, f32[2,4,64,256]{3,2,1,0:T(8,128)}, f32[2,4,64]{2,0,1:T(2,128)}, f32[2,4,64,128]{3,2,0,1:T(8,128...) while((s32[]{:T(128)}, f32[4,128,256]{2,1,0:T(8,128)S(1)}, ...), condition=%wide.region_4.5_spmd, body=%wide.region_2.4_spmd.sunk | while | flops 453865536 | bytes 5678793 | solution.py:74
  25.6 20.4 %custom-call.9 = f32[4,1,64,64]{2,3,1,0:T(8,128)S(1)} custom-call(f32[4,1,64,64]{3,2,1,0:T(8,128)} %fusion.149), custom_call_target="InvertDiagBlocksLowerTriangular" | custom-call | tf_op jit(solution)/shard_map/while/body/eval_jaxpr/triangular_solve | solution.py:47
  54.3 20.4 %custom-call.9 = f32[4,1,64,64]{2,3,1,0:T(8,128)S(1)} custom-call(f32[4,1,64,64]{3,2,1,0:T(8,128)} %fusion.149), custom_call_target="InvertDiagBlocksLowerTriangular" | custom-call | tf_op jit(solution)/shard_map/while/body/eval_jaxpr/triangular_solve | solution.py:47
  80.0 2.9 collective-permute-start.1
  82.9 11.5 %collective-permute-done.1 = f32[4,128,256]{2,1,0:T(8,128)S(1)} collective-permute-done((f32[4,128,256]{2,1,0:T(8,128)S(1)}, f32[4,128,256]{2,1,0:T(8,128)S(1)}, u32[]{:S(2)}, u32[]{:S(2)}) %collective-permute-start.1) | collective-permute-done | bytes 524320 | tf_op jit(solution)/shard_map/ppermute | solution.py:24
  95.3 4.0 collective-permute-start.2
  99.3 9.4 %collective-permute-done.2 = f32[4,128,256]{2,1,0:T(8,128)S(1)} collective-permute-done((f32[4,128,256]{2,1,0:T(8,128)S(1)}, f32[4,128,256]{2,1,0:T(8,128)S(1)}, u32[]{:S(2)}, u32[]{:S(2)}) %collective-permute-start.2) | collective-permute-done | bytes 524320 | tf_op jit(solution)/shard_map/ppermute | solution.py:24
  109.6 6.3 %collective-permute-start.3 = (f32[4,128,256]{2,1,0:T(8,128)S(1)}, f32[4,128,256]{2,1,0:T(8,128)S(1)}, u32[]{:S(2)}, u32[]{:S(2)}) collective-permute-start(f32[4,128,256]{2,1,0:T(8,128)S(1)} %pad_maximum_fusion.3), channel_id=1, source_target_pairs={{0,32},{8,40},{16,48},{24,56},{32,64},{40,72},{48,80},{56,88},{64,... | collective-permute-start | bytes 1572872 | tf_op jit(solution)/shard_map/ppermute | solution.py:24
  115.9 8.6 %collective-permute-done.3 = f32[4,128,256]{2,1,0:T(8,128)S(1)} collective-permute-done((f32[4,128,256]{2,1,0:T(8,128)S(1)}, f32[4,128,256]{2,1,0:T(8,128)S(1)}, u32[]{:S(2)}, u32[]{:S(2)}) %collective-permute-start.3) | collective-permute-done | bytes 524320 | tf_op jit(solution)/shard_map/ppermute | solution.py:24
  126.1 6.2 %collective-permute-start.4 = (f32[4,128,256]{2,1,0:T(8,128)}, f32[4,128,256]{2,1,0:T(8,128)}, u32[]{:S(2)}, u32[]{:S(2)}) collective-permute-start(f32[4,128,256]{2,1,0:T(8,128)} %pad_maximum_fusion.4), channel_id=1, source_target_pairs={{0,64},{8,72},{16,80},{24,88},{32,96},{40,104},{48,112},{56,120},{... | collective-permute-start | bytes 1572872 | tf_op jit(solution)/shard_map/ppermute | solution.py:24
  132.8 6.8 %collective-permute-done.4 = f32[4,128,256]{2,1,0:T(8,128)} collective-permute-done((f32[4,128,256]{2,1,0:T(8,128)}, f32[4,128,256]{2,1,0:T(8,128)}, u32[]{:S(2)}, u32[]{:S(2)}) %collective-permute-start.4) | collective-permute-done | bytes 524320 | tf_op jit(solution)/shard_map/ppermute | solution.py:24
  142.4 23.8 %collective-permute-start.5 = (f32[4,128,256]{2,1,0:T(8,128)S(1)}, f32[4,128,256]{2,1,0:T(8,128)S(1)}, u32[]{:S(2)}, u32[]{:S(2)}) collective-permute-start(f32[4,128,256]{2,1,0:T(8,128)S(1)} %pad_maximum_fusion.5), channel_id=1, source_target_pairs={{0,128},{8,136},{16,144},{24,152},{32,160},{40,168},{48,176},{56,1... | collective-permute-start | bytes 1572872 | tf_op jit(solution)/shard_map/ppermute | solution.py:24
  166.6 6.7 %collective-permute-done.5 = f32[4,128,256]{2,1,0:T(8,128)S(1)} collective-permute-done((f32[4,128,256]{2,1,0:T(8,128)S(1)}, f32[4,128,256]{2,1,0:T(8,128)S(1)}, u32[]{:S(2)}, u32[]{:S(2)}) %collective-permute-start.5) | collective-permute-done | bytes 524320 | tf_op jit(solution)/shard_map/ppermute | solution.py:24
  174.1 15.2 %collective-permute-start.6 = (f32[4,128,128]{2,1,0:T(8,128)S(1)}, f32[4,128,128]{2,1,0:T(8,128)S(1)}, u32[]{:S(2)}, u32[]{:S(2)}) collective-permute-start(f32[4,128,128]{2,1,0:T(8,128)S(1)} %convolution_add_fusion.4), channel_id=1, source_target_pairs={{0,256},{8,264},{16,272},{24,280},{32,288},{40,296},{48,304},{56,3... | collective-permute-start | bytes 786440 | tf_op jit(solution)/shard_map/ppermute | solution.py:24
  193.0 2.1 collective-permute-start.7
  195.1 1.8 broadcast_add_fusion
  198.0 44.3 %collective-permute-done.7 = f32[4,128,128]{2,1,0:T(8,128)S(1)} collective-permute-done((f32[4,128,128]{2,1,0:T(8,128)S(1)}, f32[4,128,128]{2,1,0:T(8,128)S(1)}, u32[]{:S(2)}, u32[]{:S(2)}) %collective-permute-start.7) | collective-permute-done | bytes 262176 | tf_op jit(solution)/shard_map/ppermute | solution.py:24
  243.7 1.7 copy.197
  245.3 2.2 convolution_convert_fusion
  249.5 5.2 scatter_custom_fusion
  255.0 38.4 %reduce-scatter.2.cloned.1.call-done = bf16[128,256]{1,0:T(8,128)(2,1)} async-done(((bf16[128,2048]{1,0:T(8,128)(2,1)}), bf16[128,256]{1,0:T(8,128)(2,1)}) %reduce-scatter.2.cloned.1.call-update) | async-done | bytes 65552 | tf_op jit(solution)/shard_map/reduce_scatter | solution.py:180
  295.6 11.9 %all-reduce.3 = (f32[128]{0:T(128)S(1)}, f32[128]{0:T(128)S(1)}) all-reduce(f32[128]{0:T(128)S(1)} %get-tuple-element.112, f32[128]{0:T(128)S(1)} %multiply_reduce_fusion.3), channel_id=1, replica_groups=mesh['seq'=64,'head'=8] {'head'}, use_global_device_ids=true, to_apply=%region_10.11 | all-reduce | flops 256 | bytes 2048 | tf_op jit(solution)/shard_map/psum | solution.py:190
  308.3 5.3 %gather_fusion = bf16[1536,256]{1,0:T(8,128)(2,1)} fusion(bf16[129,256]{1,0:T(8,128)(2,1)S(1)} %concatenate.35, s32[2048]{0:T(1024)S(1)} %pad_clamp_fusion.1), kind=kCustom, calls=%fused_computation | custom fusion | bytes 1579008 | tf_op jit(solution)/shard_map/jit(_take)/gather | solution.py:217
  313.6 1.7 gather.13
  316.0 59.0 %all_to_all.10 = bf16[64,6,4,256]{3,2,1,0:T(4,128)(2,1)S(1)} all-to-all(bf16[64,6,4,256]{3,2,1,0:T(4,128)(2,1)S(1)} %broadcast_select_fusion), channel_id=1, replica_groups=mesh['seq'=64,'head'=8] {'seq'}, dimensions={0} | all-to-all | bytes 1572864 | tf_op jit(solution)/shard_map/all_to_all | solution.py:218
  375.0 1.7 fusion.34
  376.7 70.5 %all-reduce.6.cloned.1.call-done = bf16[384,4,512]{2,0,1:T(8,128)(2,1)} async-done(((bf16[384,4,512]{2,0,1:T(8,128)(2,1)}), bf16[384,4,512]{2,0,1:T(8,128)(2,1)}) %all-reduce.6.cloned.1.call-update) | async-done | bytes 1572880 | tf_op jit(solution)/shard_map/psum | solution.py:223
  447.2 1.8 reshape.313
  451.2 15.3 %all-to-all-start.1 = ((bf16[64,6,4,256]{3,2,1,0:T(4,128)(2,1)}), bf16[64,6,4,256]{3,2,1,0:T(4,128)(2,1)}, u32[]{:S(2)}, u32[]{:S(2)}) async-start(bf16[64,6,4,256]{3,2,1,0:T(4,128)(2,1)} %bitcast.38), calls=%async_computation.2 | async-start | bytes 1572864 | tf_op jit(solution)/shard_map/all_to_all | solution.py:236
  467.1 44.2 %all-to-all-done.1 = bf16[64,6,4,256]{3,2,1,0:T(4,128)(2,1)} async-done(((bf16[64,6,4,256]{3,2,1,0:T(4,128)(2,1)}), bf16[64,6,4,256]{3,2,1,0:T(4,128)(2,1)}, u32[]{:S(2)}, u32[]{:S(2)}) %all-to-all-start.1) | async-done | bytes 786464 | tf_op jit(solution)/shard_map/all_to_all | solution.py:236
  512.8 4.7 gather_fusion.1
  (149 shorter events, 55.7 us)
Async XLA Ops:
  6.5 238.8 %copy-start = (bf16[512,2048]{1,0:T(8,128)(2,1)S(1)}, bf16[512,2048]{1,0:T(8,128)(2,1)}, u32[]{:S(2)}) copy-start(bf16[512,2048]{1,0:T(8,128)(2,1)} %param.28) | copy-start | bytes 6291460
  6.5 286.9 %reduce-scatter.2.cloned.1.call-start = ((), (), s32[]{:S(2)}) async-start(), calls=%async_computation.3 | async-start | bytes 589824 | tf_op jit(solution)/shard_map/reduce_scatter | solution.py:180
  7.4 7.9 %collective-permute-start = (bf16[3,1024]{1,0:T(4,128)(2,1)S(1)}, bf16[3,1024]{1,0:T(4,128)(2,1)S(1)}, u32[]{:S(2)}, u32[]{:S(2)}) collective-permute-start(bf16[3,1024]{1,0:T(4,128)(2,1)S(1)} %slice.100), channel_id=1, source_target_pairs={{0,8},{8,16},{16,24},{24,32},{32,40},{40,48},{48,56},{56,64},{64,7... | collective-permute-start | bytes 18440 | tf_op jit(solution)/shard_map/ppermute | solution.py:24
  80.0 14.4 %collective-permute-start.1 = (f32[4,128,256]{2,1,0:T(8,128)S(1)}, f32[4,128,256]{2,1,0:T(8,128)S(1)}, u32[]{:S(2)}, u32[]{:S(2)}) collective-permute-start(f32[4,128,256]{2,1,0:T(8,128)S(1)} %pad_maximum_fusion.1), channel_id=1, source_target_pairs={{0,8},{8,16},{16,24},{24,32},{32,40},{40,48},{48,56},{56,64},{64,7... | collective-permute-start | bytes 1572872 | tf_op jit(solution)/shard_map/ppermute | solution.py:24
  95.3 13.4 %collective-permute-start.2 = (f32[4,128,256]{2,1,0:T(8,128)S(1)}, f32[4,128,256]{2,1,0:T(8,128)S(1)}, u32[]{:S(2)}, u32[]{:S(2)}) collective-permute-start(f32[4,128,256]{2,1,0:T(8,128)S(1)} %pad_maximum_fusion.2), channel_id=1, source_target_pairs={{0,16},{8,24},{16,32},{24,40},{32,48},{40,56},{48,64},{56,72},{64,... | collective-permute-start | bytes 1572872 | tf_op jit(solution)/shard_map/ppermute | solution.py:24
  109.5 22.9 %copy-start.8 = (bf16[128,512]{1,0:T(8,128)(2,1)S(1)}, bf16[128,512]{1,0:T(8,128)(2,1)}, u32[]{:S(2)}) copy-start(bf16[128,512]{1,0:T(8,128)(2,1)} %param.23) | copy-start | bytes 393220
  109.5 23.0 %copy-start.9 = (s32[128,10]{0,1:T(8,128)S(1)}, s32[128,10]{0,1:T(8,128)}, u32[]{:S(2)}) copy-start(s32[128,10]{0,1:T(8,128)} %param.32) | copy-start | bytes 15364
  109.6 14.9 %collective-permute-start.3 = (f32[4,128,256]{2,1,0:T(8,128)S(1)}, f32[4,128,256]{2,1,0:T(8,128)S(1)}, u32[]{:S(2)}, u32[]{:S(2)}) collective-permute-start(f32[4,128,256]{2,1,0:T(8,128)S(1)} %pad_maximum_fusion.3), channel_id=1, source_target_pairs={{0,32},{8,40},{16,48},{24,56},{32,64},{40,72},{48,80},{56,88},{64,... | collective-permute-start | bytes 1572872 | tf_op jit(solution)/shard_map/ppermute | solution.py:24
  126.1 13.5 %collective-permute-start.4 = (f32[4,128,256]{2,1,0:T(8,128)}, f32[4,128,256]{2,1,0:T(8,128)}, u32[]{:S(2)}, u32[]{:S(2)}) collective-permute-start(f32[4,128,256]{2,1,0:T(8,128)} %pad_maximum_fusion.4), channel_id=1, source_target_pairs={{0,64},{8,72},{16,80},{24,88},{32,96},{40,104},{48,112},{56,120},{... | collective-permute-start | bytes 1572872 | tf_op jit(solution)/shard_map/ppermute | solution.py:24
  142.4 30.9 %collective-permute-start.5 = (f32[4,128,256]{2,1,0:T(8,128)S(1)}, f32[4,128,256]{2,1,0:T(8,128)S(1)}, u32[]{:S(2)}, u32[]{:S(2)}) collective-permute-start(f32[4,128,256]{2,1,0:T(8,128)S(1)} %pad_maximum_fusion.5), channel_id=1, source_target_pairs={{0,128},{8,136},{16,144},{24,152},{32,160},{40,168},{48,176},{56,1... | collective-permute-start | bytes 1572872 | tf_op jit(solution)/shard_map/ppermute | solution.py:24
  166.6 22.8 %copy-start.1 = (s32[256,10,128]{0,1,2:T(8,128)}, s32[256,10,128]{0,1,2:T(8,128)S(1)}, u32[]{:S(2)}) copy-start(s32[256,10,128]{0,1,2:T(8,128)S(1)} %fusion.31) | copy-start | bytes 3932164
  173.3 0.8 copy-start.6
  174.1 18.5 %collective-permute-start.6 = (f32[4,128,128]{2,1,0:T(8,128)S(1)}, f32[4,128,128]{2,1,0:T(8,128)S(1)}, u32[]{:S(2)}, u32[]{:S(2)}) collective-permute-start(f32[4,128,128]{2,1,0:T(8,128)S(1)} %convolution_add_fusion.4), channel_id=1, source_target_pairs={{0,256},{8,264},{16,272},{24,280},{32,288},{40,296},{48,304},{56,3... | collective-permute-start | bytes 786440 | tf_op jit(solution)/shard_map/ppermute | solution.py:24
  193.0 49.3 %collective-permute-start.7 = (f32[4,128,128]{2,1,0:T(8,128)S(1)}, f32[4,128,128]{2,1,0:T(8,128)S(1)}, u32[]{:S(2)}, u32[]{:S(2)}) collective-permute-start(f32[4,128,128]{2,1,0:T(8,128)S(1)} %convolution_add_fusion.3), channel_id=1, source_target_pairs={{0,8},{8,16},{16,24},{24,32},{32,40},{40,48},{48,56},{56,64},{64,7... | collective-permute-start | bytes 786440 | tf_op jit(solution)/shard_map/ppermute | solution.py:24
  197.0 1.0 copy-start.5
  197.0 45.4 %copy-start.4 = (f32[4,128,128]{2,1,0:T(8,128)S(1)}, f32[4,128,128]{2,1,0:T(8,128)}, u32[]{:S(2)}) copy-start(f32[4,128,128]{2,1,0:T(8,128)} %param.26) | copy-start | bytes 786436
  197.0 45.9 %copy-start.3 = (f32[128,4,128]{2,0,1:T(8,128)S(1)}, f32[128,4,128]{2,0,1:T(8,128)}, u32[]{:S(2)}) copy-start(f32[128,4,128]{2,0,1:T(8,128)} %copy.196) | copy-start | bytes 786436
  197.0 45.9 %copy-start.11 = (f32[128]{0:T(128)S(1)}, f32[128]{0:T(128)}, u32[]{:S(2)}) copy-start(f32[128]{0:T(128)} %param.27) | copy-start | bytes 1540
  245.3 48.1 %copy-start.7 = (bf16[128,256]{1,0:T(8,128)(2,1)S(1)}, bf16[128,256]{1,0:T(8,128)(2,1)}, u32[]{:S(2)}) copy-start(bf16[128,256]{1,0:T(8,128)(2,1)} %param.19) | copy-start | bytes 196612
  247.5 199.7 %all-reduce.6.cloned.1.call-start = ((), (), s32[]{:S(2)}) async-start(), calls=%async_computation.4 | async-start | bytes 3145728 | tf_op jit(solution)/shard_map/psum | solution.py:223
  315.3 59.7 %copy-start.2 = (bf16[4,256,512]{2,1,0:T(8,128)(2,1)S(1)}, bf16[4,256,512]{2,1,0:T(8,128)(2,1)}, u32[]{:S(2)}) copy-start(bf16[4,256,512]{2,1,0:T(8,128)(2,1)} %param.34) | copy-start | bytes 3145732
  376.7 72.4 %copy-start.12 = (bf16[4,256,256]{2,1,0:T(8,128)(2,1)S(1)}, bf16[4,256,256]{2,1,0:T(8,128)(2,1)}, u32[]{:S(2)}) copy-start(bf16[4,256,256]{2,1,0:T(8,128)(2,1)} %param.35) | copy-start | bytes 1572868
  449.7 17.3 %copy-start.10 = (f32[128,10]{0,1:T(8,128)S(1)}, f32[128,10]{0,1:T(8,128)}, u32[]{:S(2)}) copy-start(f32[128,10]{0,1:T(8,128)} %param.33) | copy-start | bytes 15364
  451.2 60.1 %all-to-all-start.1 = ((bf16[64,6,4,256]{3,2,1,0:T(4,128)(2,1)}), bf16[64,6,4,256]{3,2,1,0:T(4,128)(2,1)}, u32[]{:S(2)}, u32[]{:S(2)}) async-start(bf16[64,6,4,256]{3,2,1,0:T(4,128)(2,1)} %bitcast.38), calls=%async_computation.2 | async-start | bytes 1572864 | tf_op jit(solution)/shard_map/all_to_all | solution.py:236
Sparse Core Ops, SparseCore 0:
  247.7 45.7 reduce-scatter.1
  376.8 70.3 all-reduce.5

commit v2 on v1

--- a/solution.py
+++ b/solution.py
@@ -87,31 +87,39 @@
     return (state_end, outputs)
 
 
+SCAN_RADIX = 4
+
+
+def compose(later, earlier):
+    joined = jnp.einsum("hij,hjk->hik", later[:, :, :DK], earlier, precision=EXACT_ARITHMETIC)
+    return joined + jnp.concatenate([jnp.zeros_like(later[:, :, :DK]), later[:, :, DK:]], axis=2)
+
+
 def entering_state(transfer, carried, init_state):
     count, position = (lax.axis_size("seq"), lax.axis_index("seq"))
     first = position == 0
     folded = (
         jnp.einsum("hij,hjk->hik", transfer, init_state, precision=EXACT_ARITHMETIC) + carried
     )
-    shift = jnp.where(first, folded, carried)
-    mapping = jnp.where(first, jnp.zeros_like(transfer), transfer)
-    step = 1
-    while step < count:
-        if 2 * step >= count:
-            shift_in = passed_along(shift, "seq", step)
-            shift = (
-                jnp.einsum("hij,hjk->hik", mapping, shift_in, precision=EXACT_ARITHMETIC) + shift
-            )
-        else:
-            both_in = passed_along(jnp.concatenate([mapping, shift], axis=2), "seq", step)
-            map_in, shift_in = both_in[:, :, :DK], both_in[:, :, DK:]
-            shift = (
-                jnp.einsum("hij,hjk->hik", mapping, shift_in, precision=EXACT_ARITHMETIC) + shift
-            )
-            mapping = jnp.einsum("hij,hjk->hik", mapping, map_in, precision=EXACT_ARITHMETIC)
-        step *= 2
-    before = passed_along(shift, "seq", 1)
-    return before + first.astype(jnp.float32) * init_state
+    own = jnp.concatenate(
+        [
+            jnp.where(first, jnp.zeros_like(transfer), transfer),
+            jnp.where(first, folded, carried),
+        ],
+        axis=2,
+    )
+    inclusive = own
+    exclusive = None
+    span = 1
+    while span < count:
+        for j in range(1, SCAN_RADIX):
+            if span * j < count:
+                part = passed_along(inclusive, "seq", span * j)
+                exclusive = part if exclusive is None else compose(exclusive, part)
+        span *= SCAN_RADIX
+        if span < count:
+            inclusive = compose(own, exclusive)
+    return jnp.where(first, init_state, exclusive[:, :, DK:])
 
 
 def local(

time: 529 us -> 589 us (1.11)
  starting transfers between devices: 79.1 us -> 123 us
  matrix products: 27 us -> 35.5 us
    ppermute x8 -> x10, starting transfers between devices: 63.7 us -> 108 us  [passed_along(): lax.ppermute(value, axis, [(source, source + steps) for source in range(f...]
    dot_general x11 -> x10, matrix products: 7.19 us -> 15.7 us  [compose(): jnp.einsum('hij,hjk->hik', later[:, :, :DK], earlier, precision=EXACT_ARI...]
    ppermute x8 -> x10, waiting for transfers between devices: 88.2 us -> 95.8 us  [passed_along(): lax.ppermute(value, axis, [(source, source + steps) for source in range(f...]
  transfers between devices with their start and end apart: 11 -> 13, of which waited for: 10 -> 10; matrix products, arithmetic and copies ran while one was open for 3% -> 5% of each run, Pallas kernels for 0% -> 0%
where the time goes in v2:
time: 589 us; the launch traced here: 588 us
  waiting for transfers between devices  246 us (42%)
  starting transfers between devices  123 us (21%)
  blocking collectives  70.7 us (12%)
  other arithmetic  58.4 us (10%)
  local copies, waits for them, and re-layouts  39.9 us (7%)
  matrix products  35.5 us (6%)
  between operations  14.1 us (2%)
    ppermute x10, starting transfers between devices, passed_along(): lax.ppermute(value, axis, [(source, source + steps) for source in range(f...  108 us
    ppermute x10, waiting for transfers between devices, passed_along(): lax.ppermute(value, axis, [(source, source + steps) for source in range(f...  95.8 us
    psum x1, waiting for transfers between devices, local(): lax.psum(term_rows.reshape(row_count, -1).astype(jnp.bfloat16), 'head')  70.5 us
    all_to_all x1, blocking collectives, local(): lax.all_to_all(outgoing, 'seq', split_axis=0, concat_axis=0, tiled=True)  58.8 us
    all_to_all x1, waiting for transfers between devices, local(): lax.all_to_all(results.reshape(seq_size, capacity, experts_here, -1), 'se...  44.2 us
    another operation x8, other arithmetic, delta_block(): lax.linalg.triangular_solve(system, target, left_side=True, lower=True, u...  41 us
    reduce_scatter x1, waiting for transfers between devices, local(): lax.psum_scatter(partial_value.astype(jnp.bfloat16), 'head', scatter_dime...  35.2 us
    dot_general x10, matrix products, compose(): jnp.einsum('hij,hjk->hik', later[:, :, :DK], earlier, precision=EXACT_ARI...  15.7 us
  transfers between devices with their start and end apart: 13, of which 10 were waited for; matrix products, arithmetic and copies ran while one was open for 5% of the time, Pallas kernels for 0%

profile of v2, /device:TPU:15, one launch (start us, length us, event | category | flops | bytes accessed | tf_op | source)
XLA Modules:
  0.0 587.6 jit_solution(9796683793087596971)
XLA Ops:
  7.4 3.2 collective-permute-start
  21.2 57.3 %while.12 = (s32[]{:T(128)}, f32[4,128,256]{2,1,0:T(8,128)S(1)}, f32[2,4,64,256]{3,2,1,0:T(8,128)}, f32[2,4,64]{2,0,1:T(2,128)}, f32[2,4,64,128]{3,2,0,1:T(8,128...) while((s32[]{:T(128)}, f32[4,128,256]{2,1,0:T(8,128)S(1)}, ...), condition=%wide.region_4.5_spmd, body=%wide.region_2.4_spmd.sunk | while | flops 453865536 | bytes 5678793 | solution.py:74
  25.6 20.4 %custom-call.9 = f32[4,1,64,64]{2,3,1,0:T(8,128)S(1)} custom-call(f32[4,1,64,64]{3,2,1,0:T(8,128)} %fusion.145), custom_call_target="InvertDiagBlocksLowerTriangular" | custom-call | tf_op jit(solution)/shard_map/while/body/eval_jaxpr/triangular_solve | solution.py:47
  54.2 20.4 %custom-call.9 = f32[4,1,64,64]{2,3,1,0:T(8,128)S(1)} custom-call(f32[4,1,64,64]{3,2,1,0:T(8,128)} %fusion.145), custom_call_target="InvertDiagBlocksLowerTriangular" | custom-call | tf_op jit(solution)/shard_map/while/body/eval_jaxpr/triangular_solve | solution.py:47
  80.8 2.9 collective-permute-start.1
  83.7 4.3 collective-permute-start.2
  88.0 4.8 collective-permute-start.3
  93.2 2.4 collective-permute-done.1
  96.5 1.8 collective-permute-done.2
  99.9 2.2 collective-permute-done.3
  105.2 27.6 %collective-permute-start.4 = (f32[4,128,256]{2,1,0:T(8,128)}, f32[4,128,256]{2,1,0:T(8,128)}, u32[]{:S(2)}, u32[]{:S(2)}) collective-permute-start(f32[4,128,256]{2,1,0:T(8,128)} %convolution_add_fusion.8), channel_id=1, source_target_pairs={{0,32},{8,40},{16,48},{24,56},{32,64},{40,72},{48,80},{56,88},{64,... | collective-permute-start | bytes 1572872 | tf_op jit(solution)/shard_map/ppermute | solution.py:24
  132.7 4.9 collective-permute-start.5
  138.0 7.5 %collective-permute-start.6 = (f32[4,128,256]{2,1,0:T(8,128)}, f32[4,128,256]{2,1,0:T(8,128)}, u32[]{:S(2)}, u32[]{:S(2)}) collective-permute-start(f32[4,128,256]{2,1,0:T(8,128)} %convolution_add_fusion.8), channel_id=1, source_target_pairs={{0,96},{8,104},{16,112},{24,120},{32,128},{40,136},{48,144},{56,15... | collective-permute-start | bytes 1572872 | tf_op jit(solution)/shard_map/ppermute | solution.py:24
  147.2 5.5 collective-permute-done.5
  154.4 9.6 %collective-permute-done.6 = f32[4,128,256]{2,1,0:T(8,128)} collective-permute-done((f32[4,128,256]{2,1,0:T(8,128)}, f32[4,128,256]{2,1,0:T(8,128)}, u32[]{:S(2)}, u32[]{:S(2)}) %collective-permute-start.6) | collective-permute-done | bytes 524320 | tf_op jit(solution)/shard_map/ppermute | solution.py:24
  167.8 33.1 %collective-permute-start.7 = (f32[4,128,256]{2,1,0:T(8,128)}, f32[4,128,256]{2,1,0:T(8,128)}, u32[]{:S(2)}, u32[]{:S(2)}) collective-permute-start(f32[4,128,256]{2,1,0:T(8,128)} %convolution_add_fusion.4), channel_id=1, source_target_pairs={{0,128},{8,136},{16,144},{24,152},{32,160},{40,168},{48,176},{56,1... | collective-permute-start | bytes 1572872 | tf_op jit(solution)/shard_map/ppermute | solution.py:24
  200.9 17.6 %collective-permute-start.8 = (f32[4,128,256]{2,1,0:T(8,128)}, f32[4,128,256]{2,1,0:T(8,128)}, u32[]{:S(2)}, u32[]{:S(2)}) collective-permute-start(f32[4,128,256]{2,1,0:T(8,128)} %convolution_add_fusion.4), channel_id=1, source_target_pairs={{0,256},{8,264},{16,272},{24,280},{32,288},{40,296},{48,304},{56,3... | collective-permute-start | bytes 1572872 | tf_op jit(solution)/shard_map/ppermute | solution.py:24
  220.2 2.1 collective-permute-start.9
  223.3 2.4 copy.107
  230.4 74.0 %collective-permute-done.9 = f32[4,128,256]{2,1,0:T(8,128)} collective-permute-done((f32[4,128,256]{2,1,0:T(8,128)}, f32[4,128,256]{2,1,0:T(8,128)}, u32[]{:S(2)}, u32[]{:S(2)}) %collective-permute-start.9) | collective-permute-done | bytes 524320 | tf_op jit(solution)/shard_map/ppermute | solution.py:24
  309.1 2.2 convolution_convert_fusion
  313.3 5.2 scatter_custom_fusion
  318.8 35.2 %reduce-scatter.2.cloned.1.call-done = bf16[128,256]{1,0:T(8,128)(2,1)} async-done(((bf16[128,2048]{1,0:T(8,128)(2,1)}), bf16[128,256]{1,0:T(8,128)(2,1)}) %reduce-scatter.2.cloned.1.call-update) | async-done | bytes 65552 | tf_op jit(solution)/shard_map/reduce_scatter | solution.py:188
  356.1 11.9 %all-reduce.12 = (f32[128]{0:T(128)S(1)}, f32[128]{0:T(128)S(1)}) all-reduce(f32[128]{0:T(128)S(1)} %get-tuple-element.112, f32[128]{0:T(128)S(1)} %multiply_reduce_fusion.3), channel_id=1, replica_groups=mesh['seq'=64,'head'=8] {'head'}, use_global_device_ids=true, to_apply=%region_10.11 | all-reduce | flops 256 | bytes 2048 | tf_op jit(solution)/shard_map/psum | solution.py:198
  368.8 5.3 gather_fusion
  376.6 58.8 %all_to_all.10 = bf16[64,6,4,256]{3,2,1,0:T(4,128)(2,1)S(1)} all-to-all(bf16[64,6,4,256]{3,2,1,0:T(4,128)(2,1)S(1)} %broadcast_select_fusion), channel_id=1, replica_groups=mesh['seq'=64,'head'=8] {'seq'}, dimensions={0} | all-to-all | bytes 1572864 | tf_op jit(solution)/shard_map/all_to_all | solution.py:226
  435.4 1.7 fusion.34
  437.2 70.5 %all-reduce.15.cloned.1.call-done = bf16[384,4,512]{2,0,1:T(8,128)(2,1)} async-done(((bf16[384,4,512]{2,0,1:T(8,128)(2,1)}), bf16[384,4,512]{2,0,1:T(8,128)(2,1)}) %all-reduce.15.cloned.1.call-update) | async-done | bytes 1572880 | tf_op jit(solution)/shard_map/psum | solution.py:231
  507.7 1.8 reshape.313
  511.7 15.3 %all-to-all-start.1 = ((bf16[64,6,4,256]{3,2,1,0:T(4,128)(2,1)}), bf16[64,6,4,256]{3,2,1,0:T(4,128)(2,1)}, u32[]{:S(2)}, u32[]{:S(2)}) async-start(bf16[64,6,4,256]{3,2,1,0:T(4,128)(2,1)} %bitcast.38), calls=%async_computation.2 | async-start | bytes 1572864 | tf_op jit(solution)/shard_map/all_to_all | solution.py:244
  527.5 44.2 %all-to-all-done.1 = bf16[64,6,4,256]{3,2,1,0:T(4,128)(2,1)} async-done(((bf16[64,6,4,256]{3,2,1,0:T(4,128)(2,1)}), bf16[64,6,4,256]{3,2,1,0:T(4,128)(2,1)}, u32[]{:S(2)}, u32[]{:S(2)}) %all-to-all-start.1) | async-done | bytes 786464 | tf_op jit(solution)/shard_map/all_to_all | solution.py:244
  573.3 4.7 gather_fusion.1
  (159 shorter events, 69.7 us)
Async XLA Ops:
  6.5 302.5 %copy-start = (bf16[512,2048]{1,0:T(8,128)(2,1)S(1)}, bf16[512,2048]{1,0:T(8,128)(2,1)}, u32[]{:S(2)}) copy-start(bf16[512,2048]{1,0:T(8,128)(2,1)} %param.28) | copy-start | bytes 6291460
  6.5 347.4 %reduce-scatter.2.cloned.1.call-start = ((), (), s32[]{:S(2)}) async-start(), calls=%async_computation.3 | async-start | bytes 589824 | tf_op jit(solution)/shard_map/reduce_scatter | solution.py:188
  7.4 7.9 %collective-permute-start = (bf16[3,1024]{1,0:T(4,128)(2,1)S(1)}, bf16[3,1024]{1,0:T(4,128)(2,1)S(1)}, u32[]{:S(2)}, u32[]{:S(2)}) collective-permute-start(bf16[3,1024]{1,0:T(4,128)(2,1)S(1)} %slice.121), channel_id=1, source_target_pairs={{0,8},{8,16},{16,24},{24,32},{32,40},{40,48},{48,56},{56,64},{64,7... | collective-permute-start | bytes 18440 | tf_op jit(solution)/shard_map/ppermute | solution.py:24
  78.6 14.2 %copy-start.10 = (s32[128,10]{0,1:T(8,128)S(1)}, s32[128,10]{0,1:T(8,128)}, u32[]{:S(2)}) copy-start(s32[128,10]{0,1:T(8,128)} %param.32) | copy-start | bytes 15364
  80.8 14.7 %collective-permute-start.1 = (f32[4,128,256]{2,1,0:T(8,128)}, f32[4,128,256]{2,1,0:T(8,128)}, u32[]{:S(2)}, u32[]{:S(2)}) collective-permute-start(f32[4,128,256]{2,1,0:T(8,128)} %pad_maximum_fusion.1), channel_id=1, source_target_pairs={{0,8},{8,16},{16,24},{24,32},{32,40},{40,48},{48,56},{56,64},{64,7... | collective-permute-start | bytes 1572872 | tf_op jit(solution)/shard_map/ppermute | solution.py:24
  83.7 14.6 %collective-permute-start.2 = (f32[4,128,256]{2,1,0:T(8,128)}, f32[4,128,256]{2,1,0:T(8,128)S(1)}, u32[]{:S(2)}, u32[]{:S(2)}) collective-permute-start(f32[4,128,256]{2,1,0:T(8,128)} %pad_maximum_fusion.1), channel_id=1, source_target_pairs={{0,16},{8,24},{16,32},{24,40},{32,48},{40,56},{48,64},{56,72},{64,... | collective-permute-start | bytes 1572872 | tf_op jit(solution)/shard_map/ppermute | solution.py:24
  88.0 14.2 %collective-permute-start.3 = (f32[4,128,256]{2,1,0:T(8,128)}, f32[4,128,256]{2,1,0:T(8,128)}, u32[]{:S(2)}, u32[]{:S(2)}) collective-permute-start(f32[4,128,256]{2,1,0:T(8,128)} %pad_maximum_fusion.1), channel_id=1, source_target_pairs={{0,24},{8,32},{16,40},{24,48},{32,56},{40,64},{48,72},{56,80},{64,... | collective-permute-start | bytes 1572872 | tf_op jit(solution)/shard_map/ppermute | solution.py:24
  105.2 40.3 %collective-permute-start.4 = (f32[4,128,256]{2,1,0:T(8,128)}, f32[4,128,256]{2,1,0:T(8,128)}, u32[]{:S(2)}, u32[]{:S(2)}) collective-permute-start(f32[4,128,256]{2,1,0:T(8,128)} %convolution_add_fusion.8), channel_id=1, source_target_pairs={{0,32},{8,40},{16,48},{24,56},{32,64},{40,72},{48,80},{56,88},{64,... | collective-permute-start | bytes 1572872 | tf_op jit(solution)/shard_map/ppermute | solution.py:24
  132.7 20.0 %collective-permute-start.5 = (f32[4,128,256]{2,1,0:T(8,128)}, f32[4,128,256]{2,1,0:T(8,128)}, u32[]{:S(2)}, u32[]{:S(2)}) collective-permute-start(f32[4,128,256]{2,1,0:T(8,128)} %convolution_add_fusion.8), channel_id=1, source_target_pairs={{0,64},{8,72},{16,80},{24,88},{32,96},{40,104},{48,112},{56,120},{... | collective-permute-start | bytes 1572872 | tf_op jit(solution)/shard_map/ppermute | solution.py:24
  138.0 7.5 %copy-start.1 = (s32[256,10,128]{0,1,2:T(8,128)}, s32[256,10,128]{0,1,2:T(8,128)S(1)}, u32[]{:S(2)}) copy-start(s32[256,10,128]{0,1,2:T(8,128)S(1)} %fusion.31) | copy-start | bytes 3932164
  138.0 26.0 %collective-permute-start.6 = (f32[4,128,256]{2,1,0:T(8,128)}, f32[4,128,256]{2,1,0:T(8,128)}, u32[]{:S(2)}, u32[]{:S(2)}) collective-permute-start(f32[4,128,256]{2,1,0:T(8,128)} %convolution_add_fusion.8), channel_id=1, source_target_pairs={{0,96},{8,104},{16,112},{24,120},{32,128},{40,136},{48,144},{56,15... | collective-permute-start | bytes 1572872 | tf_op jit(solution)/shard_map/ppermute | solution.py:24
  154.3 64.1 %copy-start.2 = (s32[256,10,128]{0,1,2:T(8,128)S(1)}, s32[256,10,128]{0,1,2:T(8,128)}, u32[]{:S(2)}) copy-start(s32[256,10,128]{0,1,2:T(8,128)} %copy-done.1) | copy-start | bytes 3932164
  165.6 0.8 copy-start.3
  167.8 59.1 %collective-permute-start.7 = (f32[4,128,256]{2,1,0:T(8,128)}, f32[4,128,256]{2,1,0:T(8,128)}, u32[]{:S(2)}, u32[]{:S(2)}) collective-permute-start(f32[4,128,256]{2,1,0:T(8,128)} %convolution_add_fusion.4), channel_id=1, source_target_pairs={{0,128},{8,136},{16,144},{24,152},{32,160},{40,168},{48,176},{56,1... | collective-permute-start | bytes 1572872 | tf_op jit(solution)/shard_map/ppermute | solution.py:24
  200.9 27.9 %collective-permute-start.8 = (f32[4,128,256]{2,1,0:T(8,128)}, f32[4,128,256]{2,1,0:T(8,128)}, u32[]{:S(2)}, u32[]{:S(2)}) collective-permute-start(f32[4,128,256]{2,1,0:T(8,128)} %convolution_add_fusion.4), channel_id=1, source_target_pairs={{0,256},{8,264},{16,272},{24,280},{32,288},{40,296},{48,304},{56,3... | collective-permute-start | bytes 1572872 | tf_op jit(solution)/shard_map/ppermute | solution.py:24
  218.5 1.6 copy-start.9
  220.2 84.3 %collective-permute-start.9 = (f32[4,128,256]{2,1,0:T(8,128)}, f32[4,128,256]{2,1,0:T(8,128)}, u32[]{:S(2)}, u32[]{:S(2)}) collective-permute-start(f32[4,128,256]{2,1,0:T(8,128)} %convolution_add_fusion.4), channel_id=1, source_target_pairs={{0,384},{8,392},{16,400},{24,408},{32,416},{40,424},{48,432},{56,4... | collective-permute-start | bytes 1572872 | tf_op jit(solution)/shard_map/ppermute | solution.py:24
  223.3 3.5 copy-start.4
  223.3 3.5 slice-start
  228.5 77.6 %copy-start.6 = (f32[4,128,128]{2,1,0:T(8,128)S(1)}, f32[4,128,128]{2,1,0:T(8,128)}, u32[]{:S(2)}) copy-start(f32[4,128,128]{2,1,0:T(8,128)} %param.26) | copy-start | bytes 786436
  228.6 78.1 %copy-start.7 = (f32[128,4,128]{2,0,1:T(8,128)S(1)}, f32[128,4,128]{2,0,1:T(8,128)}, u32[]{:S(2)}) copy-start(f32[128,4,128]{2,0,1:T(8,128)} %copy.102) | copy-start | bytes 786436
  228.6 78.1 %copy-start.12 = (f32[128]{0:T(128)S(1)}, f32[128]{0:T(128)}, u32[]{:S(2)}) copy-start(f32[128]{0:T(128)} %param.27) | copy-start | bytes 1540
  309.1 44.9 %copy-start.8 = (bf16[128,256]{1,0:T(8,128)(2,1)S(1)}, bf16[128,256]{1,0:T(8,128)(2,1)}, u32[]{:S(2)}) copy-start(bf16[128,256]{1,0:T(8,128)(2,1)} %param.19) | copy-start | bytes 196612
  311.3 196.4 %all-reduce.15.cloned.1.call-start = ((), (), s32[]{:S(2)}) async-start(), calls=%async_computation.4 | async-start | bytes 3145728 | tf_op jit(solution)/shard_map/psum | solution.py:231
  375.9 59.6 %copy-start.5 = (bf16[4,256,512]{2,1,0:T(8,128)(2,1)S(1)}, bf16[4,256,512]{2,1,0:T(8,128)(2,1)}, u32[]{:S(2)}) copy-start(bf16[4,256,512]{2,1,0:T(8,128)(2,1)} %param.34) | copy-start | bytes 3145732
  437.2 72.4 %copy-start.13 = (bf16[4,256,256]{2,1,0:T(8,128)(2,1)S(1)}, bf16[4,256,256]{2,1,0:T(8,128)(2,1)}, u32[]{:S(2)}) copy-start(bf16[4,256,256]{2,1,0:T(8,128)(2,1)} %param.35) | copy-start | bytes 1572868
  510.1 17.3 %copy-start.11 = (f32[128,10]{0,1:T(8,128)S(1)}, f32[128,10]{0,1:T(8,128)}, u32[]{:S(2)}) copy-start(f32[128,10]{0,1:T(8,128)} %param.33) | copy-start | bytes 15364
  511.7 60.1 %all-to-all-start.1 = ((bf16[64,6,4,256]{3,2,1,0:T(4,128)(2,1)}), bf16[64,6,4,256]{3,2,1,0:T(4,128)(2,1)}, u32[]{:S(2)}, u32[]{:S(2)}) async-start(bf16[64,6,4,256]{3,2,1,0:T(4,128)(2,1)} %bitcast.38), calls=%async_computation.2 | async-start | bytes 1572864 | tf_op jit(solution)/shard_map/all_to_all | solution.py:244
Sparse Core Ops, SparseCore 0:
  311.4 42.5 reduce-scatter.1
  437.3 70.3 all-reduce.14

commit v3 on v2

--- a/solution.py
+++ b/solution.py
@@ -87,16 +87,25 @@
     return (state_end, outputs)
 
 
-SCAN_RADIX = 4
-
-
 def compose(later, earlier):
-    joined = jnp.einsum("hij,hjk->hik", later[:, :, :DK], earlier, precision=EXACT_ARITHMETIC)
-    return joined + jnp.concatenate([jnp.zeros_like(later[:, :, :DK]), later[:, :, DK:]], axis=2)
+    joined = jnp.einsum("...ij,...jk->...ik", later[..., :DK], earlier, precision=EXACT_ARITHMETIC)
+    return joined + jnp.concatenate([jnp.zeros_like(later[..., :DK]), later[..., DK:]], axis=-1)
+
+
+def within_group(value, group, offset):
+    count = lax.axis_size("seq")
+    pairs = [
+        (start + place, start + (place + offset) % group)
+        for start in range(0, count, group)
+        for place in range(group)
+    ]
+    return lax.ppermute(value, "seq", pairs)
 
 
 def entering_state(transfer, carried, init_state):
     count, position = (lax.axis_size("seq"), lax.axis_index("seq"))
+    group = transfer.shape[0]
+    place = position % group
     first = position == 0
     folded = (
         jnp.einsum("hij,hjk->hik", transfer, init_state, precision=EXACT_ARITHMETIC) + carried
@@ -108,18 +117,46 @@
         ],
         axis=2,
     )
-    inclusive = own
-    exclusive = None
-    span = 1
-    while span < count:
-        for j in range(1, SCAN_RADIX):
-            if span * j < count:
-                part = passed_along(inclusive, "seq", span * j)
-                exclusive = part if exclusive is None else compose(exclusive, part)
-        span *= SCAN_RADIX
-        if span < count:
-            inclusive = compose(own, exclusive)
-    return jnp.where(first, init_state, exclusive[:, :, DK:])
+    items = [lax.dynamic_index_in_dim(own, place, 0, keepdims=False)]
+    for offset in range(1, group):
+        sent = lax.dynamic_index_in_dim(own, (place + offset) % group, 0, keepdims=False)
+        items.append(within_group(sent, group, offset))
+    stacked = jnp.stack(items)
+    maps = jnp.take(stacked, (place - jnp.arange(group)) % group, axis=0)
+    identity = jnp.concatenate(
+        [jnp.eye(DK, dtype=jnp.float32), jnp.zeros((DK, DV), jnp.float32)], axis=1
+    )
+    prefixes = [identity]
+    for member in range(group):
+        prefixes.append(compose(maps[member], prefixes[-1]) if member else maps[0])
+    total = prefixes.pop()
+    groups = count // group
+    mapping, shift = total[:, :DK], total[:, DK:]
+    step = 1
+    while step < groups:
+        if 2 * step >= groups:
+            shift_in = passed_along(shift, "seq", step * group)
+            shift = jnp.dot(mapping, shift_in, precision=EXACT_ARITHMETIC) + shift
+        else:
+            both_in = passed_along(jnp.concatenate([mapping, shift], axis=1), "seq", step * group)
+            map_in, shift_in = both_in[:, :DK], both_in[:, DK:]
+            shift = jnp.dot(mapping, shift_in, precision=EXACT_ARITHMETIC) + shift
+            mapping = jnp.dot(mapping, map_in, precision=EXACT_ARITHMETIC)
+        step *= 2
+    start_state = passed_along(shift, "seq", group) + (position < group).astype(
+        jnp.float32
+    ) * lax.dynamic_index_in_dim(init_state, place, 0, keepdims=False)
+    prefixes = jnp.stack(prefixes)
+    entering = (
+        jnp.einsum("pij,jk->pik", prefixes[:, :, :DK], start_state, precision=EXACT_ARITHMETIC)
+        + prefixes[:, :, DK:]
+    )
+    heads = [lax.dynamic_index_in_dim(entering, place, 0, keepdims=False)]
+    for offset in range(1, group):
+        sent = lax.dynamic_index_in_dim(entering, (place + offset) % group, 0, keepdims=False)
+        heads.append(within_group(sent, group, offset))
+    stacked = jnp.stack(heads)
+    return jnp.take(stacked, (place - jnp.arange(group)) % group, axis=0)
 
 
 def local(

time: 589 us -> 460 us (0.78)
  waiting for transfers between devices: 246 us -> 165 us
  starting transfers between devices: 123 us -> 75.3 us
  matrix products: 35.5 us -> 24.8 us
    ppermute x10 -> x6, waiting for transfers between devices: 95.8 us -> 3.69 us  [passed_along(): lax.ppermute(value, axis, [(source, source + steps) for source in range(f...]
    ppermute x10 -> x6, starting transfers between devices: 108 us -> 38.4 us  [passed_along(): lax.ppermute(value, axis, [(source, source + steps) for source in range(f...]
    ppermute x0 -> x6, starting transfers between devices: none -> 21.4 us  [within_group(): return lax.ppermute(value, 'seq', pairs)]
    dot_general x10 -> x11, matrix products: 15.7 us -> 3.82 us  [the longest x1 1.2 us: entering_state(): jnp.einsum('pij,jk->pik', prefixes[:, :, :DK], start_state, precision=EXA...]
    reduce_scatter x1, waiting for transfers between devices: 35.2 us -> 43.6 us  [local(): lax.psum_scatter(partial_value.astype(jnp.bfloat16), 'head', scatter_dime...]
  transfers between devices with their start and end apart: 13 -> 15, of which waited for: 10 -> 8; matrix products, arithmetic and copies ran while one was open for 5% -> 5% of each run, Pallas kernels for 0% -> 0%
where the time goes in v3:
time: 460 us; the launch traced here: 459 us
  waiting for transfers between devices  165 us (36%)
  starting transfers between devices  75.3 us (16%)
  blocking collectives  70.8 us (15%)
  other arithmetic  64.1 us (14%)
  local copies, waits for them, and re-layouts  43.9 us (10%)
  matrix products  24.8 us (5%)
  between operations  14.2 us (3%)
    psum x1, waiting for transfers between devices, local(): lax.psum(term_rows.reshape(row_count, -1).astype(jnp.bfloat16), 'head')  70.5 us
    all_to_all x1, blocking collectives, local(): lax.all_to_all(outgoing, 'seq', split_axis=0, concat_axis=0, tiled=True)  59 us
    all_to_all x1, waiting for transfers between devices, local(): lax.all_to_all(results.reshape(seq_size, capacity, experts_here, -1), 'se...  44.2 us
    reduce_scatter x1, waiting for transfers between devices, local(): lax.psum_scatter(partial_value.astype(jnp.bfloat16), 'head', scatter_dime...  43.6 us
    another operation x8, other arithmetic, delta_block(): lax.linalg.triangular_solve(system, target, left_side=True, lower=True, u...  41 us
    ppermute x6, starting transfers between devices, passed_along(): lax.ppermute(value, axis, [(source, source + steps) for source in range(f...  38.4 us
    ppermute x6, starting transfers between devices, within_group(): return lax.ppermute(value, 'seq', pairs)  21.4 us
    all_to_all x1, starting transfers between devices, local(): lax.all_to_all(results.reshape(seq_size, capacity, experts_here, -1), 'se...  15.3 us
  transfers between devices with their start and end apart: 15, of which 8 were waited for; matrix products, arithmetic and copies ran while one was open for 5% of the time, Pallas kernels for 0%

profile of v3, /device:TPU:15, one launch (start us, length us, event | category | flops | bytes accessed | tf_op | source)
XLA Modules:
  0.0 458.7 jit_solution(18248927010430211081)
XLA Ops:
  7.4 3.2 collective-permute-start
  21.1 57.3 %while.12 = (s32[]{:T(128)}, f32[4,128,256]{2,1,0:T(8,128)S(1)}, f32[2,4,64,256]{3,2,1,0:T(8,128)}, f32[2,4,64]{2,0,1:T(2,128)}, f32[2,4,64,128]{3,2,0,1:T(8,128...) while((s32[]{:T(128)}, f32[4,128,256]{2,1,0:T(8,128)S(1)}, ...), condition=%wide.region_4.5_spmd, body=%wide.region_2.4_spmd.sunk | while | flops 453865536 | bytes 5678793 | solution.py:74
  25.4 20.4 %custom-call.13 = f32[4,1,64,64]{2,3,1,0:T(8,128)S(1)} custom-call(f32[4,1,64,64]{3,2,1,0:T(8,128)} %fusion.163), custom_call_target="InvertDiagBlocksLowerTriangular" | custom-call | tf_op jit(solution)/shard_map/while/body/eval_jaxpr/triangular_solve | solution.py:47
  54.1 20.4 %custom-call.13 = f32[4,1,64,64]{2,3,1,0:T(8,128)S(1)} custom-call(f32[4,1,64,64]{3,2,1,0:T(8,128)} %fusion.163), custom_call_target="InvertDiagBlocksLowerTriangular" | custom-call | tf_op jit(solution)/shard_map/while/body/eval_jaxpr/triangular_solve | solution.py:47
  79.9 2.9 collective-permute-start.1
  82.8 2.9 collective-permute-start.2
  85.7 4.0 collective-permute-start.3
  90.2 3.4 collective-permute-done.3
  96.8 3.5 collective-permute-start.4
  102.9 5.1 %collective-permute-start.5 = (f32[128,256]{1,0:T(8,128)S(1)}, f32[128,256]{1,0:T(8,128)S(1)}, u32[]{:S(2)}, u32[]{:S(2)}) collective-permute-start(f32[128,256]{1,0:T(8,128)S(1)} %pad_maximum_fusion.4), channel_id=1, source_target_pairs={{0,64},{8,72},{16,80},{24,88},{32,96},{40,104},{48,112},{56,120},{... | collective-permute-start | bytes 393224 | tf_op jit(solution)/shard_map/ppermute | solution.py:24
  110.7 12.5 %collective-permute-start.6 = (f32[128,256]{1,0:T(8,128)S(1)}, f32[128,256]{1,0:T(8,128)S(1)}, u32[]{:S(2)}, u32[]{:S(2)}) collective-permute-start(f32[128,256]{1,0:T(8,128)S(1)} %pad_maximum_fusion.5), channel_id=1, source_target_pairs={{0,128},{8,136},{16,144},{24,152},{32,160},{40,168},{48,176},{56,1... | collective-permute-start | bytes 393224 | tf_op jit(solution)/shard_map/ppermute | solution.py:24
  123.2 3.2 broadcast_add_fusion
  126.9 12.8 %collective-permute-start.7 = (f32[128,128]{1,0:T(8,128)S(1)}, f32[128,128]{1,0:T(8,128)S(1)}, u32[]{:S(2)}, u32[]{:S(2)}) collective-permute-start(f32[128,128]{1,0:T(8,128)S(1)} %convolution_add_fusion.10), channel_id=1, source_target_pairs={{0,256},{8,264},{16,272},{24,280},{32,288},{40,296},{48,304},{56,3... | collective-permute-start | bytes 196616 | tf_op jit(solution)/shard_map/ppermute | solution.py:24
  145.7 5.7 %collective-permute-start.9 = (f32[128,128]{1,0:T(8,128)}, f32[128,128]{1,0:T(8,128)}, u32[]{:S(2)}, u32[]{:S(2)}) collective-permute-start(f32[128,128]{1,0:T(8,128)} %get-tuple-element.115), channel_id=1, source_target_pairs={{0,8},{8,16},{16,24},{24,0},{32,40},{40,48},{48,56},{56,32},{64,72... | collective-permute-start | bytes 196616 | tf_op jit(solution)/shard_map/ppermute | solution.py:102
  151.4 2.0 collective-permute-start.10
  153.5 3.9 collective-permute-start.11
  158.4 2.4 copy.123
  160.7 1.9 copy.108
  164.3 2.3 gather_fusion.1
  168.3 1.7 multiply_convert_fusion
  171.7 2.2 convolution_convert_fusion
  175.9 5.2 %scatter_custom_fusion = s32[1536]{0:T(1024)S(1)} fusion(s32[1280]{0:T(1024)S(1)} %fusion.99, s32[1280]{0:T(1024)S(1)} %add_select_fusion, s32[]{:T(128)} %constant.219.clone.1), kind=kCustom, calls=%fused_computation.214 | custom fusion | bytes 6148 | tf_op jit(solution)/shard_map/scatter | solution.py:259
  181.4 43.6 %reduce-scatter.2.cloned.1.call-done = bf16[128,256]{1,0:T(8,128)(2,1)} async-done(((bf16[128,2048]{1,0:T(8,128)(2,1)}), bf16[128,256]{1,0:T(8,128)(2,1)}) %reduce-scatter.2.cloned.1.call-update) | async-done | bytes 65552 | tf_op jit(solution)/shard_map/reduce_scatter | solution.py:225
  227.1 11.9 %all-reduce.7 = (f32[128]{0:T(128)S(1)}, f32[128]{0:T(128)S(1)}) all-reduce(f32[128]{0:T(128)S(1)} %get-tuple-element.124, f32[128]{0:T(128)S(1)} %multiply_reduce_fusion.3), channel_id=1, replica_groups=mesh['seq'=64,'head'=8] {'head'}, use_global_device_ids=true, to_apply=%region_10.11 | all-reduce | flops 256 | bytes 2048 | tf_op jit(solution)/shard_map/psum | solution.py:235
  239.8 5.3 %gather_fusion.2 = bf16[1536,256]{1,0:T(8,128)(2,1)} fusion(bf16[129,256]{1,0:T(8,128)(2,1)S(1)} %concatenate.44, s32[2048]{0:T(1024)S(1)} %pad_clamp_fusion.1), kind=kCustom, calls=%fused_computation.2 | custom fusion | bytes 1579008 | tf_op jit(solution)/shard_map/jit(_take)/gather | solution.py:262
  247.6 59.0 %all_to_all.10 = bf16[64,6,4,256]{3,2,1,0:T(4,128)(2,1)S(1)} all-to-all(bf16[64,6,4,256]{3,2,1,0:T(4,128)(2,1)S(1)} %broadcast_select_fusion), channel_id=1, replica_groups=mesh['seq'=64,'head'=8] {'seq'}, dimensions={0} | all-to-all | bytes 1572864 | tf_op jit(solution)/shard_map/all_to_all | solution.py:263
  306.5 1.7 fusion.34
  308.3 70.5 %all-reduce.10.cloned.1.call-done = bf16[384,4,512]{2,0,1:T(8,128)(2,1)} async-done(((bf16[384,4,512]{2,0,1:T(8,128)(2,1)}), bf16[384,4,512]{2,0,1:T(8,128)(2,1)}) %all-reduce.10.cloned.1.call-update) | async-done | bytes 1572880 | tf_op jit(solution)/shard_map/psum | solution.py:268
  378.8 1.8 reshape.369
  382.8 15.3 %all-to-all-start.1 = ((bf16[64,6,4,256]{3,2,1,0:T(4,128)(2,1)}), bf16[64,6,4,256]{3,2,1,0:T(4,128)(2,1)}, u32[]{:S(2)}, u32[]{:S(2)}) async-start(bf16[64,6,4,256]{3,2,1,0:T(4,128)(2,1)} %bitcast.60), calls=%async_computation.2 | async-start | bytes 1572864 | tf_op jit(solution)/shard_map/all_to_all | solution.py:281
  398.6 44.2 %all-to-all-done.1 = bf16[64,6,4,256]{3,2,1,0:T(4,128)(2,1)} async-done(((bf16[64,6,4,256]{3,2,1,0:T(4,128)(2,1)}), bf16[64,6,4,256]{3,2,1,0:T(4,128)(2,1)}, u32[]{:S(2)}, u32[]{:S(2)}) %all-to-all-start.1) | async-done | bytes 786464 | tf_op jit(solution)/shard_map/all_to_all | solution.py:281
  444.4 4.7 %gather_fusion.3 = bf16[1280,256]{1,0:T(8,128)(2,1)} fusion(bf16[1536,256]{1,0:T(8,128)(2,1)S(1)} %reshape.371, s32[2048]{0:T(1024)S(1)} %pad_clamp_fusion), kind=kCustom, calls=%fused_computation.3 | custom fusion | bytes 1315840 | tf_op jit(solution)/shard_map/jit(_take)/gather | solution.py:290
  (174 shorter events, 64.5 us)
Async XLA Ops:
  6.5 165.1 %copy-start = (bf16[512,2048]{1,0:T(8,128)(2,1)S(1)}, bf16[512,2048]{1,0:T(8,128)(2,1)}, u32[]{:S(2)}) copy-start(bf16[512,2048]{1,0:T(8,128)(2,1)} %param.28) | copy-start | bytes 6291460
  6.5 9.3 %copy-start.9 = (bf16[3,1024]{1,0:T(4,128)(2,1)S(1)}, bf16[3,1024]{1,0:T(4,128)(2,1)}, u32[]{:S(2)}) copy-start(bf16[3,1024]{1,0:T(4,128)(2,1)} %param.22) | copy-start | bytes 18436
  6.5 218.4 %reduce-scatter.2.cloned.1.call-start = ((), (), s32[]{:S(2)}) async-start(), calls=%async_computation.3 | async-start | bytes 589824 | tf_op jit(solution)/shard_map/reduce_scatter | solution.py:225
  7.4 8.4 %collective-permute-start = (bf16[3,1024]{1,0:T(4,128)(2,1)S(1)}, bf16[3,1024]{1,0:T(4,128)(2,1)S(1)}, u32[]{:S(2)}, u32[]{:S(2)}) collective-permute-start(bf16[3,1024]{1,0:T(4,128)(2,1)S(1)} %slice.131), channel_id=1, source_target_pairs={{0,8},{8,16},{16,24},{24,32},{32,40},{40,48},{48,56},{56,64},{64,7... | collective-permute-start | bytes 18440 | tf_op jit(solution)/shard_map/ppermute | solution.py:24
  10.7 5.1 %copy-start.2 = (f32[128,128]{1,0:T(8,128)}, f32[128,128]{1,0:T(8,128)S(1)}, u32[]{:S(2)}) copy-start(f32[128,128]{1,0:T(8,128)S(1)} %fusion.82) | copy-start | bytes 196612
  78.4 11.3 %copy-start.7 = (s32[128,10]{0,1:T(8,128)S(1)}, s32[128,10]{0,1:T(8,128)}, u32[]{:S(2)}) copy-start(s32[128,10]{0,1:T(8,128)} %param.32) | copy-start | bytes 15364
  78.4 11.7 %copy-start.12 = (s32[4]{0:T(128)S(1)}, s32[4]{0:T(128)}, u32[]{:S(2)}) copy-start(s32[4]{0:T(128)} %fusion.105) | copy-start | bytes 52
  79.9 10.3 %collective-permute-start.1 = (f32[128,256]{1,0:T(8,128)S(1)}, f32[128,256]{1,0:T(8,128)S(1)}, u32[]{:S(2)}, u32[]{:S(2)}) collective-permute-start(f32[128,256]{1,0:T(8,128)S(1)} %get-tuple-element.107), channel_id=1, source_target_pairs={{0,8},{8,16},{16,24},{24,0},{32,40},{40,48},{48,56},{56,32},{64,72... | collective-permute-start | bytes 393224 | tf_op jit(solution)/shard_map/ppermute | solution.py:102
  82.8 7.4 %collective-permute-start.2 = (f32[128,256]{1,0:T(8,128)S(1)}, f32[128,256]{1,0:T(8,128)S(1)}, u32[]{:S(2)}, u32[]{:S(2)}) collective-permute-start(f32[128,256]{1,0:T(8,128)S(1)} %get-tuple-element.108), channel_id=1, source_target_pairs={{0,16},{8,24},{16,0},{24,8},{32,48},{40,56},{48,32},{56,40},{64,80... | collective-permute-start | bytes 393224 | tf_op jit(solution)/shard_map/ppermute | solution.py:102
  85.7 7.9 %collective-permute-start.3 = (f32[128,256]{1,0:T(8,128)S(1)}, f32[128,256]{1,0:T(8,128)S(1)}, u32[]{:S(2)}, u32[]{:S(2)}) collective-permute-start(f32[128,256]{1,0:T(8,128)S(1)} %get-tuple-element.109), channel_id=1, source_target_pairs={{0,24},{8,0},{16,8},{24,16},{32,56},{40,32},{48,40},{56,48},{64,88... | collective-permute-start | bytes 393224 | tf_op jit(solution)/shard_map/ppermute | solution.py:102
  89.7 6.2 %copy-start.11 = (pred[4]{0:T(512)(128)(4,1)}, pred[4]{0:T(512)(128)(4,1)S(1)}, u32[]{:S(2)}) copy-start(pred[4]{0:T(512)(128)(4,1)S(1)} %compare_and_fusion.2) | copy-start | bytes 16
  90.1 5.8 %copy-start.10 = (s32[1024]{0:T(1024)}, s32[1024]{0:T(1024)S(1)}, u32[]{:S(2)}) copy-start(s32[1024]{0:T(1024)S(1)} %pad_clamp_fusion.2) | copy-start | bytes 12292
  93.6 0.6 copy-start.6
  96.8 5.5 %collective-permute-start.4 = (f32[128,256]{1,0:T(8,128)S(1)}, f32[128,256]{1,0:T(8,128)S(1)}, u32[]{:S(2)}, u32[]{:S(2)}) collective-permute-start(f32[128,256]{1,0:T(8,128)S(1)} %convolution_add_fusion.5), channel_id=1, source_target_pairs={{0,32},{8,40},{16,48},{24,56},{32,64},{40,72},{48,80},{56,88},{64,... | collective-permute-start | bytes 393224 | tf_op jit(solution)/shard_map/ppermute | solution.py:24
  102.9 7.1 %collective-permute-start.5 = (f32[128,256]{1,0:T(8,128)S(1)}, f32[128,256]{1,0:T(8,128)S(1)}, u32[]{:S(2)}, u32[]{:S(2)}) collective-permute-start(f32[128,256]{1,0:T(8,128)S(1)} %pad_maximum_fusion.4), channel_id=1, source_target_pairs={{0,64},{8,72},{16,80},{24,88},{32,96},{40,104},{48,112},{56,120},{... | collective-permute-start | bytes 393224 | tf_op jit(solution)/shard_map/ppermute | solution.py:24
  110.7 15.9 %collective-permute-start.6 = (f32[128,256]{1,0:T(8,128)S(1)}, f32[128,256]{1,0:T(8,128)S(1)}, u32[]{:S(2)}, u32[]{:S(2)}) collective-permute-start(f32[128,256]{1,0:T(8,128)S(1)} %pad_maximum_fusion.5), channel_id=1, source_target_pairs={{0,128},{8,136},{16,144},{24,152},{32,160},{40,168},{48,176},{56,1... | collective-permute-start | bytes 393224 | tf_op jit(solution)/shard_map/ppermute | solution.py:24
  123.2 3.2 copy-start.5
  123.2 3.3 copy-start.3
  126.9 14.1 %collective-permute-start.7 = (f32[128,128]{1,0:T(8,128)S(1)}, f32[128,128]{1,0:T(8,128)S(1)}, u32[]{:S(2)}, u32[]{:S(2)}) collective-permute-start(f32[128,128]{1,0:T(8,128)S(1)} %convolution_add_fusion.10), channel_id=1, source_target_pairs={{0,256},{8,264},{16,272},{24,280},{32,288},{40,296},{48,304},{56,3... | collective-permute-start | bytes 196616 | tf_op jit(solution)/shard_map/ppermute | solution.py:24
  141.2 2.6 collective-permute-start.8
  145.7 16.9 %collective-permute-start.9 = (f32[128,128]{1,0:T(8,128)}, f32[128,128]{1,0:T(8,128)}, u32[]{:S(2)}, u32[]{:S(2)}) collective-permute-start(f32[128,128]{1,0:T(8,128)} %get-tuple-element.115), channel_id=1, source_target_pairs={{0,8},{8,16},{16,24},{24,0},{32,40},{40,48},{48,56},{56,32},{64,72... | collective-permute-start | bytes 196616 | tf_op jit(solution)/shard_map/ppermute | solution.py:102
  151.4 11.2 %collective-permute-start.10 = (f32[128,128]{1,0:T(8,128)}, f32[128,128]{1,0:T(8,128)}, u32[]{:S(2)}, u32[]{:S(2)}) collective-permute-start(f32[128,128]{1,0:T(8,128)} %get-tuple-element.114), channel_id=1, source_target_pairs={{0,16},{8,24},{16,0},{24,8},{32,48},{40,56},{48,32},{56,40},{64,80... | collective-permute-start | bytes 196616 | tf_op jit(solution)/shard_map/ppermute | solution.py:102
  153.5 9.2 %collective-permute-start.11 = (f32[128,128]{1,0:T(8,128)}, f32[128,128]{1,0:T(8,128)}, u32[]{:S(2)}, u32[]{:S(2)}) collective-permute-start(f32[128,128]{1,0:T(8,128)} %get-tuple-element.113), channel_id=1, source_target_pairs={{0,24},{8,0},{16,8},{24,16},{32,56},{40,32},{48,40},{56,48},{64,88... | collective-permute-start | bytes 196616 | tf_op jit(solution)/shard_map/ppermute | solution.py:102
  171.7 53.3 %copy-start.4 = (bf16[128,256]{1,0:T(8,128)(2,1)S(1)}, bf16[128,256]{1,0:T(8,128)(2,1)}, u32[]{:S(2)}) copy-start(bf16[128,256]{1,0:T(8,128)(2,1)} %param.19) | copy-start | bytes 196612
  173.9 204.9 %all-reduce.10.cloned.1.call-start = ((), (), s32[]{:S(2)}) async-start(), calls=%async_computation.4 | async-start | bytes 3145728 | tf_op jit(solution)/shard_map/psum | solution.py:268
  246.9 59.7 %copy-start.1 = (bf16[4,256,512]{2,1,0:T(8,128)(2,1)S(1)}, bf16[4,256,512]{2,1,0:T(8,128)(2,1)}, u32[]{:S(2)}) copy-start(bf16[4,256,512]{2,1,0:T(8,128)(2,1)} %param.34) | copy-start | bytes 3145732
  308.3 72.4 %copy-start.13 = (bf16[4,256,256]{2,1,0:T(8,128)(2,1)S(1)}, bf16[4,256,256]{2,1,0:T(8,128)(2,1)}, u32[]{:S(2)}) copy-start(bf16[4,256,256]{2,1,0:T(8,128)(2,1)} %param.35) | copy-start | bytes 1572868
  381.2 17.3 %copy-start.8 = (f32[128,10]{0,1:T(8,128)S(1)}, f32[128,10]{0,1:T(8,128)}, u32[]{:S(2)}) copy-start(f32[128,10]{0,1:T(8,128)} %param.33) | copy-start | bytes 15364
  382.8 60.1 %all-to-all-start.1 = ((bf16[64,6,4,256]{3,2,1,0:T(4,128)(2,1)}), bf16[64,6,4,256]{3,2,1,0:T(4,128)(2,1)}, u32[]{:S(2)}, u32[]{:S(2)}) async-start(bf16[64,6,4,256]{3,2,1,0:T(4,128)(2,1)} %bitcast.60), calls=%async_computation.2 | async-start | bytes 1572864 | tf_op jit(solution)/shard_map/all_to_all | solution.py:281
Sparse Core Ops, SparseCore 0:
  174.0 50.9 reduce-scatter.1
  308.4 70.3 all-reduce.9

commit v4 on v3

--- a/solution.py
+++ b/solution.py
@@ -11,7 +11,7 @@
 DK = 128
 DV = 128
 KCONV = 4
-STRETCH = 64
+STRETCH = 128
 
 
 EPS = 1e-06
@@ -26,6 +26,23 @@
 
 def unit_rows(vectors):
     return vectors / jnp.sqrt(jnp.sum(vectors * vectors, axis=-1, keepdims=True) + EPS)
+
+
+def unit_lower_inverse(strict_lower):
+    size_all = strict_lower.shape[-1]
+    positions = jnp.arange(size_all)
+    inverse = jnp.broadcast_to(jnp.eye(size_all, dtype=jnp.float32), strict_lower.shape)
+    size = 1
+    while size < size_all:
+        same_pair = positions[:, None] // (2 * size) == positions[None, :] // (2 * size)
+        lower_half = ((positions[:, None] // size) % 2 == 1) & ((positions[None, :] // size) % 2 == 0)
+        coupling = jnp.where(same_pair & lower_half, -strict_lower, 0.0)
+        carried = jnp.einsum("hcd,hde->hce", coupling, inverse, precision=EXACT_ARITHMETIC)
+        inverse = inverse + lax.optimization_barrier(
+            jnp.einsum("hcd,hde->hce", inverse, carried, precision=EXACT_ARITHMETIC)
+        )
+        size *= 2
+    return inverse
 
 
 def delta_block(want_output, carry_state, block):
@@ -44,8 +61,9 @@
     growth = jnp.exp(cum_decay)
     known_part = jnp.einsum("hck,hkw->hcw", key_block, carry_state, precision=EXACT_ARITHMETIC)
     target = beta_block[:, :, None] * (value_block - growth[:, :, None] * known_part)
-    update = lax.linalg.triangular_solve(
-        system, target, left_side=True, lower=True, unit_diagonal=True
+    update = jnp.einsum(
+        "hcd,hdw->hcw", unit_lower_inverse(system - jnp.eye(block_len, dtype=jnp.float32)),
+        target, precision=EXACT_ARITHMETIC,
     )
     tail_decay = jnp.exp(cum_decay[:, -1:] - cum_decay)
     new_state = growth[:, -1][:, None, None] * carry_state + jnp.einsum(

time: 460 us -> 431 us (0.937)
  other arithmetic: 64.1 us -> 24.4 us
  matrix products: 24.8 us -> 34.3 us
  waiting for transfers between devices: 165 us -> 160 us
    another operation x11 -> x3, other arithmetic: 45.9 us -> 3.57 us  [the longest x8 41 us: delta_block(): lax.linalg.triangular_solve(system, target, left_side=True, lower=True, u...]
    dot_general x0 -> x15, matrix products: none -> 7.84 us  [the longest x7 3.46 us: unit_lower_inverse(): jnp.einsum('hcd,hde->hce', inverse, carried, precision=EXACT_ARITHMETIC)]
    unnamed x31 -> x78, local copies, waits for them, and re-layouts: 1.06 us -> 7.28 us
  transfers between devices with their start and end apart: 15 -> 15, of which waited for: 8 -> 8; matrix products, arithmetic and copies ran while one was open for 5% -> 8% of each run, Pallas kernels for 0% -> 0%
where the time goes in v4:
time: 431 us; the launch traced here: 429 us
  waiting for transfers between devices  160 us (37%)
  starting transfers between devices  77.7 us (18%)
  blocking collectives  70.8 us (16%)
  local copies, waits for them, and re-layouts  46.6 us (11%)
  matrix products  34.3 us (8%)
  other arithmetic  24.4 us (6%)
  between operations  14.7 us (3%)
    psum x1, waiting for transfers between devices, local(): lax.psum(term_rows.reshape(row_count, -1).astype(jnp.bfloat16), 'head')  70.5 us
    all_to_all x1, blocking collectives, local(): lax.all_to_all(outgoing, 'seq', split_axis=0, concat_axis=0, tiled=True)  58.9 us
    all_to_all x1, waiting for transfers between devices, local(): lax.all_to_all(results.reshape(seq_size, capacity, experts_here, -1), 'se...  44.2 us
    reduce_scatter x1, waiting for transfers between devices, local(): lax.psum_scatter(partial_value.astype(jnp.bfloat16), 'head', scatter_dime...  42.9 us
    ppermute x6, starting transfers between devices, passed_along(): lax.ppermute(value, axis, [(source, source + steps) for source in range(f...  40.3 us
    ppermute x6, starting transfers between devices, within_group(): return lax.ppermute(value, 'seq', pairs)  22 us
    all_to_all x1, starting transfers between devices, local(): lax.all_to_all(results.reshape(seq_size, capacity, experts_here, -1), 'se...  15.3 us
    psum x1, blocking collectives, local(): lax.psum((jnp.sum(hidden * hidden, axis=1), jnp.sum(steered * steered, ax...  11.9 us
  transfers between devices with their start and end apart: 15, of which 8 were waited for; matrix products, arithmetic and copies ran while one was open for 8% of the time, Pallas kernels for 0%

profile of v4, /device:TPU:15, one launch (start us, length us, event | category | flops | bytes accessed | tf_op | source)
XLA Modules:
  0.0 429.0 jit_solution(10381701862072913703)
XLA Ops:
  7.4 3.2 collective-permute-start
  17.7 3.2 broadcast_add_fusion
  39.8 2.9 collective-permute-start.1
  42.7 2.9 collective-permute-start.2
  45.6 4.1 collective-permute-start.3
  58.4 4.2 collective-permute-start.4
  64.3 2.4 copy.83
  67.3 1.7 copy.63
  73.5 4.6 %collective-permute-start.5 = (f32[128,256]{1,0:T(8,128)S(1)}, f32[128,256]{1,0:T(8,128)S(1)}, u32[]{:S(2)}, u32[]{:S(2)}) collective-permute-start(f32[128,256]{1,0:T(8,128)S(1)} %pad_maximum_fusion.4), channel_id=1, source_target_pairs={{0,64},{8,72},{16,80},{24,88},{32,96},{40,104},{48,112},{56,120},{... | collective-permute-start | bytes 393224 | tf_op jit(solution)/shard_map/ppermute | solution.py:24
  79.8 2.1 convolution_multiply_fusion.3
  82.5 1.7 fusion.89
  88.0 10.7 %collective-permute-start.6 = (f32[128,256]{1,0:T(8,128)S(1)}, f32[128,256]{1,0:T(8,128)S(1)}, u32[]{:S(2)}, u32[]{:S(2)}) collective-permute-start(f32[128,256]{1,0:T(8,128)S(1)} %pad_maximum_fusion.5), channel_id=1, source_target_pairs={{0,128},{8,136},{16,144},{24,152},{32,160},{40,168},{48,176},{56,1... | collective-permute-start | bytes 393224 | tf_op jit(solution)/shard_map/ppermute | solution.py:24
  101.8 12.9 %collective-permute-start.7 = (f32[128,128]{1,0:T(8,128)S(1)}, f32[128,128]{1,0:T(8,128)S(1)}, u32[]{:S(2)}, u32[]{:S(2)}) collective-permute-start(f32[128,128]{1,0:T(8,128)S(1)} %convolution_add_fusion.10), channel_id=1, source_target_pairs={{0,256},{8,264},{16,272},{24,280},{32,288},{40,296},{48,304},{56,3... | collective-permute-start | bytes 196616 | tf_op jit(solution)/shard_map/ppermute | solution.py:24
  116.3 4.6 %collective-permute-start.8 = (f32[128,128]{1,0:T(8,128)S(1)}, f32[128,128]{1,0:T(8,128)S(1)}, u32[]{:S(2)}, u32[]{:S(2)}) collective-permute-start(f32[128,128]{1,0:T(8,128)S(1)} %convolution_add_fusion.9), channel_id=1, source_target_pairs={{0,32},{8,40},{16,48},{24,56},{32,64},{40,72},{48,80},{56,88},{64,... | collective-permute-start | bytes 196616 | tf_op jit(solution)/shard_map/ppermute | solution.py:24
  123.5 6.4 %collective-permute-start.9 = (f32[128,128]{1,0:T(8,128)S(1)}, f32[128,128]{1,0:T(8,128)S(1)}, u32[]{:S(2)}, u32[]{:S(2)}) collective-permute-start(f32[128,128]{1,0:T(8,128)S(1)} %get-tuple-element.46), channel_id=1, source_target_pairs={{0,8},{8,16},{16,24},{24,0},{32,40},{40,48},{48,56},{56,32},{64,72... | collective-permute-start | bytes 196616 | tf_op jit(solution)/shard_map/ppermute | solution.py:120
  129.9 1.9 collective-permute-start.10
  131.8 3.7 collective-permute-start.11
  137.9 2.3 gather_fusion.1
  140.3 1.7 multiply_reduce_fusion.1
  143.8 2.2 convolution_convert_fusion
  146.8 5.2 %scatter_custom_fusion = s32[1536]{0:T(1024)S(1)} fusion(s32[1280]{0:T(1024)S(1)} %fusion.117, s32[1280]{0:T(1024)S(1)} %add_select_fusion, s32[]{:T(128)} %constant.515.clone.1), kind=kCustom, calls=%fused_computation.231 | custom fusion | bytes 6148 | tf_op jit(solution)/shard_map/scatter | solution.py:277
  152.3 42.9 %reduce-scatter.2.cloned.1.call-done = bf16[128,256]{1,0:T(8,128)(2,1)} async-done(((bf16[128,2048]{1,0:T(8,128)(2,1)}), bf16[128,256]{1,0:T(8,128)(2,1)}) %reduce-scatter.2.cloned.1.call-update) | async-done | bytes 65552 | tf_op jit(solution)/shard_map/reduce_scatter | solution.py:243
  197.4 11.9 %all-reduce.7 = (f32[128]{0:T(128)S(1)}, f32[128]{0:T(128)S(1)}) all-reduce(f32[128]{0:T(128)S(1)} %get-tuple-element.57, f32[128]{0:T(128)S(1)} %multiply_reduce_fusion.3), channel_id=1, replica_groups=mesh['seq'=64,'head'=8] {'head'}, use_global_device_ids=true, to_apply=%region_8.9 | all-reduce | flops 256 | bytes 2048 | tf_op jit(solution)/shard_map/psum | solution.py:253
  210.1 5.4 %gather_fusion.2 = bf16[1536,256]{1,0:T(8,128)(2,1)} fusion(bf16[129,256]{1,0:T(8,128)(2,1)S(1)} %concatenate.44, s32[2048]{0:T(1024)S(1)} %pad_clamp_fusion.1), kind=kCustom, calls=%fused_computation.2 | custom fusion | bytes 1579008 | tf_op jit(solution)/shard_map/jit(_take)/gather | solution.py:280
  215.4 1.7 gather.23
  217.8 58.9 %all_to_all.10 = bf16[64,6,4,256]{3,2,1,0:T(4,128)(2,1)S(1)} all-to-all(bf16[64,6,4,256]{3,2,1,0:T(4,128)(2,1)S(1)} %broadcast_select_fusion), channel_id=1, replica_groups=mesh['seq'=64,'head'=8] {'seq'}, dimensions={0} | all-to-all | bytes 1572864 | tf_op jit(solution)/shard_map/all_to_all | solution.py:281
  276.7 1.7 fusion.3
  278.5 70.5 %all-reduce.10.cloned.1.call-done = bf16[384,4,512]{2,0,1:T(8,128)(2,1)} async-done(((bf16[384,4,512]{2,0,1:T(8,128)(2,1)}), bf16[384,4,512]{2,0,1:T(8,128)(2,1)}) %all-reduce.10.cloned.1.call-update) | async-done | bytes 1572880 | tf_op jit(solution)/shard_map/psum | solution.py:286
  349.0 1.8 reshape.1113
  353.0 15.3 %all-to-all-start.1 = ((bf16[64,6,4,256]{3,2,1,0:T(4,128)(2,1)}), bf16[64,6,4,256]{3,2,1,0:T(4,128)(2,1)}, u32[]{:S(2)}, u32[]{:S(2)}) async-start(bf16[64,6,4,256]{3,2,1,0:T(4,128)(2,1)} %bitcast.44), calls=%async_computation.2 | async-start | bytes 1572864 | tf_op jit(solution)/shard_map/all_to_all | solution.py:299
  368.9 44.2 %all-to-all-done.1 = bf16[64,6,4,256]{3,2,1,0:T(4,128)(2,1)} async-done(((bf16[64,6,4,256]{3,2,1,0:T(4,128)(2,1)}), bf16[64,6,4,256]{3,2,1,0:T(4,128)(2,1)}, u32[]{:S(2)}, u32[]{:S(2)}) %all-to-all-start.1) | async-done | bytes 786464 | tf_op jit(solution)/shard_map/all_to_all | solution.py:299
  414.6 4.7 %gather_fusion.3 = bf16[1280,256]{1,0:T(8,128)(2,1)} fusion(bf16[1536,256]{1,0:T(8,128)(2,1)S(1)} %reshape.1115, s32[2048]{0:T(1024)S(1)} %pad_clamp_fusion), kind=kCustom, calls=%fused_computation.3 | custom fusion | bytes 1315840 | tf_op jit(solution)/shard_map/jit(_take)/gather | solution.py:308
  (228 shorter events, 70.5 us)
Async XLA Ops:
  6.5 137.3 %copy-start = (bf16[512,2048]{1,0:T(8,128)(2,1)S(1)}, bf16[512,2048]{1,0:T(8,128)(2,1)}, u32[]{:S(2)}) copy-start(bf16[512,2048]{1,0:T(8,128)(2,1)} %param.26) | copy-start | bytes 6291460
  6.5 188.7 %reduce-scatter.2.cloned.1.call-start = ((), (), s32[]{:S(2)}) async-start(), calls=%async_computation.3 | async-start | bytes 589824 | tf_op jit(solution)/shard_map/reduce_scatter | solution.py:243
  7.4 17.9 %collective-permute-start = (bf16[3,1024]{1,0:T(4,128)(2,1)S(1)}, bf16[3,1024]{1,0:T(4,128)(2,1)S(1)}, u32[]{:S(2)}, u32[]{:S(2)}) collective-permute-start(bf16[3,1024]{1,0:T(4,128)(2,1)S(1)} %slice.129), channel_id=1, source_target_pairs={{0,8},{8,16},{16,24},{24,32},{32,40},{40,48},{48,56},{56,64},{64,7... | collective-permute-start | bytes 18440 | tf_op jit(solution)/shard_map/ppermute | solution.py:24
  12.7 14.0 %copy-start.28 = (f32[4,128]{1,0:T(4,128)}, f32[4,128]{1,0:T(4,128)S(1)}, u32[]{:S(2)}) copy-start(f32[4,128]{1,0:T(4,128)S(1)} %reduce_window_sum.27) | copy-start | bytes 6148
  14.2 12.5 %copy-start.33 = (f32[4,128]{1,0:T(4,128)}, f32[4,128]{1,0:T(4,128)S(1)}, u32[]{:S(2)}) copy-start(f32[4,128]{1,0:T(4,128)S(1)} %get-tuple-element.81) | copy-start | bytes 6148
  15.7 47.0 %copy-start.12 = (s32[128,10]{1,0:T(8,128)}, s32[128,10]{1,0:T(8,128)S(1)}, u32[]{:S(2)}) copy-start(s32[128,10]{1,0:T(8,128)S(1)} %copy.80) | copy-start | bytes 15364
  39.8 12.9 %collective-permute-start.1 = (f32[128,256]{1,0:T(8,128)S(1)}, f32[128,256]{1,0:T(8,128)S(1)}, u32[]{:S(2)}, u32[]{:S(2)}) collective-permute-start(f32[128,256]{1,0:T(8,128)S(1)} %get-tuple-element.38), channel_id=1, source_target_pairs={{0,8},{8,16},{16,24},{24,0},{32,40},{40,48},{48,56},{56,32},{64,72... | collective-permute-start | bytes 393224 | tf_op jit(solution)/shard_map/ppermute | solution.py:120
  42.7 9.9 %collective-permute-start.2 = (f32[128,256]{1,0:T(8,128)S(1)}, f32[128,256]{1,0:T(8,128)S(1)}, u32[]{:S(2)}, u32[]{:S(2)}) collective-permute-start(f32[128,256]{1,0:T(8,128)S(1)} %get-tuple-element.39), channel_id=1, source_target_pairs={{0,16},{8,24},{16,0},{24,8},{32,48},{40,56},{48,32},{56,40},{64,80... | collective-permute-start | bytes 393224 | tf_op jit(solution)/shard_map/ppermute | solution.py:120
  45.6 7.8 %collective-permute-start.3 = (f32[128,256]{1,0:T(8,128)S(1)}, f32[128,256]{1,0:T(8,128)S(1)}, u32[]{:S(2)}, u32[]{:S(2)}) collective-permute-start(f32[128,256]{1,0:T(8,128)S(1)} %get-tuple-element.40), channel_id=1, source_target_pairs={{0,24},{8,0},{16,8},{24,16},{32,56},{40,32},{48,40},{56,48},{64,88... | collective-permute-start | bytes 393224 | tf_op jit(solution)/shard_map/ppermute | solution.py:120
  58.4 10.6 %collective-permute-start.4 = (f32[128,256]{1,0:T(8,128)}, f32[128,256]{1,0:T(8,128)}, u32[]{:S(2)}, u32[]{:S(2)}) collective-permute-start(f32[128,256]{1,0:T(8,128)} %convolution_add_fusion.5), channel_id=1, source_target_pairs={{0,32},{8,40},{16,48},{24,56},{32,64},{40,72},{48,80},{56,88},{64,... | collective-permute-start | bytes 393224 | tf_op jit(solution)/shard_map/ppermute | solution.py:24
  71.5 49.4 %copy-start.8 = (f32[128,256]{1,0:T(8,128)S(1)}, f32[128,256]{1,0:T(8,128)}, u32[]{:S(2)}) copy-start(f32[128,256]{1,0:T(8,128)} %copy-done.7) | copy-start | bytes 393220
  73.5 8.3 %collective-permute-start.5 = (f32[128,256]{1,0:T(8,128)S(1)}, f32[128,256]{1,0:T(8,128)S(1)}, u32[]{:S(2)}, u32[]{:S(2)}) collective-permute-start(f32[128,256]{1,0:T(8,128)S(1)} %pad_maximum_fusion.4), channel_id=1, source_target_pairs={{0,64},{8,72},{16,80},{24,88},{32,96},{40,104},{48,112},{56,120},{... | collective-permute-start | bytes 393224 | tf_op jit(solution)/shard_map/ppermute | solution.py:24
  85.8 35.1 %copy-start.10 = (f32[128,256]{1,0:T(8,128)S(1)}, f32[128,256]{1,0:T(8,128)}, u32[]{:S(2)}) copy-start(f32[128,256]{1,0:T(8,128)} %copy-done.9) | copy-start | bytes 393220
  85.8 35.1 %copy-start.17 = (f32[1,128,256]{2,1,0:T(8,128)S(1)}, f32[1,128,256]{2,1,0:T(8,128)}, u32[]{:S(2)}) copy-start(f32[1,128,256]{2,1,0:T(8,128)} %pad_bitcast_fusion) | copy-start | bytes 393220
  85.8 35.1 %copy-start.18 = (f32[1,128,256]{2,1,0:T(8,128)S(1)}, f32[1,128,256]{2,1,0:T(8,128)}, u32[]{:S(2)}) copy-start(f32[1,128,256]{2,1,0:T(8,128)} %get-tuple-element.36) | copy-start | bytes 393220
  87.1 48.4 %copy-start.3 = (f32[4,128,256]{2,1,0:T(8,128)S(1)}, f32[4,128,256]{2,1,0:T(8,128)}, u32[]{:S(2)}) copy-start(f32[4,128,256]{2,1,0:T(8,128)} %copy-done.2) | copy-start | bytes 1572868
  87.1 48.4 %copy-start.11 = (f32[4,128,128]{2,1,0:T(8,128)S(1)}, f32[4,128,128]{2,1,0:T(8,128)}, u32[]{:S(2)}) copy-start(f32[4,128,128]{2,1,0:T(8,128)} %convolution_multiply_fusion.3) | copy-start | bytes 786436
  88.0 12.6 %collective-permute-start.6 = (f32[128,256]{1,0:T(8,128)S(1)}, f32[128,256]{1,0:T(8,128)S(1)}, u32[]{:S(2)}, u32[]{:S(2)}) collective-permute-start(f32[128,256]{1,0:T(8,128)S(1)} %pad_maximum_fusion.5), channel_id=1, source_target_pairs={{0,128},{8,136},{16,144},{24,152},{32,160},{40,168},{48,176},{56,1... | collective-permute-start | bytes 393224 | tf_op jit(solution)/shard_map/ppermute | solution.py:24
  101.8 14.3 %collective-permute-start.7 = (f32[128,128]{1,0:T(8,128)S(1)}, f32[128,128]{1,0:T(8,128)S(1)}, u32[]{:S(2)}, u32[]{:S(2)}) collective-permute-start(f32[128,128]{1,0:T(8,128)S(1)} %convolution_add_fusion.10), channel_id=1, source_target_pairs={{0,256},{8,264},{16,272},{24,280},{32,288},{40,296},{48,304},{56,3... | collective-permute-start | bytes 196616 | tf_op jit(solution)/shard_map/ppermute | solution.py:24
  116.3 5.9 %collective-permute-start.8 = (f32[128,128]{1,0:T(8,128)S(1)}, f32[128,128]{1,0:T(8,128)S(1)}, u32[]{:S(2)}, u32[]{:S(2)}) collective-permute-start(f32[128,128]{1,0:T(8,128)S(1)} %convolution_add_fusion.9), channel_id=1, source_target_pairs={{0,32},{8,40},{16,48},{24,56},{32,64},{40,72},{48,80},{56,88},{64,... | collective-permute-start | bytes 196616 | tf_op jit(solution)/shard_map/ppermute | solution.py:24
  121.0 19.3 %copy-start.35 = (pred[4]{0:T(512)(128)(4,1)S(1)}, pred[4]{0:T(512)(128)(4,1)}, u32[]{:S(2)}) copy-start(pred[4]{0:T(512)(128)(4,1)} %compare_and_fusion.2) | copy-start | bytes 16
  123.4 18.5 %copy-start.36 = (f32[128]{0:T(128)S(1)}, f32[128]{0:T(128)}, u32[]{:S(2)}) copy-start(f32[128]{0:T(128)} %param.25) | copy-start | bytes 1540
  123.5 13.5 %collective-permute-start.9 = (f32[128,128]{1,0:T(8,128)S(1)}, f32[128,128]{1,0:T(8,128)S(1)}, u32[]{:S(2)}, u32[]{:S(2)}) collective-permute-start(f32[128,128]{1,0:T(8,128)S(1)} %get-tuple-element.46), channel_id=1, source_target_pairs={{0,8},{8,16},{16,24},{24,0},{32,40},{40,48},{48,56},{56,32},{64,72... | collective-permute-start | bytes 196616 | tf_op jit(solution)/shard_map/ppermute | solution.py:120
  129.9 7.1 %collective-permute-start.10 = (f32[128,128]{1,0:T(8,128)S(1)}, f32[128,128]{1,0:T(8,128)S(1)}, u32[]{:S(2)}, u32[]{:S(2)}) collective-permute-start(f32[128,128]{1,0:T(8,128)S(1)} %get-tuple-element.45), channel_id=1, source_target_pairs={{0,16},{8,24},{16,0},{24,8},{32,48},{40,56},{48,32},{56,40},{64,80... | collective-permute-start | bytes 196616 | tf_op jit(solution)/shard_map/ppermute | solution.py:120
  131.8 5.4 %collective-permute-start.11 = (f32[128,128]{1,0:T(8,128)S(1)}, f32[128,128]{1,0:T(8,128)S(1)}, u32[]{:S(2)}, u32[]{:S(2)}) collective-permute-start(f32[128,128]{1,0:T(8,128)S(1)} %get-tuple-element.44), channel_id=1, source_target_pairs={{0,24},{8,0},{16,8},{24,16},{32,56},{40,32},{48,40},{56,48},{64,88... | collective-permute-start | bytes 196616 | tf_op jit(solution)/shard_map/ppermute | solution.py:120
  143.8 51.4 %copy-start.21 = (bf16[128,256]{1,0:T(8,128)(2,1)S(1)}, bf16[128,256]{1,0:T(8,128)(2,1)}, u32[]{:S(2)}) copy-start(bf16[128,256]{1,0:T(8,128)(2,1)} %param.17) | copy-start | bytes 196612
  146.1 202.9 %all-reduce.10.cloned.1.call-start = ((), (), s32[]{:S(2)}) async-start(), calls=%async_computation.4 | async-start | bytes 3145728 | tf_op jit(solution)/shard_map/psum | solution.py:286
  217.1 59.6 %copy-start.15 = (bf16[4,256,512]{2,1,0:T(8,128)(2,1)S(1)}, bf16[4,256,512]{2,1,0:T(8,128)(2,1)}, u32[]{:S(2)}) copy-start(bf16[4,256,512]{2,1,0:T(8,128)(2,1)} %param.32) | copy-start | bytes 3145732
  278.5 72.4 %copy-start.37 = (bf16[4,256,256]{2,1,0:T(8,128)(2,1)S(1)}, bf16[4,256,256]{2,1,0:T(8,128)(2,1)}, u32[]{:S(2)}) copy-start(bf16[4,256,256]{2,1,0:T(8,128)(2,1)} %param.33) | copy-start | bytes 1572868
  351.5 17.1 %copy-start.30 = (s32[128,10]{0,1:T(8,128)S(1)}, s32[128,10]{0,1:T(8,128)}, u32[]{:S(2)}) copy-start(s32[128,10]{0,1:T(8,128)} %param.30) | copy-start | bytes 15364
  351.5 17.3 %copy-start.31 = (f32[128,10]{0,1:T(8,128)S(1)}, f32[128,10]{0,1:T(8,128)}, u32[]{:S(2)}) copy-start(f32[128,10]{0,1:T(8,128)} %param.31) | copy-start | bytes 15364
  353.0 60.1 %all-to-all-start.1 = ((bf16[64,6,4,256]{3,2,1,0:T(4,128)(2,1)}), bf16[64,6,4,256]{3,2,1,0:T(4,128)(2,1)}, u32[]{:S(2)}, u32[]{:S(2)}) async-start(bf16[64,6,4,256]{3,2,1,0:T(4,128)(2,1)} %bitcast.44), calls=%async_computation.2 | async-start | bytes 1572864 | tf_op jit(solution)/shard_map/all_to_all | solution.py:299
  (21 other events, 55.5 us)
Sparse Core Ops, SparseCore 0:
  146.2 48.9 reduce-scatter.1
  278.6 70.3 all-reduce.9

commit v5 on v4

--- a/solution.py
+++ b/solution.py
@@ -12,6 +12,7 @@
 DV = 128
 KCONV = 4
 STRETCH = 128
+LINK = jnp.bfloat16
 
 
 EPS = 1e-06
@@ -138,7 +139,7 @@
     items = [lax.dynamic_index_in_dim(own, place, 0, keepdims=False)]
     for offset in range(1, group):
         sent = lax.dynamic_index_in_dim(own, (place + offset) % group, 0, keepdims=False)
-        items.append(within_group(sent, group, offset))
+        items.append(within_group(sent.astype(LINK), group, offset).astype(jnp.float32))
     stacked = jnp.stack(items)
     maps = jnp.take(stacked, (place - jnp.arange(group)) % group, axis=0)
     identity = jnp.concatenate(
@@ -153,10 +154,11 @@
     step = 1
     while step < groups:
         if 2 * step >= groups:
-            shift_in = passed_along(shift, "seq", step * group)
+            shift_in = passed_along(shift.astype(LINK), "seq", step * group).astype(jnp.float32)
             shift = jnp.dot(mapping, shift_in, precision=EXACT_ARITHMETIC) + shift
         else:
-            both_in = passed_along(jnp.concatenate([mapping, shift], axis=1), "seq", step * group)
+            both = jnp.concatenate([mapping, shift], axis=1).astype(LINK)
+            both_in = passed_along(both, "seq", step * group).astype(jnp.float32)
             map_in, shift_in = both_in[:, :DK], both_in[:, DK:]
             shift = jnp.dot(mapping, shift_in, precision=EXACT_ARITHMETIC) + shift
             mapping = jnp.dot(mapping, map_in, precision=EXACT_ARITHMETIC)

time: 431 us -> 441 us (1.023)
  starting transfers between devices: 77.7 us -> 70.8 us
  local copies, waits for them, and re-layouts: 46.6 us -> 53.3 us
  other arithmetic: 24.4 us -> 29.7 us
    ppermute x6, starting transfers between devices: 40.3 us -> 35 us  [passed_along(): lax.ppermute(value, axis, [(source, source + steps) for source in range(f...]
  transfers between devices with their start and end apart: 15 -> 15, of which waited for: 8 -> 6; matrix products, arithmetic and copies ran while one was open for 8% -> 8% of each run, Pallas kernels for 0% -> 0%
where the time goes in v5:
time: 441 us; the launch traced here: 439 us
  waiting for transfers between devices  164 us (37%)
  starting transfers between devices  70.8 us (16%)
  blocking collectives  70.8 us (16%)
  local copies, waits for them, and re-layouts  53.3 us (12%)
  matrix products  36 us (8%)
  other arithmetic  29.7 us (7%)
  between operations  14.6 us (3%)
    psum x1, waiting for transfers between devices, local(): lax.psum(term_rows.reshape(row_count, -1).astype(jnp.bfloat16), 'head')  70.5 us
    all_to_all x1, blocking collectives, local(): lax.all_to_all(outgoing, 'seq', split_axis=0, concat_axis=0, tiled=True)  58.9 us
    reduce_scatter x1, waiting for transfers between devices, local(): lax.psum_scatter(partial_value.astype(jnp.bfloat16), 'head', scatter_dime...  45.4 us
    all_to_all x1, waiting for transfers between devices, local(): lax.all_to_all(results.reshape(seq_size, capacity, experts_here, -1), 'se...  44.2 us
    ppermute x6, starting transfers between devices, passed_along(): lax.ppermute(value, axis, [(source, source + steps) for source in range(f...  35 us
    ppermute x6, starting transfers between devices, within_group(): return lax.ppermute(value, 'seq', pairs)  20.4 us
    all_to_all x1, starting transfers between devices, local(): lax.all_to_all(results.reshape(seq_size, capacity, experts_here, -1), 'se...  15.3 us
    psum x1, blocking collectives, local(): lax.psum((jnp.sum(hidden * hidden, axis=1), jnp.sum(steered * steered, ax...  11.9 us
  transfers between devices with their start and end apart: 15, of which 6 were waited for; matrix products, arithmetic and copies ran while one was open for 8% of the time, Pallas kernels for 0%

profile of v5, /device:TPU:15, one launch (start us, length us, event | category | flops | bytes accessed | tf_op | source)
XLA Modules:
  0.0 439.4 jit_solution(10762429827011590791)
XLA Ops:
  8.0 3.2 collective-permute-start
  21.2 3.2 broadcast_add_fusion
  29.9 2.4 copy.83
  33.0 2.9 divide_multiply_fusion
  36.0 2.0 copy.62
  50.8 1.8 copy.67
  52.7 1.8 fusion.7
  57.3 2.7 collective-permute-start.3
  60.0 3.3 collective-permute-start.2
  63.3 4.0 collective-permute-start.1
  69.4 2.5 gather_fusion
  75.3 4.1 collective-permute-start.4
  87.5 5.5 %collective-permute-start.5 = (bf16[128,256]{1,0:T(8,128)(2,1)S(1)}, bf16[128,256]{1,0:T(8,128)(2,1)S(1)}, u32[]{:S(2)}, u32[]{:S(2)}) collective-permute-start(bf16[128,256]{1,0:T(8,128)(2,1)S(1)} %pad_maximum_fusion.4), channel_id=1, source_target_pairs={{0,64},{8,72},{16,80},{24,88},{32,96},{40,104},{48,112},{56,120},{... | collective-permute-start | bytes 196616 | tf_op jit(solution)/shard_map/ppermute | solution.py:25
  94.6 2.1 convolution_multiply_fusion.3
  102.6 8.8 %collective-permute-start.6 = (bf16[128,256]{1,0:T(8,128)(2,1)S(1)}, bf16[128,256]{1,0:T(8,128)(2,1)S(1)}, u32[]{:S(2)}, u32[]{:S(2)}) collective-permute-start(bf16[128,256]{1,0:T(8,128)(2,1)S(1)} %pad_maximum_fusion.5), channel_id=1, source_target_pairs={{0,128},{8,136},{16,144},{24,152},{32,160},{40,168},{48,176},{56,1... | collective-permute-start | bytes 196616 | tf_op jit(solution)/shard_map/ppermute | solution.py:25
  114.1 12.1 %collective-permute-start.7 = (bf16[128,128]{1,0:T(8,128)(2,1)S(1)}, bf16[128,128]{1,0:T(8,128)(2,1)S(1)}, u32[]{:S(2)}, u32[]{:S(2)}) collective-permute-start(bf16[128,128]{1,0:T(8,128)(2,1)S(1)} %get-tuple-element.60), channel_id=1, source_target_pairs={{0,256},{8,264},{16,272},{24,280},{32,288},{40,296},{48,304},{56,3... | collective-permute-start | bytes 98312 | tf_op jit(solution)/shard_map/ppermute | solution.py:25
  131.4 3.9 collective-permute-start.9
  135.3 4.6 %collective-permute-start.10 = (f32[128,128]{1,0:T(8,128)S(1)}, f32[128,128]{1,0:T(8,128)S(1)}, u32[]{:S(2)}, u32[]{:S(2)}) collective-permute-start(f32[128,128]{1,0:T(8,128)S(1)} %get-tuple-element.44), channel_id=1, source_target_pairs={{0,16},{8,24},{16,0},{24,8},{32,48},{40,56},{48,32},{56,40},{64,80... | collective-permute-start | bytes 196616 | tf_op jit(solution)/shard_map/ppermute | solution.py:121
  139.9 1.9 collective-permute-start.11
  143.2 2.0 collective-permute-done.11
  145.9 2.4 gather_fusion.1
  151.8 2.2 convolution_convert_fusion
  154.8 5.2 %scatter_custom_fusion = s32[1536]{0:T(1024)S(1)} fusion(s32[1280]{0:T(1024)S(1)} %fusion.120, s32[1280]{0:T(1024)S(1)} %add_select_fusion, s32[]{:T(128)} %constant.515.clone.1), kind=kCustom, calls=%fused_computation.237 | custom fusion | bytes 6148 | tf_op jit(solution)/shard_map/scatter | solution.py:279
  160.3 45.4 %reduce-scatter.2.cloned.1.call-done = bf16[128,256]{1,0:T(8,128)(2,1)} async-done(((bf16[128,2048]{1,0:T(8,128)(2,1)}), bf16[128,256]{1,0:T(8,128)(2,1)}) %reduce-scatter.2.cloned.1.call-update) | async-done | bytes 65552 | tf_op jit(solution)/shard_map/reduce_scatter | solution.py:245
  207.8 11.9 %all-reduce.7 = (f32[128]{0:T(128)S(1)}, f32[128]{0:T(128)S(1)}) all-reduce(f32[128]{0:T(128)S(1)} %get-tuple-element.64, f32[128]{0:T(128)S(1)} %multiply_reduce_fusion.3), channel_id=1, replica_groups=mesh['seq'=64,'head'=8] {'head'}, use_global_device_ids=true, to_apply=%region_8.9 | all-reduce | flops 256 | bytes 2048 | tf_op jit(solution)/shard_map/psum | solution.py:255
  220.5 5.4 %gather_fusion.2 = bf16[1536,256]{1,0:T(8,128)(2,1)} fusion(bf16[129,256]{1,0:T(8,128)(2,1)S(1)} %concatenate.46, s32[2048]{0:T(1024)S(1)} %pad_clamp_fusion.1), kind=kCustom, calls=%fused_computation.2 | custom fusion | bytes 1579008 | tf_op jit(solution)/shard_map/jit(_take)/gather | solution.py:282
  228.2 58.9 %all_to_all.10 = bf16[64,6,4,256]{3,2,1,0:T(4,128)(2,1)S(1)} all-to-all(bf16[64,6,4,256]{3,2,1,0:T(4,128)(2,1)S(1)} %broadcast_select_fusion), channel_id=1, replica_groups=mesh['seq'=64,'head'=8] {'seq'}, dimensions={0} | all-to-all | bytes 1572864 | tf_op jit(solution)/shard_map/all_to_all | solution.py:283
  288.9 70.5 %all-reduce.10.cloned.1.call-done = bf16[384,4,512]{2,0,1:T(8,128)(2,1)} async-done(((bf16[384,4,512]{2,0,1:T(8,128)(2,1)}), bf16[384,4,512]{2,0,1:T(8,128)(2,1)}) %all-reduce.10.cloned.1.call-update) | async-done | bytes 1572880 | tf_op jit(solution)/shard_map/psum | solution.py:288
  359.4 1.8 reshape.1116
  363.4 15.3 %all-to-all-start.1 = ((bf16[64,6,4,256]{3,2,1,0:T(4,128)(2,1)}), bf16[64,6,4,256]{3,2,1,0:T(4,128)(2,1)}, u32[]{:S(2)}, u32[]{:S(2)}) async-start(bf16[64,6,4,256]{3,2,1,0:T(4,128)(2,1)} %bitcast.44), calls=%async_computation.2 | async-start | bytes 1572864 | tf_op jit(solution)/shard_map/all_to_all | solution.py:301
  379.3 44.2 %all-to-all-done.1 = bf16[64,6,4,256]{3,2,1,0:T(4,128)(2,1)} async-done(((bf16[64,6,4,256]{3,2,1,0:T(4,128)(2,1)}), bf16[64,6,4,256]{3,2,1,0:T(4,128)(2,1)}, u32[]{:S(2)}, u32[]{:S(2)}) %all-to-all-start.1) | async-done | bytes 786464 | tf_op jit(solution)/shard_map/all_to_all | solution.py:301
  425.1 4.7 %gather_fusion.3 = bf16[1280,256]{1,0:T(8,128)(2,1)} fusion(bf16[1536,256]{1,0:T(8,128)(2,1)S(1)} %reshape.1118, s32[2048]{0:T(1024)S(1)} %pad_clamp_fusion), kind=kCustom, calls=%fused_computation.3 | custom fusion | bytes 1315840 | tf_op jit(solution)/shard_map/jit(_take)/gather | solution.py:310
  (234 shorter events, 82.1 us)
Async XLA Ops:
  6.5 145.3 %copy-start = (bf16[512,2048]{1,0:T(8,128)(2,1)S(1)}, bf16[512,2048]{1,0:T(8,128)(2,1)}, u32[]{:S(2)}) copy-start(bf16[512,2048]{1,0:T(8,128)(2,1)} %param.26) | copy-start | bytes 6291460
  6.5 199.1 %reduce-scatter.2.cloned.1.call-start = ((), (), s32[]{:S(2)}) async-start(), calls=%async_computation.3 | async-start | bytes 589824 | tf_op jit(solution)/shard_map/reduce_scatter | solution.py:245
  8.0 24.3 %collective-permute-start = (bf16[3,1024]{1,0:T(4,128)(2,1)}, bf16[3,1024]{1,0:T(4,128)(2,1)}, u32[]{:S(2)}, u32[]{:S(2)}) collective-permute-start(bf16[3,1024]{1,0:T(4,128)(2,1)} %slice.129), channel_id=1, source_target_pairs={{0,8},{8,16},{16,24},{24,32},{32,40},{40,48},{48,56},{56,64},{64,7... | collective-permute-start | bytes 18440 | tf_op jit(solution)/shard_map/ppermute | solution.py:25
  19.2 9.1 %copy-start.14 = (s32[128,10]{1,0:T(8,128)}, s32[128,10]{1,0:T(8,128)S(1)}, u32[]{:S(2)}) copy-start(s32[128,10]{1,0:T(8,128)S(1)} %copy.80) | copy-start | bytes 15364
  56.2 11.2 %copy-start.2 = (f32[4,128,256]{2,1,0:T(8,128)}, f32[4,128,256]{2,1,0:T(8,128)S(1)}, u32[]{:S(2)}) copy-start(f32[4,128,256]{2,1,0:T(8,128)S(1)} %fusion.35) | copy-start | bytes 1572868
  57.3 14.6 %copy-start.35 = (pred[4]{0:T(512)(128)(4,1)S(1)}, pred[4]{0:T(512)(128)(4,1)}, u32[]{:S(2)}) copy-start(pred[4]{0:T(512)(128)(4,1)} %compare_and_fusion.2) | copy-start | bytes 16
  57.3 10.1 %collective-permute-start.3 = (bf16[128,256]{1,0:T(8,128)(2,1)S(1)}, bf16[128,256]{1,0:T(8,128)(2,1)S(1)}, u32[]{:S(2)}, u32[]{:S(2)}) collective-permute-start(bf16[128,256]{1,0:T(8,128)(2,1)S(1)} %get-tuple-element.39), channel_id=1, source_target_pairs={{0,24},{8,0},{16,8},{24,16},{32,56},{40,32},{48,40},{56,48},{64,88... | collective-permute-start | bytes 196616 | tf_op jit(solution)/shard_map/ppermute | solution.py:121
  60.0 7.4 %collective-permute-start.2 = (bf16[128,256]{1,0:T(8,128)(2,1)S(1)}, bf16[128,256]{1,0:T(8,128)(2,1)S(1)}, u32[]{:S(2)}, u32[]{:S(2)}) collective-permute-start(bf16[128,256]{1,0:T(8,128)(2,1)S(1)} %get-tuple-element.38), channel_id=1, source_target_pairs={{0,16},{8,24},{16,0},{24,8},{32,48},{40,56},{48,32},{56,40},{64,80... | collective-permute-start | bytes 196616 | tf_op jit(solution)/shard_map/ppermute | solution.py:121
  63.3 5.2 %collective-permute-start.1 = (bf16[128,256]{1,0:T(8,128)(2,1)S(1)}, bf16[128,256]{1,0:T(8,128)(2,1)S(1)}, u32[]{:S(2)}, u32[]{:S(2)}) collective-permute-start(bf16[128,256]{1,0:T(8,128)(2,1)S(1)} %get-tuple-element.37), channel_id=1, source_target_pairs={{0,8},{8,16},{16,24},{24,0},{32,40},{40,48},{48,56},{56,32},{64,72... | collective-permute-start | bytes 196616 | tf_op jit(solution)/shard_map/ppermute | solution.py:121
  75.3 6.5 %collective-permute-start.4 = (bf16[128,256]{1,0:T(8,128)(2,1)}, bf16[128,256]{1,0:T(8,128)(2,1)}, u32[]{:S(2)}, u32[]{:S(2)}) collective-permute-start(bf16[128,256]{1,0:T(8,128)(2,1)} %get-tuple-element.54), channel_id=1, source_target_pairs={{0,32},{8,40},{16,48},{24,56},{32,64},{40,72},{48,80},{56,88},{64,... | collective-permute-start | bytes 196616 | tf_op jit(solution)/shard_map/ppermute | solution.py:25
  81.7 47.0 %copy-start.10 = (f32[128,256]{1,0:T(8,128)S(1)}, f32[128,256]{1,0:T(8,128)}, u32[]{:S(2)}) copy-start(f32[128,256]{1,0:T(8,128)} %copy-done.9) | copy-start | bytes 393220
  87.5 9.2 %collective-permute-start.5 = (bf16[128,256]{1,0:T(8,128)(2,1)S(1)}, bf16[128,256]{1,0:T(8,128)(2,1)S(1)}, u32[]{:S(2)}, u32[]{:S(2)}) collective-permute-start(bf16[128,256]{1,0:T(8,128)(2,1)S(1)} %pad_maximum_fusion.4), channel_id=1, source_target_pairs={{0,64},{8,72},{16,80},{24,88},{32,96},{40,104},{48,112},{56,120},{... | collective-permute-start | bytes 196616 | tf_op jit(solution)/shard_map/ppermute | solution.py:25
  100.5 28.2 %copy-start.12 = (f32[128,256]{1,0:T(8,128)S(1)}, f32[128,256]{1,0:T(8,128)}, u32[]{:S(2)}) copy-start(f32[128,256]{1,0:T(8,128)} %copy-done.11) | copy-start | bytes 393220
  100.5 28.2 %copy-start.17 = (f32[1,128,256]{2,1,0:T(8,128)S(1)}, f32[1,128,256]{2,1,0:T(8,128)}, u32[]{:S(2)}) copy-start(f32[1,128,256]{2,1,0:T(8,128)} %pad_bitcast_fusion) | copy-start | bytes 393220
  100.6 28.3 %copy-start.18 = (f32[1,128,256]{2,1,0:T(8,128)S(1)}, f32[1,128,256]{2,1,0:T(8,128)}, u32[]{:S(2)}) copy-start(f32[1,128,256]{2,1,0:T(8,128)} %get-tuple-element.36) | copy-start | bytes 393220
  101.7 40.0 %copy-start.3 = (f32[4,128,256]{2,1,0:T(8,128)S(1)}, f32[4,128,256]{2,1,0:T(8,128)}, u32[]{:S(2)}) copy-start(f32[4,128,256]{2,1,0:T(8,128)} %copy-done.2) | copy-start | bytes 1572868
  101.8 40.0 %copy-start.13 = (f32[4,128,128]{2,1,0:T(8,128)S(1)}, f32[4,128,128]{2,1,0:T(8,128)}, u32[]{:S(2)}) copy-start(f32[4,128,128]{2,1,0:T(8,128)} %convolution_multiply_fusion.3) | copy-start | bytes 786436
  102.6 10.4 %collective-permute-start.6 = (bf16[128,256]{1,0:T(8,128)(2,1)S(1)}, bf16[128,256]{1,0:T(8,128)(2,1)S(1)}, u32[]{:S(2)}, u32[]{:S(2)}) collective-permute-start(bf16[128,256]{1,0:T(8,128)(2,1)S(1)} %pad_maximum_fusion.5), channel_id=1, source_target_pairs={{0,128},{8,136},{16,144},{24,152},{32,160},{40,168},{48,176},{56,1... | collective-permute-start | bytes 196616 | tf_op jit(solution)/shard_map/ppermute | solution.py:25
  114.1 13.2 %collective-permute-start.7 = (bf16[128,128]{1,0:T(8,128)(2,1)S(1)}, bf16[128,128]{1,0:T(8,128)(2,1)S(1)}, u32[]{:S(2)}, u32[]{:S(2)}) collective-permute-start(bf16[128,128]{1,0:T(8,128)(2,1)S(1)} %get-tuple-element.60), channel_id=1, source_target_pairs={{0,256},{8,264},{16,272},{24,280},{32,288},{40,296},{48,304},{56,3... | collective-permute-start | bytes 98312 | tf_op jit(solution)/shard_map/ppermute | solution.py:25
  127.5 2.6 collective-permute-start.8
  128.9 19.4 %copy-start.36 = (pred[4]{0:T(512)(128)(4,1)S(1)}, pred[4]{0:T(512)(128)(4,1)}, u32[]{:S(2)}) copy-start(pred[4]{0:T(512)(128)(4,1)} %compare_and_fusion.2) | copy-start | bytes 16
  131.3 18.6 %copy-start.37 = (f32[128]{0:T(128)S(1)}, f32[128]{0:T(128)}, u32[]{:S(2)}) copy-start(f32[128]{0:T(128)} %param.25) | copy-start | bytes 1540
  131.4 11.9 %collective-permute-start.9 = (f32[128,128]{1,0:T(8,128)S(1)}, f32[128,128]{1,0:T(8,128)S(1)}, u32[]{:S(2)}, u32[]{:S(2)}) collective-permute-start(f32[128,128]{1,0:T(8,128)S(1)} %get-tuple-element.45), channel_id=1, source_target_pairs={{0,8},{8,16},{16,24},{24,0},{32,40},{40,48},{48,56},{56,32},{64,72... | collective-permute-start | bytes 196616 | tf_op jit(solution)/shard_map/ppermute | solution.py:121
  135.3 7.9 %collective-permute-start.10 = (f32[128,128]{1,0:T(8,128)S(1)}, f32[128,128]{1,0:T(8,128)S(1)}, u32[]{:S(2)}, u32[]{:S(2)}) collective-permute-start(f32[128,128]{1,0:T(8,128)S(1)} %get-tuple-element.44), channel_id=1, source_target_pairs={{0,16},{8,24},{16,0},{24,8},{32,48},{40,56},{48,32},{56,40},{64,80... | collective-permute-start | bytes 196616 | tf_op jit(solution)/shard_map/ppermute | solution.py:121
  139.9 5.3 %collective-permute-start.11 = (f32[128,128]{1,0:T(8,128)S(1)}, f32[128,128]{1,0:T(8,128)S(1)}, u32[]{:S(2)}, u32[]{:S(2)}) collective-permute-start(f32[128,128]{1,0:T(8,128)S(1)} %get-tuple-element.43), channel_id=1, source_target_pairs={{0,24},{8,0},{16,8},{24,16},{32,56},{40,32},{48,40},{56,48},{64,88... | collective-permute-start | bytes 196616 | tf_op jit(solution)/shard_map/ppermute | solution.py:121
  151.8 53.8 %copy-start.21 = (bf16[128,256]{1,0:T(8,128)(2,1)S(1)}, bf16[128,256]{1,0:T(8,128)(2,1)}, u32[]{:S(2)}) copy-start(bf16[128,256]{1,0:T(8,128)(2,1)} %param.17) | copy-start | bytes 196612
  154.0 205.4 %all-reduce.10.cloned.1.call-start = ((), (), s32[]{:S(2)}) async-start(), calls=%async_computation.4 | async-start | bytes 3145728 | tf_op jit(solution)/shard_map/psum | solution.py:288
  227.5 59.6 %copy-start.16 = (bf16[4,256,512]{2,1,0:T(8,128)(2,1)S(1)}, bf16[4,256,512]{2,1,0:T(8,128)(2,1)}, u32[]{:S(2)}) copy-start(bf16[4,256,512]{2,1,0:T(8,128)(2,1)} %param.32) | copy-start | bytes 3145732
  288.9 72.4 %copy-start.38 = (bf16[4,256,256]{2,1,0:T(8,128)(2,1)S(1)}, bf16[4,256,256]{2,1,0:T(8,128)(2,1)}, u32[]{:S(2)}) copy-start(bf16[4,256,256]{2,1,0:T(8,128)(2,1)} %param.33) | copy-start | bytes 1572868
  361.9 17.1 %copy-start.29 = (s32[128,10]{0,1:T(8,128)S(1)}, s32[128,10]{0,1:T(8,128)}, u32[]{:S(2)}) copy-start(s32[128,10]{0,1:T(8,128)} %param.30) | copy-start | bytes 15364
  361.9 17.3 %copy-start.30 = (f32[128,10]{0,1:T(8,128)S(1)}, f32[128,10]{0,1:T(8,128)}, u32[]{:S(2)}) copy-start(f32[128,10]{0,1:T(8,128)} %param.31) | copy-start | bytes 15364
  363.4 60.1 %all-to-all-start.1 = ((bf16[64,6,4,256]{3,2,1,0:T(4,128)(2,1)}), bf16[64,6,4,256]{3,2,1,0:T(4,128)(2,1)}, u32[]{:S(2)}, u32[]{:S(2)}) async-start(bf16[64,6,4,256]{3,2,1,0:T(4,128)(2,1)} %bitcast.44), calls=%async_computation.2 | async-start | bytes 1572864 | tf_op jit(solution)/shard_map/all_to_all | solution.py:301
  (22 other events, 85.6 us)
Sparse Core Ops, SparseCore 0:
  154.2 51.4 reduce-scatter.1
  289.0 70.3 all-reduce.9

commit v6 on v4

--- a/solution.py
+++ b/solution.py
@@ -240,9 +240,12 @@
         .reshape(length, value_heads * DV)
     )
     partial_value = jnp.dot(normed_heads, out_weight, preferred_element_type=jnp.float32)
-    attended = lax.psum_scatter(
-        partial_value.astype(jnp.bfloat16), "head", scatter_dimension=1, tiled=True
-    ).astype(jnp.float32)
+    head_count = lax.axis_size("head")
+    blocks = partial_value.astype(jnp.bfloat16).reshape(length, head_count, -1)
+    blocks = lax.all_to_all(
+        jnp.transpose(blocks, (1, 0, 2)), "head", split_axis=0, concat_axis=0, tiled=True
+    )
+    attended = jnp.sum(blocks.astype(jnp.float32), axis=0)
     hidden = tokens_in.astype(jnp.float32) + attended
     steer_onehot = (steer_index[:, None] == jnp.arange(steer_table.shape[0])[None, :]).astype(
         jnp.float32

time: 431 us -> 395 us (0.916)
  waiting for transfers between devices: 160 us -> 129 us
  starting transfers between devices: 77.7 us -> 87.9 us
  matrix products: 34.3 us -> 26.6 us
  local copies, waits for them, and re-layouts: 46.6 us -> 40.6 us
  other arithmetic: 24.4 us -> 19 us
  blocking collectives: 70.8 us -> 75.9 us
    reduce_scatter x1 -> x0, waiting for transfers between devices: 42.9 us -> none  [local(): lax.psum_scatter(partial_value.astype(jnp.bfloat16), 'head', scatter_dime...]
    all_to_all x0 -> x1, starting transfers between devices: none -> 9.77 us  [local(): lax.all_to_all(jnp.transpose(blocks, (1, 0, 2)), 'head', split_axis=0, co...]
    all_to_all x0 -> x1, waiting for transfers between devices: none -> 7.45 us  [local(): lax.all_to_all(jnp.transpose(blocks, (1, 0, 2)), 'head', split_axis=0, co...]
    all_to_all x1, blocking collectives: 58.9 us -> 64 us  [local(): lax.all_to_all(outgoing, 'seq', split_axis=0, concat_axis=0, tiled=True)]
    ppermute x6, starting transfers between devices: 40.3 us -> 45.2 us  [passed_along(): lax.ppermute(value, axis, [(source, source + steps) for source in range(f...]
    ppermute x6, starting transfers between devices: 22 us -> 17.6 us  [within_group(): return lax.ppermute(value, 'seq', pairs)]
  transfers between devices with their start and end apart: 15 -> 15, of which waited for: 8 -> 9; matrix products, arithmetic and copies ran while one was open for 8% -> 7% of each run, Pallas kernels for 0% -> 0%
where the time goes in v6:
time: 395 us; the launch traced here: 394 us
  waiting for transfers between devices  129 us (33%)
  starting transfers between devices  87.9 us (22%)
  blocking collectives  75.9 us (19%)
  local copies, waits for them, and re-layouts  40.6 us (10%)
  matrix products  26.6 us (7%)
  other arithmetic  19 us (5%)
  between operations  14.7 us (4%)
    psum x1, waiting for transfers between devices, local(): lax.psum(term_rows.reshape(row_count, -1).astype(jnp.bfloat16), 'head')  70.7 us
    all_to_all x1, blocking collectives, local(): lax.all_to_all(outgoing, 'seq', split_axis=0, concat_axis=0, tiled=True)  64 us
    ppermute x6, starting transfers between devices, passed_along(): lax.ppermute(value, axis, [(source, source + steps) for source in range(f...  45.2 us
    all_to_all x1, waiting for transfers between devices, local(): lax.all_to_all(results.reshape(seq_size, capacity, experts_here, -1), 'se...  44.2 us
    ppermute x6, starting transfers between devices, within_group(): return lax.ppermute(value, 'seq', pairs)  17.6 us
    all_to_all x1, starting transfers between devices, local(): lax.all_to_all(results.reshape(seq_size, capacity, experts_here, -1), 'se...  15.3 us
    psum x1, blocking collectives, local(): lax.psum((jnp.sum(hidden * hidden, axis=1), jnp.sum(steered * steered, ax...  11.9 us
    all_to_all x1, starting transfers between devices, local(): lax.all_to_all(jnp.transpose(blocks, (1, 0, 2)), 'head', split_axis=0, co...  9.77 us
  transfers between devices with their start and end apart: 15, of which 9 were waited for; matrix products, arithmetic and copies ran while one was open for 7% of the time, Pallas kernels for 0%

profile of v6, /device:TPU:15, one launch (start us, length us, event | category | flops | bytes accessed | tf_op | source)
XLA Modules:
  0.0 393.9 jit_solution(14127063372004178333)
XLA Ops:
  7.4 3.2 collective-permute-start
  18.2 1.8 broadcast_add_fusion
  33.7 1.6 fusion.35
  37.8 2.9 collective-permute-start.1
  40.8 2.9 collective-permute-start.2
  43.7 4.0 %collective-permute-start.3 = (f32[128,256]{1,0:T(8,128)}, f32[128,256]{1,0:T(8,128)}, u32[]{:S(2)}, u32[]{:S(2)}) collective-permute-start(f32[128,256]{1,0:T(8,128)} %get-tuple-element.40), channel_id=1, source_target_pairs={{0,24},{8,0},{16,8},{24,16},{32,56},{40,32},{48,40},{56,48},{64,88... | collective-permute-start | bytes 393224 | tf_op jit(solution)/shard_map/ppermute | solution.py:120
  48.5 3.4 collective-permute-done.3
  52.0 1.8 pad_maximum_fusion.1
  53.8 2.5 gather_fusion
  61.0 4.2 %collective-permute-start.4 = (f32[128,256]{1,0:T(8,128)}, f32[128,256]{1,0:T(8,128)}, u32[]{:S(2)}, u32[]{:S(2)}) collective-permute-start(f32[128,256]{1,0:T(8,128)} %convolution_add_fusion.5), channel_id=1, source_target_pairs={{0,32},{8,40},{16,48},{24,56},{32,64},{40,72},{48,80},{56,88},{64,... | collective-permute-start | bytes 393224 | tf_op jit(solution)/shard_map/ppermute | solution.py:24
  66.0 5.2 %scatter_custom_fusion = s32[1536]{0:T(1024)S(1)} fusion(s32[1280]{0:T(1024)S(1)} %fusion.117, s32[1280]{0:T(1024)S(1)} %add_select_fusion, s32[]{:T(128)} %constant.515.clone.1), kind=kCustom, calls=%fused_computation.233 | custom fusion | bytes 6148 | tf_op jit(solution)/shard_map/scatter | solution.py:280
  71.9 1.7 copy.94
  76.0 4.2 %collective-permute-start.5 = (f32[128,256]{1,0:T(8,128)S(1)}, f32[128,256]{1,0:T(8,128)S(1)}, u32[]{:S(2)}, u32[]{:S(2)}) collective-permute-start(f32[128,256]{1,0:T(8,128)S(1)} %pad_maximum_fusion.4), channel_id=1, source_target_pairs={{0,64},{8,72},{16,80},{24,88},{32,96},{40,104},{48,112},{56,120},{... | collective-permute-start | bytes 393224 | tf_op jit(solution)/shard_map/ppermute | solution.py:24
  81.0 1.9 convolution_multiply_fusion.3
  85.1 9.6 %collective-permute-start.6 = (f32[128,256]{1,0:T(8,128)S(1)}, f32[128,256]{1,0:T(8,128)S(1)}, u32[]{:S(2)}, u32[]{:S(2)}) collective-permute-start(f32[128,256]{1,0:T(8,128)S(1)} %pad_maximum_fusion.5), channel_id=1, source_target_pairs={{0,128},{8,136},{16,144},{24,152},{32,160},{40,168},{48,176},{56,1... | collective-permute-start | bytes 393224 | tf_op jit(solution)/shard_map/ppermute | solution.py:24
  96.9 22.9 %collective-permute-start.7 = (f32[128,128]{1,0:T(8,128)S(1)}, f32[128,128]{1,0:T(8,128)S(1)}, u32[]{:S(2)}, u32[]{:S(2)}) collective-permute-start(f32[128,128]{1,0:T(8,128)S(1)} %convolution_add_fusion.10), channel_id=1, source_target_pairs={{0,256},{8,264},{16,272},{24,280},{32,288},{40,296},{48,304},{56,3... | collective-permute-start | bytes 196616 | tf_op jit(solution)/shard_map/ppermute | solution.py:24
  125.2 2.1 collective-permute-start.9
  127.3 1.9 collective-permute-start.10
  129.2 3.7 collective-permute-start.11
  139.8 9.8 %all-to-all-start = ((bf16[8,128,256]{2,1,0:T(8,128)(2,1)}), bf16[8,128,256]{2,1,0:T(8,128)(2,1)S(1)}, u32[]{:S(2)}, u32[]{:S(2)}) async-start(bf16[8,128,256]{2,1,0:T(8,128)(2,1)} %bitcast.119), calls=%async_computation | async-start | bytes 1048576 | tf_op jit(solution)/shard_map/all_to_all | solution.py:245
  149.8 7.5 %all-to-all-done = bf16[8,128,256]{2,1,0:T(8,128)(2,1)S(1)} async-done(((bf16[8,128,256]{2,1,0:T(8,128)(2,1)}), bf16[8,128,256]{2,1,0:T(8,128)(2,1)S(1)}, u32[]{:S(2)}, u32[]{:S(2)}) %all-to-all-start) | async-done | bytes 524320 | tf_op jit(solution)/shard_map/all_to_all | solution.py:245
  157.8 11.9 %all-reduce.7 = (f32[128]{0:T(128)S(1)}, f32[128]{0:T(128)S(1)}) all-reduce(f32[128]{0:T(128)S(1)} %get-tuple-element.57, f32[128]{0:T(128)S(1)} %multiply_reduce_fusion.3), channel_id=1, replica_groups=mesh['seq'=64,'head'=8] {'head'}, use_global_device_ids=true, to_apply=%region_8.9 | all-reduce | flops 256 | bytes 2048 | tf_op jit(solution)/shard_map/psum | solution.py:256
  169.8 5.4 %gather_fusion.2 = bf16[1536,256]{1,0:T(8,128)(2,1)} fusion(bf16[129,256]{1,0:T(8,128)(2,1)S(1)} %concatenate.44, s32[2048]{0:T(1024)S(1)} %pad_clamp_fusion.1), kind=kCustom, calls=%fused_computation.2 | custom fusion | bytes 1579008 | tf_op jit(solution)/shard_map/jit(_take)/gather | solution.py:283
  175.1 1.7 gather.23
  177.5 64.0 %all_to_all.15 = bf16[64,6,4,256]{3,2,1,0:T(4,128)(2,1)S(1)} all-to-all(bf16[64,6,4,256]{3,2,1,0:T(4,128)(2,1)S(1)} %broadcast_select_fusion), channel_id=1, replica_groups=mesh['seq'=64,'head'=8] {'seq'}, dimensions={0} | all-to-all | bytes 1572864 | tf_op jit(solution)/shard_map/all_to_all | solution.py:284
  241.5 1.7 fusion.3
  243.3 70.7 %all-reduce.10.cloned.1.call-done = bf16[384,4,512]{2,0,1:T(8,128)(2,1)} async-done(((bf16[384,4,512]{2,0,1:T(8,128)(2,1)}), bf16[384,4,512]{2,0,1:T(8,128)(2,1)}) %all-reduce.10.cloned.1.call-update) | async-done | bytes 1572880 | tf_op jit(solution)/shard_map/psum | solution.py:289
  314.0 1.8 reshape.1117
  318.0 15.3 %all-to-all-start.2 = ((bf16[64,6,4,256]{3,2,1,0:T(4,128)(2,1)}), bf16[64,6,4,256]{3,2,1,0:T(4,128)(2,1)}, u32[]{:S(2)}, u32[]{:S(2)}) async-start(bf16[64,6,4,256]{3,2,1,0:T(4,128)(2,1)} %bitcast.45), calls=%async_computation.2 | async-start | bytes 1572864 | tf_op jit(solution)/shard_map/all_to_all | solution.py:302
  333.9 44.2 %all-to-all-done.2 = bf16[64,6,4,256]{3,2,1,0:T(4,128)(2,1)} async-done(((bf16[64,6,4,256]{3,2,1,0:T(4,128)(2,1)}), bf16[64,6,4,256]{3,2,1,0:T(4,128)(2,1)}, u32[]{:S(2)}, u32[]{:S(2)}) %all-to-all-start.2) | async-done | bytes 786464 | tf_op jit(solution)/shard_map/all_to_all | solution.py:302
  378.1 1.6 reshape.1119
  379.6 4.7 %gather_fusion.3 = bf16[1280,256]{1,0:T(8,128)(2,1)} fusion(bf16[1536,256]{1,0:T(8,128)(2,1)S(1)} %reshape.1119, s32[2048]{0:T(1024)S(1)} %pad_clamp_fusion), kind=kCustom, calls=%fused_computation.3 | custom fusion | bytes 1315840 | tf_op jit(solution)/shard_map/jit(_take)/gather | solution.py:311
  (209 shorter events, 57.7 us)
Async XLA Ops:
  6.5 131.9 %copy-start = (bf16[512,2048]{1,0:T(8,128)(2,1)S(1)}, bf16[512,2048]{1,0:T(8,128)(2,1)}, u32[]{:S(2)}) copy-start(bf16[512,2048]{1,0:T(8,128)(2,1)} %param.26) | copy-start | bytes 6291460
  7.4 16.2 %collective-permute-start = (bf16[3,1024]{1,0:T(4,128)(2,1)S(1)}, bf16[3,1024]{1,0:T(4,128)(2,1)S(1)}, u32[]{:S(2)}, u32[]{:S(2)}) collective-permute-start(bf16[3,1024]{1,0:T(4,128)(2,1)S(1)} %slice.129), channel_id=1, source_target_pairs={{0,8},{8,16},{16,24},{24,32},{32,40},{40,48},{48,56},{56,64},{64,7... | collective-permute-start | bytes 18440 | tf_op jit(solution)/shard_map/ppermute | solution.py:24
  10.7 14.3 %copy-start.12 = (pred[128,128]{1,0:T(8,128)(4,1)}, pred[128,128]{1,0:T(8,128)(4,1)S(1)}, u32[]{:S(2)}) copy-start(pred[128,128]{1,0:T(8,128)(4,1)S(1)} %get-tuple-element.83) | copy-start | bytes 49156
  13.7 11.2 %copy-start.14 = (f32[4,128]{1,0:T(4,128)}, f32[4,128]{1,0:T(4,128)S(1)}, u32[]{:S(2)}) copy-start(f32[4,128]{1,0:T(4,128)S(1)} %reduce_window_sum.27) | copy-start | bytes 6148
  21.4 11.0 %copy-start.15 = (f32[4,128]{1,0:T(4,128)}, f32[4,128]{1,0:T(4,128)S(1)}, u32[]{:S(2)}) copy-start(f32[4,128]{1,0:T(4,128)S(1)} %get-tuple-element.52) | copy-start | bytes 6148
  37.8 10.7 %collective-permute-start.1 = (f32[128,256]{1,0:T(8,128)}, f32[128,256]{1,0:T(8,128)S(1)}, u32[]{:S(2)}, u32[]{:S(2)}) collective-permute-start(f32[128,256]{1,0:T(8,128)} %get-tuple-element.38), channel_id=1, source_target_pairs={{0,8},{8,16},{16,24},{24,0},{32,40},{40,48},{48,56},{56,32},{64,72... | collective-permute-start | bytes 393224 | tf_op jit(solution)/shard_map/ppermute | solution.py:120
  40.8 7.8 %collective-permute-start.2 = (f32[128,256]{1,0:T(8,128)}, f32[128,256]{1,0:T(8,128)S(1)}, u32[]{:S(2)}, u32[]{:S(2)}) collective-permute-start(f32[128,256]{1,0:T(8,128)} %get-tuple-element.39), channel_id=1, source_target_pairs={{0,16},{8,24},{16,0},{24,8},{32,48},{40,56},{48,32},{56,40},{64,80... | collective-permute-start | bytes 393224 | tf_op jit(solution)/shard_map/ppermute | solution.py:120
  43.7 8.3 %collective-permute-start.3 = (f32[128,256]{1,0:T(8,128)}, f32[128,256]{1,0:T(8,128)}, u32[]{:S(2)}, u32[]{:S(2)}) collective-permute-start(f32[128,256]{1,0:T(8,128)} %get-tuple-element.40), channel_id=1, source_target_pairs={{0,24},{8,0},{16,8},{24,16},{32,56},{40,32},{48,40},{56,48},{64,88... | collective-permute-start | bytes 393224 | tf_op jit(solution)/shard_map/ppermute | solution.py:120
  48.4 7.9 %copy-start.24 = (pred[4]{0:T(512)(128)(4,1)S(1)}, pred[4]{0:T(512)(128)(4,1)}, u32[]{:S(2)}) copy-start(pred[4]{0:T(512)(128)(4,1)} %compare_and_fusion.2) | copy-start | bytes 16
  48.5 17.5 %copy-start.18 = (s32[1280]{0:T(1024)}, s32[1280]{0:T(1024)S(1)}, u32[]{:S(2)}) copy-start(s32[1280]{0:T(1024)S(1)} %fusion.117) | copy-start | bytes 15364
  56.3 8.8 %copy-start.6 = (f32[128,512]{0,1:T(8,128)S(1)}, f32[128,512]{0,1:T(8,128)}, u32[]{:S(2)}) copy-start(f32[128,512]{0,1:T(8,128)} %convert_multiply_fusion) | copy-start | bytes 786436
  61.0 12.6 %collective-permute-start.4 = (f32[128,256]{1,0:T(8,128)}, f32[128,256]{1,0:T(8,128)}, u32[]{:S(2)}, u32[]{:S(2)}) collective-permute-start(f32[128,256]{1,0:T(8,128)} %convolution_add_fusion.5), channel_id=1, source_target_pairs={{0,32},{8,40},{16,48},{24,56},{32,64},{40,72},{48,80},{56,88},{64,... | collective-permute-start | bytes 393224 | tf_op jit(solution)/shard_map/ppermute | solution.py:24
  76.0 7.0 %collective-permute-start.5 = (f32[128,256]{1,0:T(8,128)S(1)}, f32[128,256]{1,0:T(8,128)S(1)}, u32[]{:S(2)}, u32[]{:S(2)}) collective-permute-start(f32[128,256]{1,0:T(8,128)S(1)} %pad_maximum_fusion.4), channel_id=1, source_target_pairs={{0,64},{8,72},{16,80},{24,88},{32,96},{40,104},{48,112},{56,120},{... | collective-permute-start | bytes 393224 | tf_op jit(solution)/shard_map/ppermute | solution.py:24
  85.1 47.8 %copy-start.4 = (f32[4,128,128]{2,1,0:T(8,128)S(1)}, f32[4,128,128]{2,1,0:T(8,128)}, u32[]{:S(2)}) copy-start(f32[4,128,128]{2,1,0:T(8,128)} %convolution_multiply_fusion.3) | copy-start | bytes 786436
  85.1 11.5 %collective-permute-start.6 = (f32[128,256]{1,0:T(8,128)S(1)}, f32[128,256]{1,0:T(8,128)S(1)}, u32[]{:S(2)}, u32[]{:S(2)}) collective-permute-start(f32[128,256]{1,0:T(8,128)S(1)} %pad_maximum_fusion.5), channel_id=1, source_target_pairs={{0,128},{8,136},{16,144},{24,152},{32,160},{40,168},{48,176},{56,1... | collective-permute-start | bytes 393224 | tf_op jit(solution)/shard_map/ppermute | solution.py:24
  96.9 24.2 %collective-permute-start.7 = (f32[128,128]{1,0:T(8,128)S(1)}, f32[128,128]{1,0:T(8,128)S(1)}, u32[]{:S(2)}, u32[]{:S(2)}) collective-permute-start(f32[128,128]{1,0:T(8,128)S(1)} %convolution_add_fusion.10), channel_id=1, source_target_pairs={{0,256},{8,264},{16,272},{24,280},{32,288},{40,296},{48,304},{56,3... | collective-permute-start | bytes 196616 | tf_op jit(solution)/shard_map/ppermute | solution.py:24
  121.3 2.6 collective-permute-start.8
  125.2 8.4 %collective-permute-start.9 = (f32[128,128]{1,0:T(8,128)S(1)}, f32[128,128]{1,0:T(8,128)S(1)}, u32[]{:S(2)}, u32[]{:S(2)}) collective-permute-start(f32[128,128]{1,0:T(8,128)S(1)} %get-tuple-element.46), channel_id=1, source_target_pairs={{0,8},{8,16},{16,24},{24,0},{32,40},{40,48},{48,56},{56,32},{64,72... | collective-permute-start | bytes 196616 | tf_op jit(solution)/shard_map/ppermute | solution.py:120
  127.3 6.5 %collective-permute-start.10 = (f32[128,128]{1,0:T(8,128)S(1)}, f32[128,128]{1,0:T(8,128)S(1)}, u32[]{:S(2)}, u32[]{:S(2)}) collective-permute-start(f32[128,128]{1,0:T(8,128)S(1)} %get-tuple-element.45), channel_id=1, source_target_pairs={{0,16},{8,24},{16,0},{24,8},{32,48},{40,56},{48,32},{56,40},{64,80... | collective-permute-start | bytes 196616 | tf_op jit(solution)/shard_map/ppermute | solution.py:120
  129.2 6.0 %collective-permute-start.11 = (f32[128,128]{1,0:T(8,128)S(1)}, f32[128,128]{1,0:T(8,128)S(1)}, u32[]{:S(2)}, u32[]{:S(2)}) collective-permute-start(f32[128,128]{1,0:T(8,128)S(1)} %get-tuple-element.44), channel_id=1, source_target_pairs={{0,24},{8,0},{16,8},{24,16},{32,56},{40,32},{48,40},{56,48},{64,88... | collective-permute-start | bytes 196616 | tf_op jit(solution)/shard_map/ppermute | solution.py:120
  138.9 18.4 %copy-start.10 = (bf16[128,256]{1,0:T(8,128)(2,1)S(1)}, bf16[128,256]{1,0:T(8,128)(2,1)}, u32[]{:S(2)}) copy-start(bf16[128,256]{1,0:T(8,128)(2,1)} %param.17) | copy-start | bytes 196612
  138.9 18.5 %copy-start.20 = (f32[16,256]{1,0:T(8,128)S(1)}, f32[16,256]{1,0:T(8,128)}, u32[]{:S(2)}) copy-start(f32[16,256]{1,0:T(8,128)} %param.27) | copy-start | bytes 49156
  138.9 18.5 %copy-start.26 = (s32[128]{0:T(128)S(1)}, s32[128]{0:T(128)}, u32[]{:S(2)}) copy-start(s32[128]{0:T(128)} %param.28) | copy-start | bytes 1540
  138.9 30.7 %copy-start.25 = (f32[256]{0:T(256)S(1)}, f32[256]{0:T(256)}, u32[]{:S(2)}) copy-start(f32[256]{0:T(256)} %param.29) | copy-start | bytes 3076
  139.8 17.4 %all-to-all-start = ((bf16[8,128,256]{2,1,0:T(8,128)(2,1)}), bf16[8,128,256]{2,1,0:T(8,128)(2,1)S(1)}, u32[]{:S(2)}, u32[]{:S(2)}) async-start(bf16[8,128,256]{2,1,0:T(8,128)(2,1)} %bitcast.119), calls=%async_computation | async-start | bytes 1048576 | tf_op jit(solution)/shard_map/all_to_all | solution.py:245
  149.5 164.5 %all-reduce.10.cloned.1.call-start = ((), (), s32[]{:S(2)}) async-start(), calls=%async_computation.3 | async-start | bytes 3145728 | tf_op jit(solution)/shard_map/psum | solution.py:289
  176.8 64.7 %copy-start.5 = (bf16[4,256,512]{2,1,0:T(8,128)(2,1)S(1)}, bf16[4,256,512]{2,1,0:T(8,128)(2,1)}, u32[]{:S(2)}) copy-start(bf16[4,256,512]{2,1,0:T(8,128)(2,1)} %param.32) | copy-start | bytes 3145732
  243.3 72.6 %copy-start.27 = (bf16[4,256,256]{2,1,0:T(8,128)(2,1)S(1)}, bf16[4,256,256]{2,1,0:T(8,128)(2,1)}, u32[]{:S(2)}) copy-start(bf16[4,256,256]{2,1,0:T(8,128)(2,1)} %param.33) | copy-start | bytes 1572868
  316.4 17.1 %copy-start.16 = (s32[128,10]{0,1:T(8,128)S(1)}, s32[128,10]{0,1:T(8,128)}, u32[]{:S(2)}) copy-start(s32[128,10]{0,1:T(8,128)} %param.30) | copy-start | bytes 15364
  316.5 17.3 %copy-start.17 = (f32[128,10]{0,1:T(8,128)S(1)}, f32[128,10]{0,1:T(8,128)}, u32[]{:S(2)}) copy-start(f32[128,10]{0,1:T(8,128)} %param.31) | copy-start | bytes 15364
  316.5 17.4 %copy-start.19 = (s32[1280]{0:T(1024)S(1)}, s32[1280]{0:T(1024)}, u32[]{:S(2)}) copy-start(s32[1280]{0:T(1024)} %copy-done.18) | copy-start | bytes 15364
  318.0 60.1 %all-to-all-start.2 = ((bf16[64,6,4,256]{3,2,1,0:T(4,128)(2,1)}), bf16[64,6,4,256]{3,2,1,0:T(4,128)(2,1)}, u32[]{:S(2)}, u32[]{:S(2)}) async-start(bf16[64,6,4,256]{3,2,1,0:T(4,128)(2,1)} %bitcast.45), calls=%async_computation.2 | async-start | bytes 1572864 | tf_op jit(solution)/shard_map/all_to_all | solution.py:302
  (11 other events, 26.3 us)
Sparse Core Ops, SparseCore 0:
  243.4 70.5 all-reduce.9

commit v7 on v6

--- a/solution.py
+++ b/solution.py
@@ -286,18 +286,28 @@
     arrived = arrived.reshape(row_count, experts_here, -1)
     ffn_width = w_down.shape[1]
     term_rows = jnp.einsum("red,edf->ref", arrived, w_gate_up, preferred_element_type=jnp.float32)
-    summed = lax.psum(term_rows.reshape(row_count, -1).astype(jnp.bfloat16), "head").astype(
-        jnp.float32
-    )
-    activate_summed = summed
-    activate_summed = activate_summed.reshape(activate_summed.shape[0], experts_here, 2 * ffn_width)
+    head_count = lax.axis_size("head")
+    slice_width = ffn_width // head_count
+    pieces = term_rows.astype(jnp.bfloat16).reshape(
+        row_count, experts_here, 2, head_count, slice_width
+    )
+    pieces = lax.all_to_all(
+        jnp.transpose(pieces, (3, 0, 1, 2, 4)), "head", split_axis=0, concat_axis=0, tiled=True
+    )
+    gate_up_slice = jnp.sum(pieces.astype(jnp.float32), axis=0)
+    activated_slice = (jax.nn.silu(gate_up_slice[:, :, 0]) * gate_up_slice[:, :, 1]).astype(
+        jnp.bfloat16
+    )
+    activated = lax.all_to_all(
+        jnp.broadcast_to(activated_slice[None], (head_count,) + activated_slice.shape),
+        "head",
+        split_axis=0,
+        concat_axis=0,
+        tiled=True,
+    )
+    activated = jnp.transpose(activated, (1, 2, 0, 3)).reshape(row_count, experts_here, ffn_width)
     results = jnp.einsum(
-        "ref,efd->red",
-        (jax.nn.silu(activate_summed[:, :, :ffn_width]) * activate_summed[:, :, ffn_width:]).astype(
-            jnp.bfloat16
-        ),
-        w_down,
-        preferred_element_type=jnp.float32,
+        "ref,efd->red", activated, w_down, preferred_element_type=jnp.float32
     ).astype(jnp.bfloat16)
     returned = lax.all_to_all(
         results.reshape(seq_size, capacity, experts_here, -1),

time: 395 us -> 347 us (0.88)
  the two profiles are of different devices: /device:TPU:15 before, /device:TPU:8 now
where the time goes in v7:
time: 347 us; the launch traced here: 345 us
  blocking collectives  117 us (34%)
  starting transfers between devices  75.8 us (22%)
  waiting for transfers between devices  62.2 us (18%)
  local copies, waits for them, and re-layouts  45.1 us (13%)
  matrix products  26.5 us (8%)
  other arithmetic  17.4 us (5%)
    all_to_all x1, blocking collectives, local(): lax.all_to_all(outgoing, 'seq', split_axis=0, concat_axis=0, tiled=True)  64.2 us
    ppermute x6, starting transfers between devices, passed_along(): lax.ppermute(value, axis, [(source, source + steps) for source in range(f...  43.4 us
    all_to_all x1, waiting for transfers between devices, local(): lax.all_to_all(results.reshape(seq_size, capacity, experts_here, -1), 'se...  43 us
    all_to_all x1, blocking collectives, local(): lax.all_to_all(jnp.transpose(pieces, (3, 0, 1, 2, 4)), 'head', split_axis...  24 us
    ppermute x6, starting transfers between devices, within_group(): return lax.ppermute(value, 'seq', pairs)  22 us
    all_to_all x1, blocking collectives, local(): lax.all_to_all(jnp.broadcast_to(activated_slice[None], (head_count,) + ac...  15.7 us
    psum x1, blocking collectives, local(): lax.psum((jnp.sum(hidden * hidden, axis=1), jnp.sum(steered * steered, ax...  12.7 us
    all_to_all x1, waiting for transfers between devices, local(): lax.all_to_all(jnp.transpose(blocks, (1, 0, 2)), 'head', split_axis=0, co...  10.1 us
  transfers between devices with their start and end apart: 14, of which 8 were waited for; matrix products, arithmetic and copies ran while one was open for 8% of the time, Pallas kernels for 0%

profile of v7, /device:TPU:8, one launch (start us, length us, event | category | flops | bytes accessed | tf_op | source)
XLA Modules:
  0.0 345.0 jit_solution(17577484560372587882)
XLA Ops:
  0.9 3.5 %collective-permute-start = (bf16[3,1024]{1,0:T(4,128)(2,1)S(1)}, bf16[3,1024]{1,0:T(4,128)(2,1)S(1)}, u32[]{:S(2)}, u32[]{:S(2)}) collective-permute-start(bf16[3,1024]{1,0:T(4,128)(2,1)S(1)} %slice.129), channel_id=1, source_target_pairs={{0,8},{8,16},{16,24},{24,32},{32,40},{40,48},{48,56},{56,64},{64,7... | collective-permute-start | bytes 18440 | tf_op jit(solution)/shard_map/ppermute | solution.py:24
  11.9 1.8 broadcast_add_fusion
  31.7 3.2 collective-permute-start.1
  34.9 6.3 %collective-permute-start.2 = (f32[128,256]{1,0:T(8,128)}, f32[128,256]{1,0:T(8,128)S(1)}, u32[]{:S(2)}, u32[]{:S(2)}) collective-permute-start(f32[128,256]{1,0:T(8,128)} %get-tuple-element.39), channel_id=1, source_target_pairs={{0,16},{8,24},{16,0},{24,8},{32,48},{40,56},{48,32},{56,40},{64,80... | collective-permute-start | bytes 393224 | tf_op jit(solution)/shard_map/ppermute | solution.py:120
  41.2 2.1 collective-permute-start.3
  45.3 3.1 collective-permute-done.3
  48.4 1.8 pad_maximum_fusion.1
  50.2 2.5 gather_fusion
  57.3 2.2 collective-permute-start.4
  60.4 5.2 %scatter_custom_fusion = s32[1536]{0:T(1024)S(1)} fusion(s32[1280]{0:T(1024)S(1)} %fusion.117, s32[1280]{0:T(1024)S(1)} %add_select_fusion, s32[]{:T(128)} %constant.515.clone.1), kind=kCustom, calls=%fused_computation.236 | custom fusion | bytes 6148 | tf_op jit(solution)/shard_map/scatter | solution.py:280
  66.3 1.7 copy.102
  70.4 4.8 %collective-permute-start.5 = (f32[128,256]{1,0:T(8,128)S(1)}, f32[128,256]{1,0:T(8,128)S(1)}, u32[]{:S(2)}, u32[]{:S(2)}) collective-permute-start(f32[128,256]{1,0:T(8,128)S(1)} %pad_maximum_fusion.4), channel_id=1, source_target_pairs={{0,64},{8,72},{16,80},{24,88},{32,96},{40,104},{48,112},{56,120},{... | collective-permute-start | bytes 393224 | tf_op jit(solution)/shard_map/ppermute | solution.py:24
  76.2 1.9 convolution_multiply_fusion.3
  80.3 11.7 %collective-permute-start.6 = (f32[128,256]{1,0:T(8,128)S(1)}, f32[128,256]{1,0:T(8,128)S(1)}, u32[]{:S(2)}, u32[]{:S(2)}) collective-permute-start(f32[128,256]{1,0:T(8,128)S(1)} %pad_maximum_fusion.5), channel_id=1, source_target_pairs={{0,128},{8,136},{16,144},{24,152},{32,160},{40,168},{48,176},{56,1... | collective-permute-start | bytes 393224 | tf_op jit(solution)/shard_map/ppermute | solution.py:24
  94.8 19.9 %collective-permute-start.7 = (f32[128,128]{1,0:T(8,128)S(1)}, f32[128,128]{1,0:T(8,128)S(1)}, u32[]{:S(2)}, u32[]{:S(2)}) collective-permute-start(f32[128,128]{1,0:T(8,128)S(1)} %convolution_add_fusion.10), channel_id=1, source_target_pairs={{0,256},{8,264},{16,272},{24,280},{32,288},{40,296},{48,304},{56,3... | collective-permute-start | bytes 196616 | tf_op jit(solution)/shard_map/ppermute | solution.py:24
  121.2 2.4 collective-permute-start.9
  123.6 3.4 collective-permute-start.10
  127.1 4.5 %collective-permute-start.11 = (f32[128,128]{1,0:T(8,128)S(1)}, f32[128,128]{1,0:T(8,128)S(1)}, u32[]{:S(2)}, u32[]{:S(2)}) collective-permute-start(f32[128,128]{1,0:T(8,128)S(1)} %get-tuple-element.44), channel_id=1, source_target_pairs={{0,24},{8,0},{16,8},{24,16},{32,56},{40,32},{48,40},{56,48},{64,88... | collective-permute-start | bytes 196616 | tf_op jit(solution)/shard_map/ppermute | solution.py:120
  138.1 4.3 %all-to-all-start = ((bf16[8,128,256]{2,1,0:T(8,128)(2,1)}), bf16[8,128,256]{2,1,0:T(8,128)(2,1)S(1)}, u32[]{:S(2)}, u32[]{:S(2)}) async-start(bf16[8,128,256]{2,1,0:T(8,128)(2,1)} %bitcast.138), calls=%async_computation | async-start | bytes 1048576 | tf_op jit(solution)/shard_map/all_to_all | solution.py:245
  142.6 10.1 %all-to-all-done = bf16[8,128,256]{2,1,0:T(8,128)(2,1)S(1)} async-done(((bf16[8,128,256]{2,1,0:T(8,128)(2,1)}), bf16[8,128,256]{2,1,0:T(8,128)(2,1)S(1)}, u32[]{:S(2)}, u32[]{:S(2)}) %all-to-all-start) | async-done | bytes 524320 | tf_op jit(solution)/shard_map/all_to_all | solution.py:245
  153.2 12.7 %all-reduce.7 = (f32[128]{0:T(128)S(1)}, f32[128]{0:T(128)S(1)}) all-reduce(f32[128]{0:T(128)S(1)} %get-tuple-element.57, f32[128]{0:T(128)S(1)} %multiply_reduce_fusion.3), channel_id=1, replica_groups=mesh['seq'=64,'head'=8] {'head'}, use_global_device_ids=true, to_apply=%region_8.9 | all-reduce | flops 256 | bytes 2048 | tf_op jit(solution)/shard_map/psum | solution.py:256
  166.1 5.4 %gather_fusion.2 = bf16[1536,256]{1,0:T(8,128)(2,1)} fusion(bf16[129,256]{1,0:T(8,128)(2,1)S(1)} %concatenate.44, s32[2048]{0:T(1024)S(1)} %pad_clamp_fusion.1), kind=kCustom, calls=%fused_computation.2 | custom fusion | bytes 1579008 | tf_op jit(solution)/shard_map/jit(_take)/gather | solution.py:283
  171.4 1.7 gather.23
  173.8 64.2 %all_to_all.25 = bf16[64,6,4,256]{3,2,1,0:T(4,128)(2,1)S(1)} all-to-all(bf16[64,6,4,256]{3,2,1,0:T(4,128)(2,1)S(1)} %broadcast_select_fusion), channel_id=1, replica_groups=mesh['seq'=64,'head'=8] {'seq'}, dimensions={0} | all-to-all | bytes 1572864 | tf_op jit(solution)/shard_map/all_to_all | solution.py:284
  238.0 1.7 fusion.2
  239.8 2.6 copy.128
  242.4 1.7 copy.129
  244.0 24.0 %all_to_all.26 = bf16[8,384,4,2,32]{1,4,3,2,0:T(8,128)(2,1)S(1)} all-to-all(bf16[8,384,4,2,32]{1,4,3,2,0:T(8,128)(2,1)S(1)} %copy.129), channel_id=1, replica_groups=mesh['seq'=64,'head'=8] {'head'}, dimensions={0} | all-to-all | bytes 3145728 | tf_op jit(solution)/shard_map/all_to_all | solution.py:294
  268.5 15.7 %all_to_all.27 = bf16[8,384,4,32]{1,3,2,0:T(8,128)(2,1)S(1)} all-to-all(bf16[8,384,4,32]{1,3,2,0:T(8,128)(2,1)S(1)} %broadcast_in_dim.215), channel_id=1, replica_groups=mesh['seq'=64,'head'=8] {'head'}, dimensions={0} | all-to-all | bytes 1572864 | tf_op jit(solution)/shard_map/all_to_all | solution.py:301
  286.3 6.1 %all-to-all-start.4 = ((bf16[64,6,4,256]{3,2,1,0:T(4,128)(2,1)}), bf16[64,6,4,256]{3,2,1,0:T(4,128)(2,1)}, u32[]{:S(2)}, u32[]{:S(2)}) async-start(bf16[64,6,4,256]{3,2,1,0:T(4,128)(2,1)} %bitcast.51), calls=%async_computation.4 | async-start | bytes 1572864 | tf_op jit(solution)/shard_map/all_to_all | solution.py:312
  293.0 43.0 %all-to-all-done.4 = bf16[64,6,4,256]{3,2,1,0:T(4,128)(2,1)} async-done(((bf16[64,6,4,256]{3,2,1,0:T(4,128)(2,1)}), bf16[64,6,4,256]{3,2,1,0:T(4,128)(2,1)}, u32[]{:S(2)}, u32[]{:S(2)}) %all-to-all-start.4) | async-done | bytes 786464 | tf_op jit(solution)/shard_map/all_to_all | solution.py:312
  337.5 4.7 %gather_fusion.3 = bf16[1280,256]{1,0:T(8,128)(2,1)} fusion(bf16[1536,256]{1,0:T(8,128)(2,1)S(1)} %reshape.1135, s32[2048]{0:T(1024)S(1)} %pad_clamp_fusion), kind=kCustom, calls=%fused_computation.3 | custom fusion | bytes 1315840 | tf_op jit(solution)/shard_map/jit(_take)/gather | solution.py:321
  (213 shorter events, 63.7 us)
Async XLA Ops:
  0.0 136.7 %copy-start = (bf16[512,2048]{1,0:T(8,128)(2,1)S(1)}, bf16[512,2048]{1,0:T(8,128)(2,1)}, u32[]{:S(2)}) copy-start(bf16[512,2048]{1,0:T(8,128)(2,1)} %param.26) | copy-start | bytes 6291460
  0.9 16.5 %collective-permute-start = (bf16[3,1024]{1,0:T(4,128)(2,1)S(1)}, bf16[3,1024]{1,0:T(4,128)(2,1)S(1)}, u32[]{:S(2)}, u32[]{:S(2)}) collective-permute-start(bf16[3,1024]{1,0:T(4,128)(2,1)S(1)} %slice.129), channel_id=1, source_target_pairs={{0,8},{8,16},{16,24},{24,32},{32,40},{40,48},{48,56},{56,64},{64,7... | collective-permute-start | bytes 18440 | tf_op jit(solution)/shard_map/ppermute | solution.py:24
  4.4 14.3 %copy-start.13 = (pred[128,128]{1,0:T(8,128)(4,1)}, pred[128,128]{1,0:T(8,128)(4,1)S(1)}, u32[]{:S(2)}) copy-start(pred[128,128]{1,0:T(8,128)(4,1)S(1)} %get-tuple-element.83) | copy-start | bytes 49156
  7.5 11.2 %copy-start.15 = (f32[4,128]{1,0:T(4,128)}, f32[4,128]{1,0:T(4,128)S(1)}, u32[]{:S(2)}) copy-start(f32[4,128]{1,0:T(4,128)S(1)} %reduce_window_sum.27) | copy-start | bytes 6148
  15.1 11.1 %copy-start.16 = (f32[4,128]{1,0:T(4,128)}, f32[4,128]{1,0:T(4,128)S(1)}, u32[]{:S(2)}) copy-start(f32[4,128]{1,0:T(4,128)S(1)} %get-tuple-element.52) | copy-start | bytes 6148
  31.7 12.4 %collective-permute-start.1 = (f32[128,256]{1,0:T(8,128)}, f32[128,256]{1,0:T(8,128)S(1)}, u32[]{:S(2)}, u32[]{:S(2)}) collective-permute-start(f32[128,256]{1,0:T(8,128)} %get-tuple-element.38), channel_id=1, source_target_pairs={{0,8},{8,16},{16,24},{24,0},{32,40},{40,48},{48,56},{56,32},{64,72... | collective-permute-start | bytes 393224 | tf_op jit(solution)/shard_map/ppermute | solution.py:120
  34.9 10.4 %collective-permute-start.2 = (f32[128,256]{1,0:T(8,128)}, f32[128,256]{1,0:T(8,128)S(1)}, u32[]{:S(2)}, u32[]{:S(2)}) collective-permute-start(f32[128,256]{1,0:T(8,128)} %get-tuple-element.39), channel_id=1, source_target_pairs={{0,16},{8,24},{16,0},{24,8},{32,48},{40,56},{48,32},{56,40},{64,80... | collective-permute-start | bytes 393224 | tf_op jit(solution)/shard_map/ppermute | solution.py:120
  41.2 7.2 %collective-permute-start.3 = (f32[128,256]{1,0:T(8,128)}, f32[128,256]{1,0:T(8,128)}, u32[]{:S(2)}, u32[]{:S(2)}) collective-permute-start(f32[128,256]{1,0:T(8,128)} %get-tuple-element.40), channel_id=1, source_target_pairs={{0,24},{8,0},{16,8},{24,16},{32,56},{40,32},{48,40},{56,48},{64,88... | collective-permute-start | bytes 393224 | tf_op jit(solution)/shard_map/ppermute | solution.py:120
  44.0 8.7 %copy-start.25 = (pred[4]{0:T(512)(128)(4,1)S(1)}, pred[4]{0:T(512)(128)(4,1)}, u32[]{:S(2)}) copy-start(pred[4]{0:T(512)(128)(4,1)} %compare_and_fusion.2) | copy-start | bytes 16
  44.1 16.3 %copy-start.19 = (s32[1280]{0:T(1024)}, s32[1280]{0:T(1024)S(1)}, u32[]{:S(2)}) copy-start(s32[1280]{0:T(1024)S(1)} %fusion.117) | copy-start | bytes 15364
  52.7 6.9 %copy-start.6 = (f32[128,512]{0,1:T(8,128)S(1)}, f32[128,512]{0,1:T(8,128)}, u32[]{:S(2)}) copy-start(f32[128,512]{0,1:T(8,128)} %convert_multiply_fusion) | copy-start | bytes 786436
  57.3 10.7 %collective-permute-start.4 = (f32[128,256]{1,0:T(8,128)}, f32[128,256]{1,0:T(8,128)}, u32[]{:S(2)}, u32[]{:S(2)}) collective-permute-start(f32[128,256]{1,0:T(8,128)} %convolution_add_fusion.5), channel_id=1, source_target_pairs={{0,32},{8,40},{16,48},{24,56},{32,64},{40,72},{48,80},{56,88},{64,... | collective-permute-start | bytes 393224 | tf_op jit(solution)/shard_map/ppermute | solution.py:24
  70.4 7.7 %copy-start.7 = (f32[128,128]{1,0:T(8,128)}, f32[128,128]{1,0:T(8,128)S(1)}, u32[]{:S(2)}) copy-start(f32[128,128]{1,0:T(8,128)S(1)} %convolution_add_fusion.12) | copy-start | bytes 196612
  70.4 7.6 %collective-permute-start.5 = (f32[128,256]{1,0:T(8,128)S(1)}, f32[128,256]{1,0:T(8,128)S(1)}, u32[]{:S(2)}, u32[]{:S(2)}) collective-permute-start(f32[128,256]{1,0:T(8,128)S(1)} %pad_maximum_fusion.4), channel_id=1, source_target_pairs={{0,64},{8,72},{16,80},{24,88},{32,96},{40,104},{48,112},{56,120},{... | collective-permute-start | bytes 393224 | tf_op jit(solution)/shard_map/ppermute | solution.py:24
  80.3 51.4 %copy-start.4 = (f32[4,128,128]{2,1,0:T(8,128)S(1)}, f32[4,128,128]{2,1,0:T(8,128)}, u32[]{:S(2)}) copy-start(f32[4,128,128]{2,1,0:T(8,128)} %convolution_multiply_fusion.3) | copy-start | bytes 786436
  80.3 14.2 %collective-permute-start.6 = (f32[128,256]{1,0:T(8,128)S(1)}, f32[128,256]{1,0:T(8,128)S(1)}, u32[]{:S(2)}, u32[]{:S(2)}) collective-permute-start(f32[128,256]{1,0:T(8,128)S(1)} %pad_maximum_fusion.5), channel_id=1, source_target_pairs={{0,128},{8,136},{16,144},{24,152},{32,160},{40,168},{48,176},{56,1... | collective-permute-start | bytes 393224 | tf_op jit(solution)/shard_map/ppermute | solution.py:24
  94.8 21.8 %collective-permute-start.7 = (f32[128,128]{1,0:T(8,128)S(1)}, f32[128,128]{1,0:T(8,128)S(1)}, u32[]{:S(2)}, u32[]{:S(2)}) collective-permute-start(f32[128,128]{1,0:T(8,128)S(1)} %convolution_add_fusion.10), channel_id=1, source_target_pairs={{0,256},{8,264},{16,272},{24,280},{32,288},{40,296},{48,304},{56,3... | collective-permute-start | bytes 196616 | tf_op jit(solution)/shard_map/ppermute | solution.py:24
  116.8 3.2 collective-permute-start.8
  121.2 11.0 %collective-permute-start.9 = (f32[128,128]{1,0:T(8,128)S(1)}, f32[128,128]{1,0:T(8,128)S(1)}, u32[]{:S(2)}, u32[]{:S(2)}) collective-permute-start(f32[128,128]{1,0:T(8,128)S(1)} %get-tuple-element.46), channel_id=1, source_target_pairs={{0,8},{8,16},{16,24},{24,0},{32,40},{40,48},{48,56},{56,32},{64,72... | collective-permute-start | bytes 196616 | tf_op jit(solution)/shard_map/ppermute | solution.py:120
  123.6 8.6 %collective-permute-start.10 = (f32[128,128]{1,0:T(8,128)S(1)}, f32[128,128]{1,0:T(8,128)S(1)}, u32[]{:S(2)}, u32[]{:S(2)}) collective-permute-start(f32[128,128]{1,0:T(8,128)S(1)} %get-tuple-element.45), channel_id=1, source_target_pairs={{0,16},{8,24},{16,0},{24,8},{32,48},{40,56},{48,32},{56,40},{64,80... | collective-permute-start | bytes 196616 | tf_op jit(solution)/shard_map/ppermute | solution.py:120
  127.1 6.4 %collective-permute-start.11 = (f32[128,128]{1,0:T(8,128)S(1)}, f32[128,128]{1,0:T(8,128)S(1)}, u32[]{:S(2)}, u32[]{:S(2)}) collective-permute-start(f32[128,128]{1,0:T(8,128)S(1)} %get-tuple-element.44), channel_id=1, source_target_pairs={{0,24},{8,0},{16,8},{24,16},{32,56},{40,32},{48,40},{56,48},{64,88... | collective-permute-start | bytes 196616 | tf_op jit(solution)/shard_map/ppermute | solution.py:120
  137.2 15.6 %copy-start.11 = (bf16[128,256]{1,0:T(8,128)(2,1)S(1)}, bf16[128,256]{1,0:T(8,128)(2,1)}, u32[]{:S(2)}) copy-start(bf16[128,256]{1,0:T(8,128)(2,1)} %param.17) | copy-start | bytes 196612
  137.2 15.7 %copy-start.21 = (f32[16,256]{1,0:T(8,128)S(1)}, f32[16,256]{1,0:T(8,128)}, u32[]{:S(2)}) copy-start(f32[16,256]{1,0:T(8,128)} %param.27) | copy-start | bytes 49156
  137.2 15.7 %copy-start.27 = (s32[128]{0:T(128)S(1)}, s32[128]{0:T(128)}, u32[]{:S(2)}) copy-start(s32[128]{0:T(128)} %param.28) | copy-start | bytes 1540
  137.2 28.7 %copy-start.26 = (f32[256]{0:T(256)S(1)}, f32[256]{0:T(256)}, u32[]{:S(2)}) copy-start(f32[256]{0:T(256)} %param.29) | copy-start | bytes 3076
  138.1 14.6 %all-to-all-start = ((bf16[8,128,256]{2,1,0:T(8,128)(2,1)}), bf16[8,128,256]{2,1,0:T(8,128)(2,1)S(1)}, u32[]{:S(2)}, u32[]{:S(2)}) async-start(bf16[8,128,256]{2,1,0:T(8,128)(2,1)} %bitcast.138), calls=%async_computation | async-start | bytes 1048576 | tf_op jit(solution)/shard_map/all_to_all | solution.py:245
  173.1 64.9 %copy-start.5 = (bf16[4,256,512]{2,1,0:T(8,128)(2,1)S(1)}, bf16[4,256,512]{2,1,0:T(8,128)(2,1)}, u32[]{:S(2)}) copy-start(bf16[4,256,512]{2,1,0:T(8,128)(2,1)} %param.32) | copy-start | bytes 3145732
  268.4 15.9 %copy-start.8 = (bf16[4,256,256]{2,1,0:T(8,128)(2,1)S(1)}, bf16[4,256,256]{2,1,0:T(8,128)(2,1)}, u32[]{:S(2)}) copy-start(bf16[4,256,256]{2,1,0:T(8,128)(2,1)} %param.33) | copy-start | bytes 1572868
  284.7 7.9 %copy-start.17 = (s32[128,10]{0,1:T(8,128)S(1)}, s32[128,10]{0,1:T(8,128)}, u32[]{:S(2)}) copy-start(s32[128,10]{0,1:T(8,128)} %param.30) | copy-start | bytes 15364
  284.7 8.1 %copy-start.18 = (f32[128,10]{0,1:T(8,128)S(1)}, f32[128,10]{0,1:T(8,128)}, u32[]{:S(2)}) copy-start(f32[128,10]{0,1:T(8,128)} %param.31) | copy-start | bytes 15364
  284.7 8.2 %copy-start.20 = (s32[1280]{0:T(1024)S(1)}, s32[1280]{0:T(1024)}, u32[]{:S(2)}) copy-start(s32[1280]{0:T(1024)} %copy-done.19) | copy-start | bytes 15364
  286.3 49.6 %all-to-all-start.4 = ((bf16[64,6,4,256]{3,2,1,0:T(4,128)(2,1)}), bf16[64,6,4,256]{3,2,1,0:T(4,128)(2,1)}, u32[]{:S(2)}, u32[]{:S(2)}) async-start(bf16[64,6,4,256]{3,2,1,0:T(4,128)(2,1)} %bitcast.51), calls=%async_computation.4 | async-start | bytes 1572864 | tf_op jit(solution)/shard_map/all_to_all | solution.py:312
  (10 other events, 19.5 us)

commit v8 on v7

--- a/solution.py
+++ b/solution.py
@@ -12,6 +12,7 @@
 DV = 128
 KCONV = 4
 STRETCH = 128
+SCAN_RADIX = 4
 
 
 EPS = 1e-06
@@ -149,21 +150,22 @@
         prefixes.append(compose(maps[member], prefixes[-1]) if member else maps[0])
     total = prefixes.pop()
     groups = count // group
-    mapping, shift = total[:, :DK], total[:, DK:]
-    step = 1
-    while step < groups:
-        if 2 * step >= groups:
-            shift_in = passed_along(shift, "seq", step * group)
-            shift = jnp.dot(mapping, shift_in, precision=EXACT_ARITHMETIC) + shift
-        else:
-            both_in = passed_along(jnp.concatenate([mapping, shift], axis=1), "seq", step * group)
-            map_in, shift_in = both_in[:, :DK], both_in[:, DK:]
-            shift = jnp.dot(mapping, shift_in, precision=EXACT_ARITHMETIC) + shift
-            mapping = jnp.dot(mapping, map_in, precision=EXACT_ARITHMETIC)
-        step *= 2
-    start_state = passed_along(shift, "seq", group) + (position < group).astype(
-        jnp.float32
-    ) * lax.dynamic_index_in_dim(init_state, place, 0, keepdims=False)
+    inclusive = total
+    exclusive = None
+    span = 1
+    while span < groups:
+        for hop in range(1, SCAN_RADIX):
+            if span * hop < groups:
+                part = passed_along(inclusive, "seq", span * hop * group)
+                exclusive = part if exclusive is None else compose(exclusive, part)
+        span *= SCAN_RADIX
+        if span < groups:
+            inclusive = compose(total, exclusive)
+    start_state = jnp.where(
+        position < group,
+        lax.dynamic_index_in_dim(init_state, place, 0, keepdims=False),
+        exclusive[:, DK:],
+    )
     prefixes = jnp.stack(prefixes)
     entering = (
         jnp.einsum("pij,jk->pik", prefixes[:, :, :DK], start_state, precision=EXACT_ARITHMETIC)
@@ -253,9 +255,15 @@
     steered = hidden + jnp.dot(
         steer_onehot, steer_table, precision=EXACT_ARITHMETIC, preferred_element_type=jnp.float32
     )
-    sum_hidden, sum_steered = lax.psum(
-        (jnp.sum(hidden * hidden, axis=1), jnp.sum(steered * steered, axis=1)), "head"
-    )
+    row_sums = jnp.stack([jnp.sum(hidden * hidden, axis=1), jnp.sum(steered * steered, axis=1)])
+    row_sums = lax.all_to_all(
+        jnp.broadcast_to(row_sums[None], (head_count,) + row_sums.shape),
+        "head",
+        split_axis=0,
+        concat_axis=0,
+        tiled=True,
+    )
+    sum_hidden, sum_steered = jnp.sum(row_sums, axis=0)
     rescaled = steered * jnp.sqrt((sum_hidden / D + EPS) / (sum_steered / D + EPS))[:, None]
     normed = (post_norm_weight * steered * lax.rsqrt(sum_steered / D + EPS)[:, None]).astype(
         jnp.bfloat16

time: 347 us -> 330 us (0.951)
  blocking collectives: 117 us -> 96.4 us
  waiting for transfers between devices: 62.2 us -> 75.2 us
  matrix products: 26.5 us -> 18.8 us
    ppermute x6 -> x7, waiting for transfers between devices: 3.6 us -> 16.9 us  [passed_along(): lax.ppermute(value, axis, [(source, source + steps) for source in range(f...]
    psum x1 -> x0, blocking collectives: 12.7 us -> none  [local(): lax.psum((jnp.sum(hidden * hidden, axis=1), jnp.sum(steered * steered, ax...]
    all_to_all x1, blocking collectives: 64.2 us -> 56.4 us  [local(): lax.all_to_all(outgoing, 'seq', split_axis=0, concat_axis=0, tiled=True)]
    all_to_all x1, waiting for transfers between devices: 10.1 us -> 5.02 us  [local(): lax.all_to_all(jnp.transpose(blocks, (1, 0, 2)), 'head', split_axis=0, co...]
    all_to_all x0 -> x1, waiting for transfers between devices: none -> 5.04 us  [local(): lax.all_to_all(jnp.broadcast_to(row_sums[None], (head_count,) + row_sums....]
    dot_general x7 -> x0, matrix products: 4.49 us -> none  [the longest x4 2.76 us: entering_state(): shift = jnp.dot(mapping, shift_in, precision=EXACT_ARITHMETIC) + shift]
    ppermute x6 -> x7, starting transfers between devices: 43.4 us -> 42.6 us  [passed_along(): lax.ppermute(value, axis, [(source, source + steps) for source in range(f...]
  transfers between devices with their start and end apart: 14 -> 16, of which waited for: 8 -> 9; matrix products, arithmetic and copies ran while one was open for 8% -> 7% of each run, Pallas kernels for 0% -> 0%
where the time goes in v8:
time: 330 us; the launch traced here: 329 us
  blocking collectives  96.4 us (29%)
  starting transfers between devices  77.5 us (23%)
  waiting for transfers between devices  75.2 us (23%)
  local copies, waits for them, and re-layouts  43 us (13%)
  matrix products  18.8 us (6%)
  other arithmetic  16.7 us (5%)
    all_to_all x1, blocking collectives, local(): lax.all_to_all(outgoing, 'seq', split_axis=0, concat_axis=0, tiled=True)  56.4 us
    all_to_all x1, waiting for transfers between devices, local(): lax.all_to_all(results.reshape(seq_size, capacity, experts_here, -1), 'se...  43 us
    ppermute x7, starting transfers between devices, passed_along(): lax.ppermute(value, axis, [(source, source + steps) for source in range(f...  42.6 us
    all_to_all x1, blocking collectives, local(): lax.all_to_all(jnp.transpose(pieces, (3, 0, 1, 2, 4)), 'head', split_axis...  24.2 us
    ppermute x6, starting transfers between devices, within_group(): return lax.ppermute(value, 'seq', pairs)  21.1 us
    ppermute x7, waiting for transfers between devices, passed_along(): lax.ppermute(value, axis, [(source, source + steps) for source in range(f...  16.9 us
    all_to_all x1, blocking collectives, local(): lax.all_to_all(jnp.broadcast_to(activated_slice[None], (head_count,) + ac...  15.7 us
    gather x2, local copies, waits for them, and re-layouts, local(): jnp.take(padded_rows, source, axis=0)  7.04 us
  transfers between devices with their start and end apart: 16, of which 9 were waited for; matrix products, arithmetic and copies ran while one was open for 7% of the time, Pallas kernels for 0%

profile of v8, /device:TPU:8, one launch (start us, length us, event | category | flops | bytes accessed | tf_op | source)
XLA Modules:
  0.0 328.9 jit_solution(2471517688657650484)
XLA Ops:
  0.9 3.5 %collective-permute-start = (bf16[3,1024]{1,0:T(4,128)(2,1)S(1)}, bf16[3,1024]{1,0:T(4,128)(2,1)S(1)}, u32[]{:S(2)}, u32[]{:S(2)}) collective-permute-start(bf16[3,1024]{1,0:T(4,128)(2,1)S(1)} %slice.143), channel_id=1, source_target_pairs={{0,8},{8,16},{16,24},{24,32},{32,40},{40,48},{48,56},{56,64},{64,7... | collective-permute-start | bytes 18440 | tf_op jit(solution)/shard_map/ppermute | solution.py:25
  12.6 1.8 broadcast_add_fusion
  34.4 3.2 collective-permute-start.1
  37.6 6.5 %collective-permute-start.2 = (f32[128,256]{1,0:T(8,128)}, f32[128,256]{1,0:T(8,128)}, u32[]{:S(2)}, u32[]{:S(2)}) collective-permute-start(f32[128,256]{1,0:T(8,128)} %get-tuple-element.37), channel_id=1, source_target_pairs={{0,16},{8,24},{16,0},{24,8},{32,48},{40,56},{48,32},{56,40},{64,80... | collective-permute-start | bytes 393224 | tf_op jit(solution)/shard_map/ppermute | solution.py:121
  44.0 1.9 collective-permute-start.3
  48.1 3.1 collective-permute-done.3
  51.2 1.9 pad_maximum_fusion.1
  53.1 2.5 gather_fusion
  59.3 5.5 %collective-permute-start.5 = (f32[128,256]{1,0:T(8,128)S(1)}, f32[128,256]{1,0:T(8,128)S(1)}, u32[]{:S(2)}, u32[]{:S(2)}) collective-permute-start(f32[128,256]{1,0:T(8,128)S(1)} %convolution_add_fusion.10), channel_id=1, source_target_pairs={{0,64},{8,72},{16,80},{24,88},{32,96},{40,104},{48,112},{56,120},{... | collective-permute-start | bytes 393224 | tf_op jit(solution)/shard_map/ppermute | solution.py:25
  65.2 7.5 %collective-permute-start.6 = (f32[128,256]{1,0:T(8,128)S(1)}, f32[128,256]{1,0:T(8,128)S(1)}, u32[]{:S(2)}, u32[]{:S(2)}) collective-permute-start(f32[128,256]{1,0:T(8,128)S(1)} %convolution_add_fusion.10), channel_id=1, source_target_pairs={{0,96},{8,104},{16,112},{24,120},{32,128},{40,136},{48,144},{56,15... | collective-permute-start | bytes 393224 | tf_op jit(solution)/shard_map/ppermute | solution.py:25
  73.0 2.2 collective-permute-done.6
  75.7 10.2 %collective-permute-start.7 = (f32[128,256]{1,0:T(8,128)S(1)}, f32[128,256]{1,0:T(8,128)S(1)}, u32[]{:S(2)}, u32[]{:S(2)}) collective-permute-start(f32[128,256]{1,0:T(8,128)S(1)} %convolution_add_fusion.7), channel_id=1, source_target_pairs={{0,128},{8,136},{16,144},{24,152},{32,160},{40,168},{48,176},{56,1... | collective-permute-start | bytes 393224 | tf_op jit(solution)/shard_map/ppermute | solution.py:25
  86.6 13.1 %collective-permute-start.8 = (f32[128,256]{1,0:T(8,128)S(1)}, f32[128,256]{1,0:T(8,128)S(1)}, u32[]{:S(2)}, u32[]{:S(2)}) collective-permute-start(f32[128,256]{1,0:T(8,128)S(1)} %convolution_add_fusion.7), channel_id=1, source_target_pairs={{0,256},{8,264},{16,272},{24,280},{32,288},{40,296},{48,304},{56,3... | collective-permute-start | bytes 393224 | tf_op jit(solution)/shard_map/ppermute | solution.py:25
  102.5 13.9 %collective-permute-done.9 = f32[128,256]{1,0:T(8,128)S(1)} collective-permute-done((f32[128,256]{1,0:T(8,128)S(1)}, f32[128,256]{1,0:T(8,128)S(1)}, u32[]{:S(2)}, u32[]{:S(2)}) %collective-permute-start.9) | collective-permute-done | bytes 131104 | tf_op jit(solution)/shard_map/ppermute | solution.py:25
  117.9 3.3 %collective-permute-start.10 = (f32[128,128]{1,0:T(8,128)S(1)}, f32[128,128]{1,0:T(8,128)S(1)}, u32[]{:S(2)}, u32[]{:S(2)}) collective-permute-start(f32[128,128]{1,0:T(8,128)S(1)} %get-tuple-element.44), channel_id=1, source_target_pairs={{0,8},{8,16},{16,24},{24,0},{32,40},{40,48},{48,56},{56,32},{64,72... | collective-permute-start | bytes 196616 | tf_op jit(solution)/shard_map/ppermute | solution.py:121
  121.3 2.7 collective-permute-start.11
  124.0 3.5 %collective-permute-start.12 = (f32[128,128]{1,0:T(8,128)S(1)}, f32[128,128]{1,0:T(8,128)S(1)}, u32[]{:S(2)}, u32[]{:S(2)}) collective-permute-start(f32[128,128]{1,0:T(8,128)S(1)} %get-tuple-element.42), channel_id=1, source_target_pairs={{0,24},{8,0},{16,8},{24,16},{32,56},{40,32},{48,40},{56,48},{64,88... | collective-permute-start | bytes 196616 | tf_op jit(solution)/shard_map/ppermute | solution.py:121
  133.1 4.3 %all-to-all-start = ((bf16[8,128,256]{2,1,0:T(8,128)(2,1)}), bf16[8,128,256]{2,1,0:T(8,128)(2,1)S(1)}, u32[]{:S(2)}, u32[]{:S(2)}) async-start(bf16[8,128,256]{2,1,0:T(8,128)(2,1)} %bitcast.144), calls=%async_computation | async-start | bytes 1048576 | tf_op jit(solution)/shard_map/all_to_all | solution.py:247
  137.4 5.2 %scatter_custom_fusion = s32[1536]{0:T(1024)S(1)} fusion(s32[1280]{0:T(1024)S(1)} %fusion.116, s32[1280]{0:T(1024)S(1)} %add_select_fusion, s32[]{:T(128)} %constant.515.clone.1), kind=kCustom, calls=%fused_computation.233 | custom fusion | bytes 6148 | tf_op jit(solution)/shard_map/scatter | solution.py:288
  142.7 5.0 %all-to-all-done = bf16[8,128,256]{2,1,0:T(8,128)(2,1)S(1)} async-done(((bf16[8,128,256]{2,1,0:T(8,128)(2,1)}), bf16[8,128,256]{2,1,0:T(8,128)(2,1)S(1)}, u32[]{:S(2)}, u32[]{:S(2)}) %all-to-all-start) | async-done | bytes 524320 | tf_op jit(solution)/shard_map/all_to_all | solution.py:247
  148.9 3.3 %all-to-all-start.1 = ((f32[8,2,128]{2,1,0:T(2,128)}), f32[8,2,128]{2,1,0:T(2,128)S(1)}, u32[]{:S(2)}, u32[]{:S(2)}) async-start(f32[8,2,128]{2,1,0:T(2,128)} %broadcast_in_dim.215), calls=%async_computation.1 | async-start | bytes 16384 | tf_op jit(solution)/shard_map/all_to_all | solution.py:259
  152.4 5.0 %all-to-all-done.1 = f32[8,2,128]{2,1,0:T(2,128)S(1)} async-done(((f32[8,2,128]{2,1,0:T(2,128)}), f32[8,2,128]{2,1,0:T(2,128)S(1)}, u32[]{:S(2)}, u32[]{:S(2)}) %all-to-all-start.1) | async-done | bytes 8224 | tf_op jit(solution)/shard_map/all_to_all | solution.py:259
  157.6 5.4 %gather_fusion.2 = bf16[1536,256]{1,0:T(8,128)(2,1)} fusion(bf16[129,256]{1,0:T(8,128)(2,1)S(1)} %concatenate.59, s32[2048]{0:T(1024)S(1)} %pad_clamp_fusion.1), kind=kCustom, calls=%fused_computation.2 | custom fusion | bytes 1579008 | tf_op jit(solution)/shard_map/jit(_take)/gather | solution.py:291
  163.0 1.7 gather.23
  165.4 56.4 %all_to_all.30 = bf16[64,6,4,256]{3,2,1,0:T(4,128)(2,1)S(1)} all-to-all(bf16[64,6,4,256]{3,2,1,0:T(4,128)(2,1)S(1)} %broadcast_select_fusion), channel_id=1, replica_groups=mesh['seq'=64,'head'=8] {'seq'}, dimensions={0} | all-to-all | bytes 1572864 | tf_op jit(solution)/shard_map/all_to_all | solution.py:292
  221.8 1.7 fusion.2
  223.5 2.6 copy.180
  227.8 24.2 %all_to_all.31 = bf16[8,384,4,2,32]{1,4,3,2,0:T(8,128)(2,1)S(1)} all-to-all(bf16[8,384,4,2,32]{1,4,3,2,0:T(8,128)(2,1)S(1)} %copy.181), channel_id=1, replica_groups=mesh['seq'=64,'head'=8] {'head'}, dimensions={0} | all-to-all | bytes 3145728 | tf_op jit(solution)/shard_map/all_to_all | solution.py:302
  252.4 15.7 %all_to_all.32 = bf16[8,384,4,32]{1,3,2,0:T(8,128)(2,1)S(1)} all-to-all(bf16[8,384,4,32]{1,3,2,0:T(8,128)(2,1)S(1)} %broadcast_in_dim.222), channel_id=1, replica_groups=mesh['seq'=64,'head'=8] {'head'}, dimensions={0} | all-to-all | bytes 1572864 | tf_op jit(solution)/shard_map/all_to_all | solution.py:309
  270.2 6.1 %all-to-all-start.5 = ((bf16[64,6,4,256]{3,2,1,0:T(4,128)(2,1)}), bf16[64,6,4,256]{3,2,1,0:T(4,128)(2,1)}, u32[]{:S(2)}, u32[]{:S(2)}) async-start(bf16[64,6,4,256]{3,2,1,0:T(4,128)(2,1)} %bitcast.55), calls=%async_computation.5 | async-start | bytes 1572864 | tf_op jit(solution)/shard_map/all_to_all | solution.py:320
  276.9 43.0 %all-to-all-done.5 = bf16[64,6,4,256]{3,2,1,0:T(4,128)(2,1)} async-done(((bf16[64,6,4,256]{3,2,1,0:T(4,128)(2,1)}), bf16[64,6,4,256]{3,2,1,0:T(4,128)(2,1)}, u32[]{:S(2)}, u32[]{:S(2)}) %all-to-all-start.5) | async-done | bytes 786464 | tf_op jit(solution)/shard_map/all_to_all | solution.py:320
  321.4 4.7 %gather_fusion.3 = bf16[1280,256]{1,0:T(8,128)(2,1)} fusion(bf16[1536,256]{1,0:T(8,128)(2,1)S(1)} %reshape.1161, s32[2048]{0:T(1024)S(1)} %pad_clamp_fusion), kind=kCustom, calls=%fused_computation.3 | custom fusion | bytes 1315840 | tf_op jit(solution)/shard_map/jit(_take)/gather | solution.py:329
  (214 shorter events, 56.8 us)
Async XLA Ops:
  0.0 131.7 %copy-start = (bf16[512,2048]{1,0:T(8,128)(2,1)S(1)}, bf16[512,2048]{1,0:T(8,128)(2,1)}, u32[]{:S(2)}) copy-start(bf16[512,2048]{1,0:T(8,128)(2,1)} %param.26) | copy-start | bytes 6291460
  0.9 18.8 %collective-permute-start = (bf16[3,1024]{1,0:T(4,128)(2,1)S(1)}, bf16[3,1024]{1,0:T(4,128)(2,1)S(1)}, u32[]{:S(2)}, u32[]{:S(2)}) collective-permute-start(bf16[3,1024]{1,0:T(4,128)(2,1)S(1)} %slice.143), channel_id=1, source_target_pairs={{0,8},{8,16},{16,24},{24,32},{32,40},{40,48},{48,56},{56,64},{64,7... | collective-permute-start | bytes 18440 | tf_op jit(solution)/shard_map/ppermute | solution.py:25
  14.4 5.2 %copy-start.8 = (bf16[128,1024]{1,0:T(8,128)(2,1)S(1)}, bf16[128,1024]{1,0:T(8,128)(2,1)}, u32[]{:S(2)}) copy-start(bf16[128,1024]{1,0:T(8,128)(2,1)} %param.18) | copy-start | bytes 786436
  14.4 5.3 %copy-start.19 = (bf16[3,1024]{1,0:T(4,128)(2,1)S(1)}, bf16[3,1024]{1,0:T(4,128)(2,1)}, u32[]{:S(2)}) copy-start(bf16[3,1024]{1,0:T(4,128)(2,1)} %param.20) | copy-start | bytes 18436
  16.3 5.4 %copy-start.17 = (f32[4,128]{1,0:T(4,128)}, f32[4,128]{1,0:T(4,128)S(1)}, u32[]{:S(2)}) copy-start(f32[4,128]{1,0:T(4,128)S(1)} %get-tuple-element.79) | copy-start | bytes 6148
  32.5 13.7 %copy-start.3 = (f32[128,512]{0,1:T(8,128)S(1)}, f32[128,512]{0,1:T(8,128)}, u32[]{:S(2)}) copy-start(f32[128,512]{0,1:T(8,128)} %convert_multiply_fusion) | copy-start | bytes 786436
  34.4 13.7 %collective-permute-start.1 = (f32[128,256]{1,0:T(8,128)}, f32[128,256]{1,0:T(8,128)}, u32[]{:S(2)}, u32[]{:S(2)}) collective-permute-start(f32[128,256]{1,0:T(8,128)} %get-tuple-element.36), channel_id=1, source_target_pairs={{0,8},{8,16},{16,24},{24,0},{32,40},{40,48},{48,56},{56,32},{64,72... | collective-permute-start | bytes 393224 | tf_op jit(solution)/shard_map/ppermute | solution.py:121
  37.6 10.5 %collective-permute-start.2 = (f32[128,256]{1,0:T(8,128)}, f32[128,256]{1,0:T(8,128)}, u32[]{:S(2)}, u32[]{:S(2)}) collective-permute-start(f32[128,256]{1,0:T(8,128)} %get-tuple-element.37), channel_id=1, source_target_pairs={{0,16},{8,24},{16,0},{24,8},{32,48},{40,56},{48,32},{56,40},{64,80... | collective-permute-start | bytes 393224 | tf_op jit(solution)/shard_map/ppermute | solution.py:121
  44.0 7.2 %collective-permute-start.3 = (f32[128,256]{1,0:T(8,128)}, f32[128,256]{1,0:T(8,128)}, u32[]{:S(2)}, u32[]{:S(2)}) collective-permute-start(f32[128,256]{1,0:T(8,128)} %get-tuple-element.38), channel_id=1, source_target_pairs={{0,24},{8,0},{16,8},{24,16},{32,56},{40,32},{48,40},{56,48},{64,88... | collective-permute-start | bytes 393224 | tf_op jit(solution)/shard_map/ppermute | solution.py:121
  57.4 29.1 %copy-start.6 = (f32[1,128,256]{2,1,0:T(8,128)S(1)}, f32[1,128,256]{2,1,0:T(8,128)}, u32[]{:S(2)}) copy-start(f32[1,128,256]{2,1,0:T(8,128)} %pad_bitcast_fusion) | copy-start | bytes 393220
  57.7 15.0 %collective-permute-start.4 = (f32[128,256]{1,0:T(8,128)S(1)}, f32[128,256]{1,0:T(8,128)S(1)}, u32[]{:S(2)}, u32[]{:S(2)}) collective-permute-start(f32[128,256]{1,0:T(8,128)S(1)} %convolution_add_fusion.10), channel_id=1, source_target_pairs={{0,32},{8,40},{16,48},{24,56},{32,64},{40,72},{48,80},{56,88},{64,... | collective-permute-start | bytes 393224 | tf_op jit(solution)/shard_map/ppermute | solution.py:25
  59.3 13.4 %collective-permute-start.5 = (f32[128,256]{1,0:T(8,128)S(1)}, f32[128,256]{1,0:T(8,128)S(1)}, u32[]{:S(2)}, u32[]{:S(2)}) collective-permute-start(f32[128,256]{1,0:T(8,128)S(1)} %convolution_add_fusion.10), channel_id=1, source_target_pairs={{0,64},{8,72},{16,80},{24,88},{32,96},{40,104},{48,112},{56,120},{... | collective-permute-start | bytes 393224 | tf_op jit(solution)/shard_map/ppermute | solution.py:25
  65.2 10.0 %collective-permute-start.6 = (f32[128,256]{1,0:T(8,128)S(1)}, f32[128,256]{1,0:T(8,128)S(1)}, u32[]{:S(2)}, u32[]{:S(2)}) collective-permute-start(f32[128,256]{1,0:T(8,128)S(1)} %convolution_add_fusion.10), channel_id=1, source_target_pairs={{0,96},{8,104},{16,112},{24,120},{32,128},{40,136},{48,144},{56,15... | collective-permute-start | bytes 393224 | tf_op jit(solution)/shard_map/ppermute | solution.py:25
  75.7 25.3 %collective-permute-start.7 = (f32[128,256]{1,0:T(8,128)S(1)}, f32[128,256]{1,0:T(8,128)S(1)}, u32[]{:S(2)}, u32[]{:S(2)}) collective-permute-start(f32[128,256]{1,0:T(8,128)S(1)} %convolution_add_fusion.7), channel_id=1, source_target_pairs={{0,128},{8,136},{16,144},{24,152},{32,160},{40,168},{48,176},{56,1... | collective-permute-start | bytes 393224 | tf_op jit(solution)/shard_map/ppermute | solution.py:25
  86.6 15.6 %collective-permute-start.8 = (f32[128,256]{1,0:T(8,128)S(1)}, f32[128,256]{1,0:T(8,128)S(1)}, u32[]{:S(2)}, u32[]{:S(2)}) collective-permute-start(f32[128,256]{1,0:T(8,128)S(1)} %convolution_add_fusion.7), channel_id=1, source_target_pairs={{0,256},{8,264},{16,272},{24,280},{32,288},{40,296},{48,304},{56,3... | collective-permute-start | bytes 393224 | tf_op jit(solution)/shard_map/ppermute | solution.py:25
  99.7 16.6 %collective-permute-start.9 = (f32[128,256]{1,0:T(8,128)S(1)}, f32[128,256]{1,0:T(8,128)S(1)}, u32[]{:S(2)}, u32[]{:S(2)}) collective-permute-start(f32[128,256]{1,0:T(8,128)S(1)} %convolution_add_fusion.7), channel_id=1, source_target_pairs={{0,384},{8,392},{16,400},{24,408},{32,416},{40,424},{48,432},{56,4... | collective-permute-start | bytes 393224 | tf_op jit(solution)/shard_map/ppermute | solution.py:25
  117.9 13.6 %copy-start.4 = (f32[128,4,128]{2,0,1:T(8,128)S(1)}, f32[128,4,128]{2,0,1:T(8,128)}, u32[]{:S(2)}) copy-start(f32[128,4,128]{2,0,1:T(8,128)} %copy.168) | copy-start | bytes 786436
  117.9 13.6 %copy-start.24 = (f32[128]{0:T(128)S(1)}, f32[128]{0:T(128)}, u32[]{:S(2)}) copy-start(f32[128]{0:T(128)} %param.25) | copy-start | bytes 1540
  117.9 10.2 %collective-permute-start.10 = (f32[128,128]{1,0:T(8,128)S(1)}, f32[128,128]{1,0:T(8,128)S(1)}, u32[]{:S(2)}, u32[]{:S(2)}) collective-permute-start(f32[128,128]{1,0:T(8,128)S(1)} %get-tuple-element.44), channel_id=1, source_target_pairs={{0,8},{8,16},{16,24},{24,0},{32,40},{40,48},{48,56},{56,32},{64,72... | collective-permute-start | bytes 196616 | tf_op jit(solution)/shard_map/ppermute | solution.py:121
  121.3 7.8 %collective-permute-start.11 = (f32[128,128]{1,0:T(8,128)S(1)}, f32[128,128]{1,0:T(8,128)S(1)}, u32[]{:S(2)}, u32[]{:S(2)}) collective-permute-start(f32[128,128]{1,0:T(8,128)S(1)} %get-tuple-element.43), channel_id=1, source_target_pairs={{0,16},{8,24},{16,0},{24,8},{32,48},{40,56},{48,32},{56,40},{64,80... | collective-permute-start | bytes 196616 | tf_op jit(solution)/shard_map/ppermute | solution.py:121
  124.0 6.2 %collective-permute-start.12 = (f32[128,128]{1,0:T(8,128)S(1)}, f32[128,128]{1,0:T(8,128)S(1)}, u32[]{:S(2)}, u32[]{:S(2)}) collective-permute-start(f32[128,128]{1,0:T(8,128)S(1)} %get-tuple-element.42), channel_id=1, source_target_pairs={{0,24},{8,0},{16,8},{24,16},{32,56},{40,32},{48,40},{56,48},{64,88... | collective-permute-start | bytes 196616 | tf_op jit(solution)/shard_map/ppermute | solution.py:121
  131.8 16.0 %copy-start.9 = (bf16[128,256]{1,0:T(8,128)(2,1)S(1)}, bf16[128,256]{1,0:T(8,128)(2,1)}, u32[]{:S(2)}) copy-start(bf16[128,256]{1,0:T(8,128)(2,1)} %param.17) | copy-start | bytes 196612
  132.2 15.7 %copy-start.15 = (f32[16,256]{1,0:T(8,128)S(1)}, f32[16,256]{1,0:T(8,128)}, u32[]{:S(2)}) copy-start(f32[16,256]{1,0:T(8,128)} %param.27) | copy-start | bytes 49156
  132.3 15.7 %copy-start.23 = (s32[128]{0:T(128)S(1)}, s32[128]{0:T(128)}, u32[]{:S(2)}) copy-start(s32[128]{0:T(128)} %param.28) | copy-start | bytes 1540
  132.3 25.2 %copy-start.22 = (f32[256]{0:T(256)S(1)}, f32[256]{0:T(256)}, u32[]{:S(2)}) copy-start(f32[256]{0:T(256)} %param.29) | copy-start | bytes 3076
  133.1 14.6 %all-to-all-start = ((bf16[8,128,256]{2,1,0:T(8,128)(2,1)}), bf16[8,128,256]{2,1,0:T(8,128)(2,1)S(1)}, u32[]{:S(2)}, u32[]{:S(2)}) async-start(bf16[8,128,256]{2,1,0:T(8,128)(2,1)} %bitcast.144), calls=%async_computation | async-start | bytes 1048576 | tf_op jit(solution)/shard_map/all_to_all | solution.py:247
  148.9 8.6 %all-to-all-start.1 = ((f32[8,2,128]{2,1,0:T(2,128)}), f32[8,2,128]{2,1,0:T(2,128)S(1)}, u32[]{:S(2)}, u32[]{:S(2)}) async-start(f32[8,2,128]{2,1,0:T(2,128)} %broadcast_in_dim.215), calls=%async_computation.1 | async-start | bytes 16384 | tf_op jit(solution)/shard_map/all_to_all | solution.py:259
  164.7 57.1 %copy-start.2 = (bf16[4,256,512]{2,1,0:T(8,128)(2,1)S(1)}, bf16[4,256,512]{2,1,0:T(8,128)(2,1)}, u32[]{:S(2)}) copy-start(bf16[4,256,512]{2,1,0:T(8,128)(2,1)} %param.32) | copy-start | bytes 3145732
  252.3 15.9 %copy-start.5 = (bf16[4,256,256]{2,1,0:T(8,128)(2,1)S(1)}, bf16[4,256,256]{2,1,0:T(8,128)(2,1)}, u32[]{:S(2)}) copy-start(bf16[4,256,256]{2,1,0:T(8,128)(2,1)} %param.33) | copy-start | bytes 1572868
  268.7 7.9 %copy-start.13 = (s32[128,10]{0,1:T(8,128)S(1)}, s32[128,10]{0,1:T(8,128)}, u32[]{:S(2)}) copy-start(s32[128,10]{0,1:T(8,128)} %param.30) | copy-start | bytes 15364
  268.7 8.1 %copy-start.14 = (f32[128,10]{0,1:T(8,128)S(1)}, f32[128,10]{0,1:T(8,128)}, u32[]{:S(2)}) copy-start(f32[128,10]{0,1:T(8,128)} %param.31) | copy-start | bytes 15364
  270.2 49.6 %all-to-all-start.5 = ((bf16[64,6,4,256]{3,2,1,0:T(4,128)(2,1)}), bf16[64,6,4,256]{3,2,1,0:T(4,128)(2,1)}, u32[]{:S(2)}, u32[]{:S(2)}) async-start(bf16[64,6,4,256]{3,2,1,0:T(4,128)(2,1)} %bitcast.55), calls=%async_computation.5 | async-start | bytes 1572864 | tf_op jit(solution)/shard_map/all_to_all | solution.py:320
  (9 other events, 22.9 us)

commit v9 on v8

--- a/solution.py
+++ b/solution.py
@@ -12,6 +12,7 @@
 DV = 128
 KCONV = 4
 STRETCH = 128
+LINK = jnp.bfloat16
 SCAN_RADIX = 4
 
 
@@ -156,7 +157,8 @@
     while span < groups:
         for hop in range(1, SCAN_RADIX):
             if span * hop < groups:
-                part = passed_along(inclusive, "seq", span * hop * group)
+                part = passed_along(inclusive.astype(LINK), "seq", span * hop * group)
+                part = part.astype(jnp.float32)
                 exclusive = part if exclusive is None else compose(exclusive, part)
         span *= SCAN_RADIX
         if span < groups:

time: 330 us -> 310 us (0.939)
  waiting for transfers between devices: 75.2 us -> 64.8 us
  starting transfers between devices: 77.5 us -> 72.3 us
  other arithmetic: 16.7 us -> 11.8 us
    ppermute x7, waiting for transfers between devices: 16.9 us -> 5.66 us  [passed_along(): lax.ppermute(value, axis, [(source, source + steps) for source in range(f...]
    ppermute x7, starting transfers between devices: 42.6 us -> 37.2 us  [passed_along(): lax.ppermute(value, axis, [(source, source + steps) for source in range(f...]
where the time goes in v9:
time: 310 us; the launch traced here: 309 us
  blocking collectives  97 us (31%)
  starting transfers between devices  72.3 us (23%)
  waiting for transfers between devices  64.8 us (21%)
  local copies, waits for them, and re-layouts  41.9 us (14%)
  matrix products  19.3 us (6%)
  other arithmetic  11.8 us (4%)
    all_to_all x1, blocking collectives, local(): lax.all_to_all(outgoing, 'seq', split_axis=0, concat_axis=0, tiled=True)  57.3 us
    all_to_all x1, waiting for transfers between devices, local(): lax.all_to_all(results.reshape(seq_size, capacity, experts_here, -1), 'se...  43 us
    ppermute x7, starting transfers between devices, passed_along(): lax.ppermute(value, axis, [(source, source + steps) for source in range(f...  37.2 us
    all_to_all x1, blocking collectives, local(): lax.all_to_all(jnp.transpose(pieces, (3, 0, 1, 2, 4)), 'head', split_axis...  24 us
    ppermute x6, starting transfers between devices, within_group(): return lax.ppermute(value, 'seq', pairs)  21.4 us
    all_to_all x1, blocking collectives, local(): lax.all_to_all(jnp.broadcast_to(activated_slice[None], (head_count,) + ac...  15.7 us
    gather x2, local copies, waits for them, and re-layouts, local(): jnp.take(padded_rows, source, axis=0)  7.05 us
  transfers between devices with their start and end apart: 16, of which 9 were waited for; matrix products, arithmetic and copies ran while one was open for 7% of the time, Pallas kernels for 0%

profile of v9, /device:TPU:8, one launch (start us, length us, event | category | flops | bytes accessed | tf_op | source)
XLA Modules:
  0.0 308.6 jit_solution(16648075686301965196)
XLA Ops:
  0.9 3.5 %collective-permute-start = (bf16[3,1024]{1,0:T(4,128)(2,1)S(1)}, bf16[3,1024]{1,0:T(4,128)(2,1)S(1)}, u32[]{:S(2)}, u32[]{:S(2)}) collective-permute-start(bf16[3,1024]{1,0:T(4,128)(2,1)S(1)} %slice.144), channel_id=1, source_target_pairs={{0,8},{8,16},{16,24},{24,32},{32,40},{40,48},{48,56},{56,64},{64,7... | collective-permute-start | bytes 18440 | tf_op jit(solution)/shard_map/ppermute | solution.py:26
  12.4 1.8 broadcast_add_fusion
  32.0 3.2 %collective-permute-start.1 = (f32[128,256]{1,0:T(8,128)S(1)}, f32[128,256]{1,0:T(8,128)S(1)}, u32[]{:S(2)}, u32[]{:S(2)}) collective-permute-start(f32[128,256]{1,0:T(8,128)S(1)} %get-tuple-element.36), channel_id=1, source_target_pairs={{0,8},{8,16},{16,24},{24,0},{32,40},{40,48},{48,56},{56,32},{64,72... | collective-permute-start | bytes 393224 | tf_op jit(solution)/shard_map/ppermute | solution.py:122
  35.1 6.3 %collective-permute-start.2 = (f32[128,256]{1,0:T(8,128)S(1)}, f32[128,256]{1,0:T(8,128)S(1)}, u32[]{:S(2)}, u32[]{:S(2)}) collective-permute-start(f32[128,256]{1,0:T(8,128)S(1)} %get-tuple-element.37), channel_id=1, source_target_pairs={{0,16},{8,24},{16,0},{24,8},{32,48},{40,56},{48,32},{56,40},{64,80... | collective-permute-start | bytes 393224 | tf_op jit(solution)/shard_map/ppermute | solution.py:122
  41.5 1.9 collective-permute-start.3
  45.2 3.2 %collective-permute-done.3 = f32[128,256]{1,0:T(8,128)S(1)} collective-permute-done((f32[128,256]{1,0:T(8,128)S(1)}, f32[128,256]{1,0:T(8,128)S(1)}, u32[]{:S(2)}, u32[]{:S(2)}) %collective-permute-start.3) | collective-permute-done | bytes 131104 | tf_op jit(solution)/shard_map/ppermute | solution.py:122
  49.2 2.4 gather_fusion
  55.2 5.4 %collective-permute-start.5 = (bf16[128,256]{1,0:T(8,128)(2,1)S(1)}, bf16[128,256]{1,0:T(8,128)(2,1)S(1)}, u32[]{:S(2)}, u32[]{:S(2)}) collective-permute-start(bf16[128,256]{1,0:T(8,128)(2,1)S(1)} %get-tuple-element.53), channel_id=1, source_target_pairs={{0,64},{8,72},{16,80},{24,88},{32,96},{40,104},{48,112},{56,120},{... | collective-permute-start | bytes 196616 | tf_op jit(solution)/shard_map/ppermute | solution.py:26
  61.2 7.5 %collective-permute-start.6 = (bf16[128,256]{1,0:T(8,128)(2,1)S(1)}, bf16[128,256]{1,0:T(8,128)(2,1)S(1)}, u32[]{:S(2)}, u32[]{:S(2)}) collective-permute-start(bf16[128,256]{1,0:T(8,128)(2,1)S(1)} %get-tuple-element.53), channel_id=1, source_target_pairs={{0,96},{8,104},{16,112},{24,120},{32,128},{40,136},{48,144},{56,15... | collective-permute-start | bytes 196616 | tf_op jit(solution)/shard_map/ppermute | solution.py:26
  69.0 1.7 collective-permute-done.6
  71.1 9.0 %collective-permute-start.7 = (bf16[128,256]{1,0:T(8,128)(2,1)S(1)}, bf16[128,256]{1,0:T(8,128)(2,1)S(1)}, u32[]{:S(2)}, u32[]{:S(2)}) collective-permute-start(bf16[128,256]{1,0:T(8,128)(2,1)S(1)} %fusion.14), channel_id=1, source_target_pairs={{0,128},{8,136},{16,144},{24,152},{32,160},{40,168},{48,176},{56,1... | collective-permute-start | bytes 196616 | tf_op jit(solution)/shard_map/ppermute | solution.py:26
  80.2 8.9 %collective-permute-start.8 = (bf16[128,256]{1,0:T(8,128)(2,1)S(1)}, bf16[128,256]{1,0:T(8,128)(2,1)S(1)}, u32[]{:S(2)}, u32[]{:S(2)}) collective-permute-start(bf16[128,256]{1,0:T(8,128)(2,1)S(1)} %fusion.14), channel_id=1, source_target_pairs={{0,256},{8,264},{16,272},{24,280},{32,288},{40,296},{48,304},{56,3... | collective-permute-start | bytes 196616 | tf_op jit(solution)/shard_map/ppermute | solution.py:26
  91.2 3.6 %collective-permute-done.9 = bf16[128,256]{1,0:T(8,128)(2,1)S(1)} collective-permute-done((bf16[128,256]{1,0:T(8,128)(2,1)S(1)}, bf16[128,256]{1,0:T(8,128)(2,1)S(1)}, u32[]{:S(2)}, u32[]{:S(2)}) %collective-permute-start.9) | collective-permute-done | bytes 65568 | tf_op jit(solution)/shard_map/ppermute | solution.py:26
  96.3 2.8 collective-permute-start.10
  99.1 4.0 %collective-permute-start.11 = (f32[128,128]{1,0:T(8,128)S(1)}, f32[128,128]{1,0:T(8,128)S(1)}, u32[]{:S(2)}, u32[]{:S(2)}) collective-permute-start(f32[128,128]{1,0:T(8,128)S(1)} %get-tuple-element.43), channel_id=1, source_target_pairs={{0,16},{8,24},{16,0},{24,8},{32,48},{40,56},{48,32},{56,40},{64,80... | collective-permute-start | bytes 196616 | tf_op jit(solution)/shard_map/ppermute | solution.py:122
  103.1 3.2 %collective-permute-start.12 = (f32[128,128]{1,0:T(8,128)S(1)}, f32[128,128]{1,0:T(8,128)S(1)}, u32[]{:S(2)}, u32[]{:S(2)}) collective-permute-start(f32[128,128]{1,0:T(8,128)S(1)} %get-tuple-element.42), channel_id=1, source_target_pairs={{0,24},{8,0},{16,8},{24,16},{32,56},{40,32},{48,40},{56,48},{64,88... | collective-permute-start | bytes 196616 | tf_op jit(solution)/shard_map/ppermute | solution.py:122
  106.9 2.4 collective-permute-done.12
  112.1 4.3 %all-to-all-start = ((bf16[8,128,256]{2,1,0:T(8,128)(2,1)}), bf16[8,128,256]{2,1,0:T(8,128)(2,1)S(1)}, u32[]{:S(2)}, u32[]{:S(2)}) async-start(bf16[8,128,256]{2,1,0:T(8,128)(2,1)} %bitcast.144), calls=%async_computation | async-start | bytes 1048576 | tf_op jit(solution)/shard_map/all_to_all | solution.py:249
  116.5 5.2 %scatter_custom_fusion = s32[1536]{0:T(1024)S(1)} fusion(s32[1280]{0:T(1024)S(1)} %fusion.117, s32[1280]{0:T(1024)S(1)} %add_select_fusion, s32[]{:T(128)} %constant.517.clone.1), kind=kCustom, calls=%fused_computation.234 | custom fusion | bytes 6148 | tf_op jit(solution)/shard_map/scatter | solution.py:290
  121.7 5.0 %all-to-all-done = bf16[8,128,256]{2,1,0:T(8,128)(2,1)S(1)} async-done(((bf16[8,128,256]{2,1,0:T(8,128)(2,1)}), bf16[8,128,256]{2,1,0:T(8,128)(2,1)S(1)}, u32[]{:S(2)}, u32[]{:S(2)}) %all-to-all-start) | async-done | bytes 524320 | tf_op jit(solution)/shard_map/all_to_all | solution.py:249
  127.9 3.3 %all-to-all-start.1 = ((f32[8,2,128]{2,1,0:T(2,128)}), f32[8,2,128]{2,1,0:T(2,128)S(1)}, u32[]{:S(2)}, u32[]{:S(2)}) async-start(f32[8,2,128]{2,1,0:T(2,128)} %broadcast_in_dim.215), calls=%async_computation.1 | async-start | bytes 16384 | tf_op jit(solution)/shard_map/all_to_all | solution.py:261
  131.5 5.0 %all-to-all-done.1 = f32[8,2,128]{2,1,0:T(2,128)S(1)} async-done(((f32[8,2,128]{2,1,0:T(2,128)}), f32[8,2,128]{2,1,0:T(2,128)S(1)}, u32[]{:S(2)}, u32[]{:S(2)}) %all-to-all-start.1) | async-done | bytes 8224 | tf_op jit(solution)/shard_map/all_to_all | solution.py:261
  136.7 5.4 %gather_fusion.2 = bf16[1536,256]{1,0:T(8,128)(2,1)} fusion(bf16[129,256]{1,0:T(8,128)(2,1)S(1)} %concatenate.62, s32[2048]{0:T(1024)S(1)} %pad_clamp_fusion.1), kind=kCustom, calls=%fused_computation.2 | custom fusion | bytes 1579008 | tf_op jit(solution)/shard_map/jit(_take)/gather | solution.py:293
  142.0 1.7 gather.23
  144.4 57.3 %all_to_all.30 = bf16[64,6,4,256]{3,2,1,0:T(4,128)(2,1)S(1)} all-to-all(bf16[64,6,4,256]{3,2,1,0:T(4,128)(2,1)S(1)} %broadcast_select_fusion), channel_id=1, replica_groups=mesh['seq'=64,'head'=8] {'seq'}, dimensions={0} | all-to-all | bytes 1572864 | tf_op jit(solution)/shard_map/all_to_all | solution.py:294
  201.7 1.7 fusion.2
  203.4 2.6 copy.180
  207.7 24.0 %all_to_all.31 = bf16[8,384,4,2,32]{1,4,3,2,0:T(8,128)(2,1)S(1)} all-to-all(bf16[8,384,4,2,32]{1,4,3,2,0:T(8,128)(2,1)S(1)} %copy.181), channel_id=1, replica_groups=mesh['seq'=64,'head'=8] {'head'}, dimensions={0} | all-to-all | bytes 3145728 | tf_op jit(solution)/shard_map/all_to_all | solution.py:304
  232.1 15.7 %all_to_all.32 = bf16[8,384,4,32]{1,3,2,0:T(8,128)(2,1)S(1)} all-to-all(bf16[8,384,4,32]{1,3,2,0:T(8,128)(2,1)S(1)} %broadcast_in_dim.222), channel_id=1, replica_groups=mesh['seq'=64,'head'=8] {'head'}, dimensions={0} | all-to-all | bytes 1572864 | tf_op jit(solution)/shard_map/all_to_all | solution.py:311
  249.9 6.1 %all-to-all-start.5 = ((bf16[64,6,4,256]{3,2,1,0:T(4,128)(2,1)}), bf16[64,6,4,256]{3,2,1,0:T(4,128)(2,1)}, u32[]{:S(2)}, u32[]{:S(2)}) async-start(bf16[64,6,4,256]{3,2,1,0:T(4,128)(2,1)} %bitcast.55), calls=%async_computation.5 | async-start | bytes 1572864 | tf_op jit(solution)/shard_map/all_to_all | solution.py:322
  256.6 43.0 %all-to-all-done.5 = bf16[64,6,4,256]{3,2,1,0:T(4,128)(2,1)} async-done(((bf16[64,6,4,256]{3,2,1,0:T(4,128)(2,1)}), bf16[64,6,4,256]{3,2,1,0:T(4,128)(2,1)}, u32[]{:S(2)}, u32[]{:S(2)}) %all-to-all-start.5) | async-done | bytes 786464 | tf_op jit(solution)/shard_map/all_to_all | solution.py:322
  301.1 4.7 %gather_fusion.3 = bf16[1280,256]{1,0:T(8,128)(2,1)} fusion(bf16[1536,256]{1,0:T(8,128)(2,1)S(1)} %reshape.1161, s32[2048]{0:T(1024)S(1)} %pad_clamp_fusion), kind=kCustom, calls=%fused_computation.3 | custom fusion | bytes 1315840 | tf_op jit(solution)/shard_map/jit(_take)/gather | solution.py:331
  (202 shorter events, 51.4 us)
Async XLA Ops:
  0.0 110.8 %copy-start = (bf16[512,2048]{1,0:T(8,128)(2,1)S(1)}, bf16[512,2048]{1,0:T(8,128)(2,1)}, u32[]{:S(2)}) copy-start(bf16[512,2048]{1,0:T(8,128)(2,1)} %param.26) | copy-start | bytes 6291460
  0.9 16.4 %collective-permute-start = (bf16[3,1024]{1,0:T(4,128)(2,1)S(1)}, bf16[3,1024]{1,0:T(4,128)(2,1)S(1)}, u32[]{:S(2)}, u32[]{:S(2)}) collective-permute-start(bf16[3,1024]{1,0:T(4,128)(2,1)S(1)} %slice.144), channel_id=1, source_target_pairs={{0,8},{8,16},{16,24},{24,32},{32,40},{40,48},{48,56},{56,64},{64,7... | collective-permute-start | bytes 18440 | tf_op jit(solution)/shard_map/ppermute | solution.py:26
  15.0 2.3 copy-start.15
  24.2 2.4 copy-start.5
  30.6 12.7 %copy-start.6 = (f32[128,2,128]{2,0,1:T(8,128)S(1)}, f32[128,2,128]{2,0,1:T(8,128)}, u32[]{:S(2)}) copy-start(f32[128,2,128]{2,0,1:T(8,128)} %copy.157) | copy-start | bytes 393220
  32.0 12.6 %collective-permute-start.1 = (f32[128,256]{1,0:T(8,128)S(1)}, f32[128,256]{1,0:T(8,128)S(1)}, u32[]{:S(2)}, u32[]{:S(2)}) collective-permute-start(f32[128,256]{1,0:T(8,128)S(1)} %get-tuple-element.36), channel_id=1, source_target_pairs={{0,8},{8,16},{16,24},{24,0},{32,40},{40,48},{48,56},{56,32},{64,72... | collective-permute-start | bytes 393224 | tf_op jit(solution)/shard_map/ppermute | solution.py:122
  35.1 10.0 %collective-permute-start.2 = (f32[128,256]{1,0:T(8,128)S(1)}, f32[128,256]{1,0:T(8,128)S(1)}, u32[]{:S(2)}, u32[]{:S(2)}) collective-permute-start(f32[128,256]{1,0:T(8,128)S(1)} %get-tuple-element.37), channel_id=1, source_target_pairs={{0,16},{8,24},{16,0},{24,8},{32,48},{40,56},{48,32},{56,40},{64,80... | collective-permute-start | bytes 393224 | tf_op jit(solution)/shard_map/ppermute | solution.py:122
  41.5 6.9 %collective-permute-start.3 = (f32[128,256]{1,0:T(8,128)S(1)}, f32[128,256]{1,0:T(8,128)S(1)}, u32[]{:S(2)}, u32[]{:S(2)}) collective-permute-start(f32[128,256]{1,0:T(8,128)S(1)} %get-tuple-element.38), channel_id=1, source_target_pairs={{0,24},{8,0},{16,8},{24,16},{32,56},{40,32},{48,40},{56,48},{64,88... | collective-permute-start | bytes 393224 | tf_op jit(solution)/shard_map/ppermute | solution.py:122
  52.8 27.3 %copy-start.8 = (f32[1,128,256]{2,1,0:T(8,128)S(1)}, f32[1,128,256]{2,1,0:T(8,128)}, u32[]{:S(2)}) copy-start(f32[1,128,256]{2,1,0:T(8,128)} %pad_bitcast_fusion) | copy-start | bytes 393220
  53.6 15.1 %collective-permute-start.4 = (bf16[128,256]{1,0:T(8,128)(2,1)S(1)}, bf16[128,256]{1,0:T(8,128)(2,1)S(1)}, u32[]{:S(2)}, u32[]{:S(2)}) collective-permute-start(bf16[128,256]{1,0:T(8,128)(2,1)S(1)} %get-tuple-element.53), channel_id=1, source_target_pairs={{0,32},{8,40},{16,48},{24,56},{32,64},{40,72},{48,80},{56,88},{64,... | collective-permute-start | bytes 196616 | tf_op jit(solution)/shard_map/ppermute | solution.py:26
  55.2 13.5 %collective-permute-start.5 = (bf16[128,256]{1,0:T(8,128)(2,1)S(1)}, bf16[128,256]{1,0:T(8,128)(2,1)S(1)}, u32[]{:S(2)}, u32[]{:S(2)}) collective-permute-start(bf16[128,256]{1,0:T(8,128)(2,1)S(1)} %get-tuple-element.53), channel_id=1, source_target_pairs={{0,64},{8,72},{16,80},{24,88},{32,96},{40,104},{48,112},{56,120},{... | collective-permute-start | bytes 196616 | tf_op jit(solution)/shard_map/ppermute | solution.py:26
  61.2 9.4 %collective-permute-start.6 = (bf16[128,256]{1,0:T(8,128)(2,1)S(1)}, bf16[128,256]{1,0:T(8,128)(2,1)S(1)}, u32[]{:S(2)}, u32[]{:S(2)}) collective-permute-start(bf16[128,256]{1,0:T(8,128)(2,1)S(1)} %get-tuple-element.53), channel_id=1, source_target_pairs={{0,96},{8,104},{16,112},{24,120},{32,128},{40,136},{48,144},{56,15... | collective-permute-start | bytes 196616 | tf_op jit(solution)/shard_map/ppermute | solution.py:26
  68.9 37.4 %copy-start.2 = (f32[4,128,128]{2,1,0:T(8,128)S(1)}, f32[4,128,128]{2,1,0:T(8,128)}, u32[]{:S(2)}) copy-start(f32[4,128,128]{2,1,0:T(8,128)} %convolution_multiply_fusion.3) | copy-start | bytes 786436
  71.1 19.3 %collective-permute-start.7 = (bf16[128,256]{1,0:T(8,128)(2,1)S(1)}, bf16[128,256]{1,0:T(8,128)(2,1)S(1)}, u32[]{:S(2)}, u32[]{:S(2)}) collective-permute-start(bf16[128,256]{1,0:T(8,128)(2,1)S(1)} %fusion.14), channel_id=1, source_target_pairs={{0,128},{8,136},{16,144},{24,152},{32,160},{40,168},{48,176},{56,1... | collective-permute-start | bytes 196616 | tf_op jit(solution)/shard_map/ppermute | solution.py:26
  80.2 10.8 %collective-permute-start.8 = (bf16[128,256]{1,0:T(8,128)(2,1)S(1)}, bf16[128,256]{1,0:T(8,128)(2,1)S(1)}, u32[]{:S(2)}, u32[]{:S(2)}) collective-permute-start(bf16[128,256]{1,0:T(8,128)(2,1)S(1)} %fusion.14), channel_id=1, source_target_pairs={{0,256},{8,264},{16,272},{24,280},{32,288},{40,296},{48,304},{56,3... | collective-permute-start | bytes 196616 | tf_op jit(solution)/shard_map/ppermute | solution.py:26
  89.1 5.7 %collective-permute-start.9 = (bf16[128,256]{1,0:T(8,128)(2,1)S(1)}, bf16[128,256]{1,0:T(8,128)(2,1)S(1)}, u32[]{:S(2)}, u32[]{:S(2)}) collective-permute-start(bf16[128,256]{1,0:T(8,128)(2,1)S(1)} %fusion.14), channel_id=1, source_target_pairs={{0,384},{8,392},{16,400},{24,408},{32,416},{40,424},{48,432},{56,4... | collective-permute-start | bytes 196616 | tf_op jit(solution)/shard_map/ppermute | solution.py:26
  96.3 14.2 %copy-start.4 = (f32[128,4,128]{2,0,1:T(8,128)S(1)}, f32[128,4,128]{2,0,1:T(8,128)}, u32[]{:S(2)}) copy-start(f32[128,4,128]{2,0,1:T(8,128)} %copy.168) | copy-start | bytes 786436
  96.3 14.2 %copy-start.18 = (f32[128]{0:T(128)S(1)}, f32[128]{0:T(128)}, u32[]{:S(2)}) copy-start(f32[128]{0:T(128)} %param.25) | copy-start | bytes 1540
  96.3 10.6 %collective-permute-start.10 = (f32[128,128]{1,0:T(8,128)S(1)}, f32[128,128]{1,0:T(8,128)S(1)}, u32[]{:S(2)}, u32[]{:S(2)}) collective-permute-start(f32[128,128]{1,0:T(8,128)S(1)} %get-tuple-element.44), channel_id=1, source_target_pairs={{0,8},{8,16},{16,24},{24,0},{32,40},{40,48},{48,56},{56,32},{64,72... | collective-permute-start | bytes 196616 | tf_op jit(solution)/shard_map/ppermute | solution.py:122
  99.1 7.8 %collective-permute-start.11 = (f32[128,128]{1,0:T(8,128)S(1)}, f32[128,128]{1,0:T(8,128)S(1)}, u32[]{:S(2)}, u32[]{:S(2)}) collective-permute-start(f32[128,128]{1,0:T(8,128)S(1)} %get-tuple-element.43), channel_id=1, source_target_pairs={{0,16},{8,24},{16,0},{24,8},{32,48},{40,56},{48,32},{56,40},{64,80... | collective-permute-start | bytes 196616 | tf_op jit(solution)/shard_map/ppermute | solution.py:122
  103.1 6.2 %collective-permute-start.12 = (f32[128,128]{1,0:T(8,128)S(1)}, f32[128,128]{1,0:T(8,128)S(1)}, u32[]{:S(2)}, u32[]{:S(2)}) collective-permute-start(f32[128,128]{1,0:T(8,128)S(1)} %get-tuple-element.42), channel_id=1, source_target_pairs={{0,24},{8,0},{16,8},{24,16},{32,56},{40,32},{48,40},{56,48},{64,88... | collective-permute-start | bytes 196616 | tf_op jit(solution)/shard_map/ppermute | solution.py:122
  110.8 16.1 %copy-start.11 = (bf16[128,256]{1,0:T(8,128)(2,1)S(1)}, bf16[128,256]{1,0:T(8,128)(2,1)}, u32[]{:S(2)}) copy-start(bf16[128,256]{1,0:T(8,128)(2,1)} %param.17) | copy-start | bytes 196612
  111.3 15.7 %copy-start.14 = (f32[16,256]{1,0:T(8,128)S(1)}, f32[16,256]{1,0:T(8,128)}, u32[]{:S(2)}) copy-start(f32[16,256]{1,0:T(8,128)} %param.27) | copy-start | bytes 49156
  111.3 15.7 %copy-start.17 = (s32[128]{0:T(128)S(1)}, s32[128]{0:T(128)}, u32[]{:S(2)}) copy-start(s32[128]{0:T(128)} %param.28) | copy-start | bytes 1540
  111.3 25.3 %copy-start.16 = (f32[256]{0:T(256)S(1)}, f32[256]{0:T(256)}, u32[]{:S(2)}) copy-start(f32[256]{0:T(256)} %param.29) | copy-start | bytes 3076
  112.1 14.6 %all-to-all-start = ((bf16[8,128,256]{2,1,0:T(8,128)(2,1)}), bf16[8,128,256]{2,1,0:T(8,128)(2,1)S(1)}, u32[]{:S(2)}, u32[]{:S(2)}) async-start(bf16[8,128,256]{2,1,0:T(8,128)(2,1)} %bitcast.144), calls=%async_computation | async-start | bytes 1048576 | tf_op jit(solution)/shard_map/all_to_all | solution.py:249
  127.9 8.6 %all-to-all-start.1 = ((f32[8,2,128]{2,1,0:T(2,128)}), f32[8,2,128]{2,1,0:T(2,128)S(1)}, u32[]{:S(2)}, u32[]{:S(2)}) async-start(f32[8,2,128]{2,1,0:T(2,128)} %broadcast_in_dim.215), calls=%async_computation.1 | async-start | bytes 16384 | tf_op jit(solution)/shard_map/all_to_all | solution.py:261
  143.7 58.0 %copy-start.3 = (bf16[4,256,512]{2,1,0:T(8,128)(2,1)S(1)}, bf16[4,256,512]{2,1,0:T(8,128)(2,1)}, u32[]{:S(2)}) copy-start(bf16[4,256,512]{2,1,0:T(8,128)(2,1)} %param.32) | copy-start | bytes 3145732
  232.0 15.9 %copy-start.7 = (bf16[4,256,256]{2,1,0:T(8,128)(2,1)S(1)}, bf16[4,256,256]{2,1,0:T(8,128)(2,1)}, u32[]{:S(2)}) copy-start(bf16[4,256,256]{2,1,0:T(8,128)(2,1)} %param.33) | copy-start | bytes 1572868
  248.4 7.9 %copy-start.12 = (s32[128,10]{0,1:T(8,128)S(1)}, s32[128,10]{0,1:T(8,128)}, u32[]{:S(2)}) copy-start(s32[128,10]{0,1:T(8,128)} %param.30) | copy-start | bytes 15364
  248.4 8.0 %copy-start.13 = (f32[128,10]{0,1:T(8,128)S(1)}, f32[128,10]{0,1:T(8,128)}, u32[]{:S(2)}) copy-start(f32[128,10]{0,1:T(8,128)} %param.31) | copy-start | bytes 15364
  249.9 49.6 %all-to-all-start.5 = ((bf16[64,6,4,256]{3,2,1,0:T(4,128)(2,1)}), bf16[64,6,4,256]{3,2,1,0:T(4,128)(2,1)}, u32[]{:S(2)}, u32[]{:S(2)}) async-start(bf16[64,6,4,256]{3,2,1,0:T(4,128)(2,1)} %bitcast.55), calls=%async_computation.5 | async-start | bytes 1572864 | tf_op jit(solution)/shard_map/all_to_all | solution.py:322
  (3 other events, 5.7 us)

commit v10 on v9

--- a/solution.py
+++ b/solution.py
@@ -140,7 +140,7 @@
     items = [lax.dynamic_index_in_dim(own, place, 0, keepdims=False)]
     for offset in range(1, group):
         sent = lax.dynamic_index_in_dim(own, (place + offset) % group, 0, keepdims=False)
-        items.append(within_group(sent, group, offset))
+        items.append(within_group(sent.astype(LINK), group, offset).astype(jnp.float32))
     stacked = jnp.stack(items)
     maps = jnp.take(stacked, (place - jnp.arange(group)) % group, axis=0)
     identity = jnp.concatenate(
@@ -176,7 +176,7 @@
     heads = [lax.dynamic_index_in_dim(entering, place, 0, keepdims=False)]
     for offset in range(1, group):
         sent = lax.dynamic_index_in_dim(entering, (place + offset) % group, 0, keepdims=False)
-        heads.append(within_group(sent, group, offset))
+        heads.append(within_group(sent.astype(LINK), group, offset).astype(jnp.float32))
     stacked = jnp.stack(heads)
     return jnp.take(stacked, (place - jnp.arange(group)) % group, axis=0)
 

time: 310 us -> 315 us (1.016)
  other arithmetic: 11.8 us -> 16.4 us
  transfers between devices with their start and end apart: 16 -> 16, of which waited for: 9 -> 10; matrix products, arithmetic and copies ran while one was open for 7% -> 8% of each run, Pallas kernels for 0% -> 0%
where the time goes in v10:
time: 315 us; the launch traced here: 313 us
  blocking collectives  97.6 us (31%)
  starting transfers between devices  73.8 us (23%)
  waiting for transfers between devices  62.2 us (20%)
  local copies, waits for them, and re-layouts  41.9 us (13%)
  matrix products  19.9 us (6%)
  other arithmetic  16.4 us (5%)
    all_to_all x1, blocking collectives, local(): lax.all_to_all(outgoing, 'seq', split_axis=0, concat_axis=0, tiled=True)  57.6 us
    all_to_all x1, waiting for transfers between devices, local(): lax.all_to_all(results.reshape(seq_size, capacity, experts_here, -1), 'se...  43 us
    ppermute x7, starting transfers between devices, passed_along(): lax.ppermute(value, axis, [(source, source + steps) for source in range(f...  38.2 us
    all_to_all x1, blocking collectives, local(): lax.all_to_all(jnp.transpose(pieces, (3, 0, 1, 2, 4)), 'head', split_axis...  24 us
    ppermute x6, starting transfers between devices, within_group(): return lax.ppermute(value, 'seq', pairs)  21.8 us
    all_to_all x1, blocking collectives, local(): lax.all_to_all(jnp.broadcast_to(activated_slice[None], (head_count,) + ac...  15.9 us
    gather x2, local copies, waits for them, and re-layouts, local(): jnp.take(padded_rows, source, axis=0)  7.04 us
  transfers between devices with their start and end apart: 16, of which 10 were waited for; matrix products, arithmetic and copies ran while one was open for 8% of the time, Pallas kernels for 0%

profile of v10, /device:TPU:8, one launch (start us, length us, event | category | flops | bytes accessed | tf_op | source)
XLA Modules:
  0.0 313.3 jit_solution(8563787491854955986)
XLA Ops:
  0.9 3.5 %collective-permute-start = (bf16[3,1024]{1,0:T(4,128)(2,1)S(1)}, bf16[3,1024]{1,0:T(4,128)(2,1)S(1)}, u32[]{:S(2)}, u32[]{:S(2)}) collective-permute-start(bf16[3,1024]{1,0:T(4,128)(2,1)S(1)} %slice.144), channel_id=1, source_target_pairs={{0,8},{8,16},{16,24},{24,32},{32,40},{40,48},{48,56},{56,64},{64,7... | collective-permute-start | bytes 18440 | tf_op jit(solution)/shard_map/ppermute | solution.py:26
  14.6 1.8 broadcast_add_fusion
  32.5 1.7 copy.157
  40.3 5.5 %collective-permute-start.3 = (bf16[128,256]{1,0:T(8,128)(2,1)S(1)}, bf16[128,256]{1,0:T(8,128)(2,1)S(1)}, u32[]{:S(2)}, u32[]{:S(2)}) collective-permute-start(bf16[128,256]{1,0:T(8,128)(2,1)S(1)} %get-tuple-element.37), channel_id=1, source_target_pairs={{0,24},{8,0},{16,8},{24,16},{32,56},{40,32},{48,40},{56,48},{64,88... | collective-permute-start | bytes 196616 | tf_op jit(solution)/shard_map/ppermute | solution.py:122
  45.8 1.9 collective-permute-start.2
  47.7 3.4 %collective-permute-start.1 = (bf16[128,256]{1,0:T(8,128)(2,1)S(1)}, bf16[128,256]{1,0:T(8,128)(2,1)S(1)}, u32[]{:S(2)}, u32[]{:S(2)}) collective-permute-start(bf16[128,256]{1,0:T(8,128)(2,1)S(1)} %get-tuple-element.34), channel_id=1, source_target_pairs={{0,8},{8,16},{16,24},{24,0},{32,40},{40,48},{48,56},{56,32},{64,72... | collective-permute-start | bytes 196616 | tf_op jit(solution)/shard_map/ppermute | solution.py:122
  51.1 2.3 collective-permute-done.2
  57.6 3.0 collective-permute-start.4
  60.6 6.2 %collective-permute-start.5 = (bf16[128,256]{1,0:T(8,128)(2,1)S(1)}, bf16[128,256]{1,0:T(8,128)(2,1)S(1)}, u32[]{:S(2)}, u32[]{:S(2)}) collective-permute-start(bf16[128,256]{1,0:T(8,128)(2,1)S(1)} %get-tuple-element.51), channel_id=1, source_target_pairs={{0,64},{8,72},{16,80},{24,88},{32,96},{40,104},{48,112},{56,120},{... | collective-permute-start | bytes 196616 | tf_op jit(solution)/shard_map/ppermute | solution.py:26
  67.4 6.7 %collective-permute-start.6 = (bf16[128,256]{1,0:T(8,128)(2,1)S(1)}, bf16[128,256]{1,0:T(8,128)(2,1)S(1)}, u32[]{:S(2)}, u32[]{:S(2)}) collective-permute-start(bf16[128,256]{1,0:T(8,128)(2,1)S(1)} %get-tuple-element.51), channel_id=1, source_target_pairs={{0,96},{8,104},{16,112},{24,120},{32,128},{40,136},{48,144},{56,15... | collective-permute-start | bytes 196616 | tf_op jit(solution)/shard_map/ppermute | solution.py:26
  74.3 1.7 collective-permute-done.6
  76.5 9.7 %collective-permute-start.7 = (bf16[128,256]{1,0:T(8,128)(2,1)S(1)}, bf16[128,256]{1,0:T(8,128)(2,1)S(1)}, u32[]{:S(2)}, u32[]{:S(2)}) collective-permute-start(bf16[128,256]{1,0:T(8,128)(2,1)S(1)} %fusion.14), channel_id=1, source_target_pairs={{0,128},{8,136},{16,144},{24,152},{32,160},{40,168},{48,176},{56,1... | collective-permute-start | bytes 196616 | tf_op jit(solution)/shard_map/ppermute | solution.py:26
  86.3 7.8 %collective-permute-start.8 = (bf16[128,256]{1,0:T(8,128)(2,1)S(1)}, bf16[128,256]{1,0:T(8,128)(2,1)S(1)}, u32[]{:S(2)}, u32[]{:S(2)}) collective-permute-start(bf16[128,256]{1,0:T(8,128)(2,1)S(1)} %fusion.14), channel_id=1, source_target_pairs={{0,256},{8,264},{16,272},{24,280},{32,288},{40,296},{48,304},{56,3... | collective-permute-start | bytes 196616 | tf_op jit(solution)/shard_map/ppermute | solution.py:26
  96.2 2.8 collective-permute-done.9
  100.5 4.5 %collective-permute-start.12 = (bf16[128,128]{1,0:T(8,128)(2,1)S(1)}, bf16[128,128]{1,0:T(8,128)(2,1)S(1)}, u32[]{:S(2)}, u32[]{:S(2)}) collective-permute-start(bf16[128,128]{1,0:T(8,128)(2,1)S(1)} %get-tuple-element.41), channel_id=1, source_target_pairs={{0,24},{8,0},{16,8},{24,16},{32,56},{40,32},{48,40},{56,48},{64,88... | collective-permute-start | bytes 98312 | tf_op jit(solution)/shard_map/ppermute | solution.py:122
  105.0 2.5 collective-permute-start.11
  107.5 4.1 %collective-permute-start.10 = (bf16[128,128]{1,0:T(8,128)(2,1)S(1)}, bf16[128,128]{1,0:T(8,128)(2,1)S(1)}, u32[]{:S(2)}, u32[]{:S(2)}) collective-permute-start(bf16[128,128]{1,0:T(8,128)(2,1)S(1)} %get-tuple-element.40), channel_id=1, source_target_pairs={{0,8},{8,16},{16,24},{24,0},{32,40},{40,48},{48,56},{56,32},{64,72... | collective-permute-start | bytes 98312 | tf_op jit(solution)/shard_map/ppermute | solution.py:122
  116.3 4.3 %all-to-all-start = ((bf16[8,128,256]{2,1,0:T(8,128)(2,1)}), bf16[8,128,256]{2,1,0:T(8,128)(2,1)S(1)}, u32[]{:S(2)}, u32[]{:S(2)}) async-start(bf16[8,128,256]{2,1,0:T(8,128)(2,1)} %bitcast.156), calls=%async_computation | async-start | bytes 1048576 | tf_op jit(solution)/shard_map/all_to_all | solution.py:249
  120.6 5.2 %scatter_custom_fusion = s32[1536]{0:T(1024)S(1)} fusion(s32[1280]{0:T(1024)S(1)} %copy-done.18, s32[1280]{0:T(1024)S(1)} %add_select_fusion, s32[]{:T(128)} %constant.517.clone.1), kind=kCustom, calls=%fused_computation.246 | custom fusion | bytes 6148 | tf_op jit(solution)/shard_map/scatter | solution.py:290
  125.9 5.0 %all-to-all-done = bf16[8,128,256]{2,1,0:T(8,128)(2,1)S(1)} async-done(((bf16[8,128,256]{2,1,0:T(8,128)(2,1)}), bf16[8,128,256]{2,1,0:T(8,128)(2,1)S(1)}, u32[]{:S(2)}, u32[]{:S(2)}) %all-to-all-start) | async-done | bytes 524320 | tf_op jit(solution)/shard_map/all_to_all | solution.py:249
  132.0 3.3 %all-to-all-start.1 = ((f32[8,2,128]{2,1,0:T(2,128)}), f32[8,2,128]{2,1,0:T(2,128)S(1)}, u32[]{:S(2)}, u32[]{:S(2)}) async-start(f32[8,2,128]{2,1,0:T(2,128)} %broadcast_in_dim.215), calls=%async_computation.1 | async-start | bytes 16384 | tf_op jit(solution)/shard_map/all_to_all | solution.py:261
  135.6 5.0 %all-to-all-done.1 = f32[8,2,128]{2,1,0:T(2,128)S(1)} async-done(((f32[8,2,128]{2,1,0:T(2,128)}), f32[8,2,128]{2,1,0:T(2,128)S(1)}, u32[]{:S(2)}, u32[]{:S(2)}) %all-to-all-start.1) | async-done | bytes 8224 | tf_op jit(solution)/shard_map/all_to_all | solution.py:261
  140.8 5.4 %gather_fusion.2 = bf16[1536,256]{1,0:T(8,128)(2,1)} fusion(bf16[129,256]{1,0:T(8,128)(2,1)S(1)} %concatenate.62, s32[2048]{0:T(1024)S(1)} %pad_clamp_fusion.1), kind=kCustom, calls=%fused_computation.2 | custom fusion | bytes 1579008 | tf_op jit(solution)/shard_map/jit(_take)/gather | solution.py:293
  146.1 1.7 gather.23
  148.5 57.6 %all_to_all.30 = bf16[64,6,4,256]{3,2,1,0:T(4,128)(2,1)S(1)} all-to-all(bf16[64,6,4,256]{3,2,1,0:T(4,128)(2,1)S(1)} %broadcast_select_fusion), channel_id=1, replica_groups=mesh['seq'=64,'head'=8] {'seq'}, dimensions={0} | all-to-all | bytes 1572864 | tf_op jit(solution)/shard_map/all_to_all | solution.py:294
  206.2 1.8 fusion.2
  207.9 2.6 copy.180
  212.2 24.0 %all_to_all.31 = bf16[8,384,4,2,32]{1,4,3,2,0:T(8,128)(2,1)S(1)} all-to-all(bf16[8,384,4,2,32]{1,4,3,2,0:T(8,128)(2,1)S(1)} %copy.181), channel_id=1, replica_groups=mesh['seq'=64,'head'=8] {'head'}, dimensions={0} | all-to-all | bytes 3145728 | tf_op jit(solution)/shard_map/all_to_all | solution.py:304
  236.6 15.9 %all_to_all.32 = bf16[8,384,4,32]{1,3,2,0:T(8,128)(2,1)S(1)} all-to-all(bf16[8,384,4,32]{1,3,2,0:T(8,128)(2,1)S(1)} %broadcast_in_dim.222), channel_id=1, replica_groups=mesh['seq'=64,'head'=8] {'head'}, dimensions={0} | all-to-all | bytes 1572864 | tf_op jit(solution)/shard_map/all_to_all | solution.py:311
  254.6 6.1 %all-to-all-start.5 = ((bf16[64,6,4,256]{3,2,1,0:T(4,128)(2,1)}), bf16[64,6,4,256]{3,2,1,0:T(4,128)(2,1)}, u32[]{:S(2)}, u32[]{:S(2)}) async-start(bf16[64,6,4,256]{3,2,1,0:T(4,128)(2,1)} %bitcast.55), calls=%async_computation.5 | async-start | bytes 1572864 | tf_op jit(solution)/shard_map/all_to_all | solution.py:322
  261.3 43.0 %all-to-all-done.5 = bf16[64,6,4,256]{3,2,1,0:T(4,128)(2,1)} async-done(((bf16[64,6,4,256]{3,2,1,0:T(4,128)(2,1)}), bf16[64,6,4,256]{3,2,1,0:T(4,128)(2,1)}, u32[]{:S(2)}, u32[]{:S(2)}) %all-to-all-start.5) | async-done | bytes 786464 | tf_op jit(solution)/shard_map/all_to_all | solution.py:322
  305.8 4.7 %gather_fusion.3 = bf16[1280,256]{1,0:T(8,128)(2,1)} fusion(bf16[1536,256]{1,0:T(8,128)(2,1)S(1)} %reshape.1167, s32[2048]{0:T(1024)S(1)} %pad_clamp_fusion), kind=kCustom, calls=%fused_computation.3 | custom fusion | bytes 1315840 | tf_op jit(solution)/shard_map/jit(_take)/gather | solution.py:331
  (228 shorter events, 57.1 us)
Async XLA Ops:
  0.0 114.9 %copy-start = (bf16[512,2048]{1,0:T(8,128)(2,1)S(1)}, bf16[512,2048]{1,0:T(8,128)(2,1)}, u32[]{:S(2)}) copy-start(bf16[512,2048]{1,0:T(8,128)(2,1)} %param.26) | copy-start | bytes 6291460
  0.9 22.1 %collective-permute-start = (bf16[3,1024]{1,0:T(4,128)(2,1)S(1)}, bf16[3,1024]{1,0:T(4,128)(2,1)S(1)}, u32[]{:S(2)}, u32[]{:S(2)}) collective-permute-start(bf16[3,1024]{1,0:T(4,128)(2,1)S(1)} %slice.144), channel_id=1, source_target_pairs={{0,8},{8,16},{16,24},{24,32},{32,40},{40,48},{48,56},{56,64},{64,7... | collective-permute-start | bytes 18440 | tf_op jit(solution)/shard_map/ppermute | solution.py:26
  31.3 6.4 %copy-start.21 = (f32[4,128]{1,0:T(4,128)S(1)}, f32[4,128]{1,0:T(4,128)}, u32[]{:S(2)}) copy-start(f32[4,128]{1,0:T(4,128)} %get-tuple-element.79) | copy-start | bytes 6148
  40.2 15.2 %copy-start.24 = (pred[4]{0:T(512)(128)(4,1)S(1)}, pred[4]{0:T(512)(128)(4,1)}, u32[]{:S(2)}) copy-start(pred[4]{0:T(512)(128)(4,1)} %compare_and_fusion.2) | copy-start | bytes 16
  40.3 10.9 %collective-permute-start.3 = (bf16[128,256]{1,0:T(8,128)(2,1)S(1)}, bf16[128,256]{1,0:T(8,128)(2,1)S(1)}, u32[]{:S(2)}, u32[]{:S(2)}) collective-permute-start(bf16[128,256]{1,0:T(8,128)(2,1)S(1)} %get-tuple-element.37), channel_id=1, source_target_pairs={{0,24},{8,0},{16,8},{24,16},{32,56},{40,32},{48,40},{56,48},{64,88... | collective-permute-start | bytes 196616 | tf_op jit(solution)/shard_map/ppermute | solution.py:122
  45.8 7.7 %collective-permute-start.2 = (bf16[128,256]{1,0:T(8,128)(2,1)S(1)}, bf16[128,256]{1,0:T(8,128)(2,1)S(1)}, u32[]{:S(2)}, u32[]{:S(2)}) collective-permute-start(bf16[128,256]{1,0:T(8,128)(2,1)S(1)} %get-tuple-element.36), channel_id=1, source_target_pairs={{0,16},{8,24},{16,0},{24,8},{32,48},{40,56},{48,32},{56,40},{64,80... | collective-permute-start | bytes 196616 | tf_op jit(solution)/shard_map/ppermute | solution.py:122
  47.7 6.2 %collective-permute-start.1 = (bf16[128,256]{1,0:T(8,128)(2,1)S(1)}, bf16[128,256]{1,0:T(8,128)(2,1)S(1)}, u32[]{:S(2)}, u32[]{:S(2)}) collective-permute-start(bf16[128,256]{1,0:T(8,128)(2,1)S(1)} %get-tuple-element.34), channel_id=1, source_target_pairs={{0,8},{8,16},{16,24},{24,0},{32,40},{40,48},{48,56},{56,32},{64,72... | collective-permute-start | bytes 196616 | tf_op jit(solution)/shard_map/ppermute | solution.py:122
  55.4 11.3 %copy-start.2 = (f32[4,128,256]{2,1,0:T(8,128)S(1)}, f32[4,128,256]{2,1,0:T(8,128)}, u32[]{:S(2)}) copy-start(f32[4,128,256]{2,1,0:T(8,128)} %convolution_multiply_fusion.1) | copy-start | bytes 1572868
  55.4 11.3 %copy-start.3 = (f32[4,128,128]{2,1,0:T(8,128)S(1)}, f32[4,128,128]{2,1,0:T(8,128)}, u32[]{:S(2)}) copy-start(f32[4,128,128]{2,1,0:T(8,128)} %convolution_multiply_fusion.3) | copy-start | bytes 786436
  57.0 29.2 %copy-start.8 = (f32[1,128,256]{2,1,0:T(8,128)S(1)}, f32[1,128,256]{2,1,0:T(8,128)}, u32[]{:S(2)}) copy-start(f32[1,128,256]{2,1,0:T(8,128)} %pad_bitcast_fusion) | copy-start | bytes 393220
  57.6 16.5 %collective-permute-start.4 = (bf16[128,256]{1,0:T(8,128)(2,1)S(1)}, bf16[128,256]{1,0:T(8,128)(2,1)S(1)}, u32[]{:S(2)}, u32[]{:S(2)}) collective-permute-start(bf16[128,256]{1,0:T(8,128)(2,1)S(1)} %get-tuple-element.51), channel_id=1, source_target_pairs={{0,32},{8,40},{16,48},{24,56},{32,64},{40,72},{48,80},{56,88},{64,... | collective-permute-start | bytes 196616 | tf_op jit(solution)/shard_map/ppermute | solution.py:26
  60.6 13.6 %collective-permute-start.5 = (bf16[128,256]{1,0:T(8,128)(2,1)S(1)}, bf16[128,256]{1,0:T(8,128)(2,1)S(1)}, u32[]{:S(2)}, u32[]{:S(2)}) collective-permute-start(bf16[128,256]{1,0:T(8,128)(2,1)S(1)} %get-tuple-element.51), channel_id=1, source_target_pairs={{0,64},{8,72},{16,80},{24,88},{32,96},{40,104},{48,112},{56,120},{... | collective-permute-start | bytes 196616 | tf_op jit(solution)/shard_map/ppermute | solution.py:26
  67.4 8.6 %collective-permute-start.6 = (bf16[128,256]{1,0:T(8,128)(2,1)S(1)}, bf16[128,256]{1,0:T(8,128)(2,1)S(1)}, u32[]{:S(2)}, u32[]{:S(2)}) collective-permute-start(bf16[128,256]{1,0:T(8,128)(2,1)S(1)} %get-tuple-element.51), channel_id=1, source_target_pairs={{0,96},{8,104},{16,112},{24,120},{32,128},{40,136},{48,144},{56,15... | collective-permute-start | bytes 196616 | tf_op jit(solution)/shard_map/ppermute | solution.py:26
  76.5 19.0 %collective-permute-start.7 = (bf16[128,256]{1,0:T(8,128)(2,1)S(1)}, bf16[128,256]{1,0:T(8,128)(2,1)S(1)}, u32[]{:S(2)}, u32[]{:S(2)}) collective-permute-start(bf16[128,256]{1,0:T(8,128)(2,1)S(1)} %fusion.14), channel_id=1, source_target_pairs={{0,128},{8,136},{16,144},{24,152},{32,160},{40,168},{48,176},{56,1... | collective-permute-start | bytes 196616 | tf_op jit(solution)/shard_map/ppermute | solution.py:26
  86.3 9.7 %collective-permute-start.8 = (bf16[128,256]{1,0:T(8,128)(2,1)S(1)}, bf16[128,256]{1,0:T(8,128)(2,1)S(1)}, u32[]{:S(2)}, u32[]{:S(2)}) collective-permute-start(bf16[128,256]{1,0:T(8,128)(2,1)S(1)} %fusion.14), channel_id=1, source_target_pairs={{0,256},{8,264},{16,272},{24,280},{32,288},{40,296},{48,304},{56,3... | collective-permute-start | bytes 196616 | tf_op jit(solution)/shard_map/ppermute | solution.py:26
  94.1 4.9 %collective-permute-start.9 = (bf16[128,256]{1,0:T(8,128)(2,1)S(1)}, bf16[128,256]{1,0:T(8,128)(2,1)S(1)}, u32[]{:S(2)}, u32[]{:S(2)}) collective-permute-start(bf16[128,256]{1,0:T(8,128)(2,1)S(1)} %fusion.14), channel_id=1, source_target_pairs={{0,384},{8,392},{16,400},{24,408},{32,416},{40,424},{48,432},{56,4... | collective-permute-start | bytes 196616 | tf_op jit(solution)/shard_map/ppermute | solution.py:26
  95.6 18.9 %copy-start.5 = (f32[128,4,128]{2,0,1:T(8,128)S(1)}, f32[128,4,128]{2,0,1:T(8,128)}, u32[]{:S(2)}) copy-start(f32[128,4,128]{2,0,1:T(8,128)} %copy.168) | copy-start | bytes 786436
  95.7 18.9 %copy-start.27 = (f32[128]{0:T(128)S(1)}, f32[128]{0:T(128)}, u32[]{:S(2)}) copy-start(f32[128]{0:T(128)} %param.25) | copy-start | bytes 1540
  100.5 11.1 %collective-permute-start.12 = (bf16[128,128]{1,0:T(8,128)(2,1)S(1)}, bf16[128,128]{1,0:T(8,128)(2,1)S(1)}, u32[]{:S(2)}, u32[]{:S(2)}) collective-permute-start(bf16[128,128]{1,0:T(8,128)(2,1)S(1)} %get-tuple-element.41), channel_id=1, source_target_pairs={{0,24},{8,0},{16,8},{24,16},{32,56},{40,32},{48,40},{56,48},{64,88... | collective-permute-start | bytes 98312 | tf_op jit(solution)/shard_map/ppermute | solution.py:122
  105.0 7.3 %collective-permute-start.11 = (bf16[128,128]{1,0:T(8,128)(2,1)S(1)}, bf16[128,128]{1,0:T(8,128)(2,1)S(1)}, u32[]{:S(2)}, u32[]{:S(2)}) collective-permute-start(bf16[128,128]{1,0:T(8,128)(2,1)S(1)} %get-tuple-element.42), channel_id=1, source_target_pairs={{0,16},{8,24},{16,0},{24,8},{32,48},{40,56},{48,32},{56,40},{64,80... | collective-permute-start | bytes 98312 | tf_op jit(solution)/shard_map/ppermute | solution.py:122
  107.5 5.8 %collective-permute-start.10 = (bf16[128,128]{1,0:T(8,128)(2,1)S(1)}, bf16[128,128]{1,0:T(8,128)(2,1)S(1)}, u32[]{:S(2)}, u32[]{:S(2)}) collective-permute-start(bf16[128,128]{1,0:T(8,128)(2,1)S(1)} %get-tuple-element.40), channel_id=1, source_target_pairs={{0,8},{8,16},{16,24},{24,0},{32,40},{40,48},{48,56},{56,32},{64,72... | collective-permute-start | bytes 98312 | tf_op jit(solution)/shard_map/ppermute | solution.py:122
  114.9 16.0 %copy-start.11 = (bf16[128,256]{1,0:T(8,128)(2,1)S(1)}, bf16[128,256]{1,0:T(8,128)(2,1)}, u32[]{:S(2)}) copy-start(bf16[128,256]{1,0:T(8,128)(2,1)} %param.17) | copy-start | bytes 196612
  115.4 15.7 %copy-start.19 = (f32[16,256]{1,0:T(8,128)S(1)}, f32[16,256]{1,0:T(8,128)}, u32[]{:S(2)}) copy-start(f32[16,256]{1,0:T(8,128)} %param.27) | copy-start | bytes 49156
  115.4 15.7 %copy-start.26 = (s32[128]{0:T(128)S(1)}, s32[128]{0:T(128)}, u32[]{:S(2)}) copy-start(s32[128]{0:T(128)} %param.28) | copy-start | bytes 1540
  115.4 25.2 %copy-start.25 = (f32[256]{0:T(256)S(1)}, f32[256]{0:T(256)}, u32[]{:S(2)}) copy-start(f32[256]{0:T(256)} %param.29) | copy-start | bytes 3076
  116.3 14.6 %all-to-all-start = ((bf16[8,128,256]{2,1,0:T(8,128)(2,1)}), bf16[8,128,256]{2,1,0:T(8,128)(2,1)S(1)}, u32[]{:S(2)}, u32[]{:S(2)}) async-start(bf16[8,128,256]{2,1,0:T(8,128)(2,1)} %bitcast.156), calls=%async_computation | async-start | bytes 1048576 | tf_op jit(solution)/shard_map/all_to_all | solution.py:249
  132.0 8.6 %all-to-all-start.1 = ((f32[8,2,128]{2,1,0:T(2,128)}), f32[8,2,128]{2,1,0:T(2,128)S(1)}, u32[]{:S(2)}, u32[]{:S(2)}) async-start(f32[8,2,128]{2,1,0:T(2,128)} %broadcast_in_dim.215), calls=%async_computation.1 | async-start | bytes 16384 | tf_op jit(solution)/shard_map/all_to_all | solution.py:261
  147.8 58.3 %copy-start.4 = (bf16[4,256,512]{2,1,0:T(8,128)(2,1)S(1)}, bf16[4,256,512]{2,1,0:T(8,128)(2,1)}, u32[]{:S(2)}) copy-start(bf16[4,256,512]{2,1,0:T(8,128)(2,1)} %param.32) | copy-start | bytes 3145732
  236.5 16.1 %copy-start.7 = (bf16[4,256,256]{2,1,0:T(8,128)(2,1)S(1)}, bf16[4,256,256]{2,1,0:T(8,128)(2,1)}, u32[]{:S(2)}) copy-start(bf16[4,256,256]{2,1,0:T(8,128)(2,1)} %param.33) | copy-start | bytes 1572868
  253.1 7.9 %copy-start.16 = (s32[128,10]{0,1:T(8,128)S(1)}, s32[128,10]{0,1:T(8,128)}, u32[]{:S(2)}) copy-start(s32[128,10]{0,1:T(8,128)} %param.30) | copy-start | bytes 15364
  253.1 8.1 %copy-start.17 = (f32[128,10]{0,1:T(8,128)S(1)}, f32[128,10]{0,1:T(8,128)}, u32[]{:S(2)}) copy-start(f32[128,10]{0,1:T(8,128)} %param.31) | copy-start | bytes 15364
  254.6 49.6 %all-to-all-start.5 = ((bf16[64,6,4,256]{3,2,1,0:T(4,128)(2,1)}), bf16[64,6,4,256]{3,2,1,0:T(4,128)(2,1)}, u32[]{:S(2)}, u32[]{:S(2)}) async-start(bf16[64,6,4,256]{3,2,1,0:T(4,128)(2,1)} %bitcast.55), calls=%async_computation.5 | async-start | bytes 1572864 | tf_op jit(solution)/shard_map/all_to_all | solution.py:322
  (12 other events, 39.6 us)
